TPU v7x, 512 devices: a whole 4x8x8 slice. The times are simulated.
512 devices in a mesh: pipe: 4 (over z_hi), ctx: 32 (over y, z_lo, core), dp: 4 (over x).
Axes of the slice: x: 4, y: 8, z: 8 (z_hi: 4, z_lo: 2; z = z_hi * 2 + z_lo), core: 2. Of those that a mesh axis runs over, the one named last changes fastest.
Arguments:
- queries: bfloat16 [4, 4, 4096, 4096], P('pipe', 'dp', 'ctx'), may hold values from -7 to 7
- key_input: bfloat16 [4, 4, 4096, 512], P('pipe', 'dp', 'ctx'), may hold values from -4 to 4
- value_input: bfloat16 [4, 4, 4096, 512], P('pipe', 'dp', 'ctx'), may hold values from -6 to 6
- incoming: bfloat16 [4, 4, 4096, 4096], P('pipe', 'dp', 'ctx'), may hold values from -6 to 6
- segments: int32 [4, 4096], P('dp'), may hold values from 0 to 15, never falling along the last dimension, each value on 1 to 512 neighbouring positions
Outputs:
- query_grad: bfloat16 [4, 4, 4096, 4096], P('pipe', 'dp', 'ctx')
- key_grad: bfloat16 [4, 4, 4096, 512], P('pipe', 'dp', 'ctx')
- value_grad: bfloat16 [4, 4, 4096, 512], P('pipe', 'dp', 'ctx')
- bias_grad: float32 [4, 5120], P('pipe')
Inputs may be any that keep to these rules, and one draw needn't show every extreme that they name: `segments`: tokens of one document are contiguous; every document holds 1 to 512 tokens and one holds exactly 512.
All inputs are finite; a program needn't handle non-finite values.
Results may differ from a plain program's by a relative error of at most 0.009.
Values may be sent and summed in bfloat16 or wider, within the bound.
No kernel may reach another device: no remote copies, remote signals or barrier semaphores. Data moves between devices by JAX's collectives and lax.ppermute only.
A program may use at most 64 MiB of HBM per device.

v0:
```python
import math

import jax
import jax.numpy as jnp
from jax import lax
from jax.sharding import PartitionSpec as P

ASKER_STREAMS = 32
SHARED_GROUPS = 4
FEATURE_SIZE = 128
QUERY_PER_KEY = 8


def passed_along(value, axis, steps):
    count = lax.axis_size(axis)
    pairs = [(source, (source + steps) % count) for source in range(count)]
    return lax.ppermute(value, axis, pairs)


def attend(
    queries, key_rows, value_rows, cotangent, query_doc, key_doc, query_pos, key_pos, scaling
):
    scores = (
        jnp.einsum("gqd,kd->gqk", queries, key_rows, preferred_element_type=jnp.float32) * scaling
    )
    visible = (query_doc[:, None] == key_doc[None, :]) & (key_pos[None, :] <= query_pos[:, None])
    scores = jnp.where(visible[None], scores, -1e30)
    row_max = jnp.max(scores, axis=-1, keepdims=True)
    weights = jnp.where(visible[None], jnp.exp(scores - row_max), 0.0)
    probs = weights / jnp.sum(weights, axis=-1, keepdims=True)
    probs_b = probs.astype(jnp.bfloat16)
    attn_out = jnp.einsum("gqk,kd->gqd", probs_b, value_rows, preferred_element_type=jnp.float32)
    dot_out = jnp.sum(cotangent.astype(jnp.float32) * attn_out, axis=-1, keepdims=True)
    grad_prob = jnp.einsum("gqd,kd->gqk", cotangent, value_rows, preferred_element_type=jnp.float32)
    grad_score = (probs * (grad_prob - dot_out) * scaling).astype(jnp.bfloat16)
    asker_derivative = jnp.einsum(
        "gqk,kd->gqd", grad_score, key_rows, preferred_element_type=jnp.float32
    )
    lookup_derivative = jnp.einsum(
        "gqk,gqd->kd", grad_score, queries, preferred_element_type=jnp.float32
    )
    content_derivative = jnp.einsum(
        "gqk,gqd->kd", probs_b, cotangent, preferred_element_type=jnp.float32
    )
    return (asker_derivative, lookup_derivative, content_derivative)


def banded(queries, key_rows, value_rows, cotangent, doc_ids, block_len, scaling):
    length = doc_ids.shape[0]
    blocks = length // block_len
    width = key_rows.shape[1]
    key_pad = jnp.concatenate([jnp.zeros((block_len, width), key_rows.dtype), key_rows], axis=0)
    value_pad = jnp.concatenate(
        [jnp.zeros((block_len, width), value_rows.dtype), value_rows], axis=0
    )
    doc_pad = jnp.concatenate([jnp.full((block_len,), -1, jnp.int32), doc_ids])
    pos_pad = jnp.arange(length + block_len, dtype=jnp.int32) - block_len

    def step(carried, block):
        key_acc, value_acc = carried
        anchor = block * block_len
        query_blk = lax.dynamic_slice_in_dim(queries, anchor, block_len, 1)
        cot_blk = lax.dynamic_slice_in_dim(cotangent, anchor, block_len, 1)
        key_blk = lax.dynamic_slice_in_dim(key_pad, anchor, 2 * block_len, 0)
        value_blk = lax.dynamic_slice_in_dim(value_pad, anchor, 2 * block_len, 0)
        query_doc = lax.dynamic_slice_in_dim(doc_ids, anchor, block_len, 0)
        key_doc = lax.dynamic_slice_in_dim(doc_pad, anchor, 2 * block_len, 0)
        query_pos = anchor + jnp.arange(block_len, dtype=jnp.int32)
        key_pos = lax.dynamic_slice_in_dim(pos_pad, anchor, 2 * block_len, 0)
        asker_derivative, lookup_derivative, content_derivative = attend(
            query_blk, key_blk, value_blk, cot_blk, query_doc, key_doc, query_pos, key_pos, scaling
        )
        key_acc = lax.dynamic_update_slice_in_dim(
            key_acc,
            lax.dynamic_slice_in_dim(key_acc, anchor, 2 * block_len, 0) + lookup_derivative,
            anchor,
            0,
        )
        value_acc = lax.dynamic_update_slice_in_dim(
            value_acc,
            lax.dynamic_slice_in_dim(value_acc, anchor, 2 * block_len, 0) + content_derivative,
            anchor,
            0,
        )
        return ((key_acc, value_acc), asker_derivative)

    start_acc = jnp.zeros((length + block_len, width), jnp.float32)
    (key_acc, value_acc), query_blocks = lax.scan(
        step, (start_acc, start_acc), jnp.arange(blocks, dtype=jnp.int32)
    )
    groups = queries.shape[0]
    asker_derivative = query_blocks.transpose(1, 0, 2, 3).reshape(groups, length, width)
    return (asker_derivative, key_acc[block_len:], value_acc[block_len:])


def body(queries, key_input, value_input, incoming, segments):
    shard_length = queries.shape[2]
    ctx_size = lax.axis_size("ctx")
    reach_dev = min(4, ctx_size - 1)
    block_len = reach_dev * shard_length
    scaling = 1.0 / math.sqrt(FEATURE_SIZE)
    doc_ids = segments[0]
    handed = passed_along(incoming, "pipe", -1)
    query_tok = queries[0, 0].reshape(shard_length, ASKER_STREAMS, FEATURE_SIZE)
    cot_tok = handed[0, 0].reshape(shard_length, ASKER_STREAMS, FEATURE_SIZE)
    key_widened = jnp.repeat(
        key_input[0, 0].reshape(shard_length, SHARED_GROUPS, FEATURE_SIZE), QUERY_PER_KEY, axis=1
    )
    value_widened = jnp.repeat(
        value_input[0, 0].reshape(shard_length, SHARED_GROUPS, FEATURE_SIZE), QUERY_PER_KEY, axis=1
    )
    query_head, key_head, value_head, cot_head = (
        lax.all_to_all(query_tok, "ctx", split_axis=1, concat_axis=0, tiled=True),
        lax.all_to_all(key_widened, "ctx", split_axis=1, concat_axis=0, tiled=True),
        lax.all_to_all(value_widened, "ctx", split_axis=1, concat_axis=0, tiled=True),
        lax.all_to_all(cot_tok, "ctx", split_axis=1, concat_axis=0, tiled=True),
    )

    def per_head(members):
        return banded(
            members[0][None], members[1], members[2], members[3][None], doc_ids, block_len, scaling
        )

    asker_derivative, lookup_derivative, content_derivative = lax.map(
        per_head,
        (
            query_head.transpose(1, 0, 2),
            key_head.transpose(1, 0, 2),
            value_head.transpose(1, 0, 2),
            cot_head.transpose(1, 0, 2),
        ),
    )
    asker_derivative = asker_derivative[:, 0].transpose(1, 0, 2)
    lookup_derivative = lookup_derivative.transpose(1, 0, 2)
    content_derivative = content_derivative.transpose(1, 0, 2)
    query_back, key_backward, value_backward = (
        lax.all_to_all(asker_derivative, "ctx", split_axis=0, concat_axis=1, tiled=True),
        lax.all_to_all(lookup_derivative, "ctx", split_axis=0, concat_axis=1, tiled=True),
        lax.all_to_all(content_derivative, "ctx", split_axis=0, concat_axis=1, tiled=True),
    )
    query_flat = query_back.reshape(shard_length, ASKER_STREAMS * FEATURE_SIZE)
    key_flattened = (
        key_backward.reshape(shard_length, SHARED_GROUPS, QUERY_PER_KEY, FEATURE_SIZE)
        .sum(axis=2)
        .reshape(shard_length, SHARED_GROUPS * FEATURE_SIZE)
    )
    value_flat = (
        value_backward.reshape(shard_length, SHARED_GROUPS, QUERY_PER_KEY, FEATURE_SIZE)
        .sum(axis=2)
        .reshape(shard_length, SHARED_GROUPS * FEATURE_SIZE)
    )
    offset_parts = jnp.concatenate(
        [jnp.sum(query_flat, axis=0), jnp.sum(key_flattened, axis=0), jnp.sum(value_flat, axis=0)]
    )
    offset_overall = lax.psum(offset_parts, ("ctx", "dp"))
    bias_scaled = offset_overall / math.sqrt(lax.axis_size("dp") * shard_length * ctx_size)
    query_grad = query_flat.astype(jnp.bfloat16)[None, None]
    key_grad = key_flattened.astype(jnp.bfloat16)[None, None]
    value_grad = value_flat.astype(jnp.bfloat16)[None, None]
    return (query_grad, key_grad, value_grad, bias_scaled[None])


def solution(mesh):
    return jax.shard_map(
        body,
        mesh=mesh,
        in_specs=(
            P("pipe", "dp", "ctx", None),
            P("pipe", "dp", "ctx", None),
            P("pipe", "dp", "ctx", None),
            P("pipe", "dp", "ctx", None),
            P("dp", None),
        ),
        out_specs=(
            P("pipe", "dp", "ctx", None),
            P("pipe", "dp", "ctx", None),
            P("pipe", "dp", "ctx", None),
            P("pipe", None),
        ),
        check_vma=False,
    )
```

profile of v0, /device:TPU:1, one launch (start us, length us, event | category | flops | bytes accessed | tf_op | source)
XLA Modules:
  0.0 1037.9 jit_solution(12610844461914456718)
XLA Ops:
  2.9 10.6 %all-to-all-start.1 = ((bf16[128,32,128]{2,0,1:T(8,128)(2,1)}), bf16[128,32,128]{2,0,1:T(8,128)(2,1)S(1)}, u32[]{:S(2)}, u32[]{:S(2)}) async-start(bf16[128,32,128]{2,0,1:T(8,128)(2,1)} %bitcast.9), calls=%async_computation.1 | async-start | bytes 2097152 | tf_op jit(solution)/shard_map/all_to_all | solution.py:114
  13.5 28.0 %all-to-all-done.1 = bf16[128,32,128]{2,0,1:T(8,128)(2,1)S(1)} async-done(((bf16[128,32,128]{2,0,1:T(8,128)(2,1)}), bf16[128,32,128]{2,0,1:T(8,128)(2,1)S(1)}, u32[]{:S(2)}, u32[]{:S(2)}) %all-to-all-start.1) | async-done | bytes 1048608 | tf_op jit(solution)/shard_map/all_to_all | solution.py:114
  42.7 4.3 all-to-all-start.3
  47.0 9.8 collective-permute-start
  56.8 54.2 %collective-permute-done = bf16[1,1,128,4096]{3,2,1,0:T(8,128)(2,1)S(1)} collective-permute-done((bf16[1,1,128,4096]{3,2,1,0:T(8,128)(2,1)}, bf16[1,1,128,4096]{3,2,1,0:T(8,128)(2,1)S(1)}, u32[]{:S(2)}, u32[]{:S(2)}) %collective-permute-start) | collective-permute-done | bytes 1048608 | tf_op jit(solution)/shard_map/ppermute | solution.py:17
  112.3 6.5 all-to-all-start.2
  121.7 25.2 %all-to-all-done.2 = bf16[128,32,128]{0,2,1:T(8,128)(2,1)S(1)} async-done(((bf16[128,32,128]{0,2,1:T(8,128)(2,1)}), bf16[128,32,128]{0,2,1:T(8,128)(2,1)S(1)}, u32[]{:S(2)}, u32[]{:S(2)}) %all-to-all-start.2) | async-done | bytes 1048608 | tf_op jit(solution)/shard_map/all_to_all | solution.py:116
  146.9 5.0 all-to-all-start
  155.8 24.2 %all-to-all-done = bf16[128,32,128]{2,0,1:T(8,128)(2,1)} async-done(((bf16[128,32,128]{2,0,1:T(8,128)(2,1)}), bf16[128,32,128]{2,0,1:T(8,128)(2,1)}, u32[]{:S(2)}, u32[]{:S(2)}) %all-to-all-start) | async-done | bytes 1048608 | tf_op jit(solution)/shard_map/all_to_all | solution.py:113
  183.6 126.3 %while.25 = (s32[]{:T(128)}, f32[4608,128]{1,0:T(8,128)}, f32[4608,128]{1,0:T(8,128)}, f32[8,1,512,128]{3,2,1,0:T(8,128)}, s32[8]{0:T(128)}, /*index=5*/s32[4096...) while((s32[]{:T(128)}, f32[4608,128]{1,0:T(8,128)}, ...), condition=%wide.region_4.5_spmd, body=%wide.region_0.4_spmd.sunk | while | flops 820444160 | bytes 22487844 | solution.py:88
  192.6 2.4 fusion.59
  195.0 2.1 fusion.61
  197.1 2.3 fusion.60
  208.4 2.4 fusion.59
  210.8 2.1 fusion.61
  212.9 2.3 fusion.60
  218.6 1.7 fusion.55
  224.2 2.4 fusion.59
  226.6 2.1 fusion.61
  228.7 2.3 fusion.60
  234.4 1.7 fusion.55
  240.0 2.4 fusion.59
  242.4 2.1 fusion.61
  244.5 2.3 fusion.60
  250.2 1.7 fusion.55
  255.8 2.4 fusion.59
  258.2 2.1 fusion.61
  260.3 2.3 fusion.60
  266.0 1.7 fusion.55
  271.6 2.4 fusion.59
  274.0 2.1 fusion.61
  276.1 2.3 fusion.60
  287.4 2.4 fusion.59
  289.8 2.1 fusion.61
  291.9 2.3 fusion.60
  303.2 2.4 fusion.59
  305.6 2.1 fusion.61
  307.7 2.3 fusion.60
  310.0 3.1 slice.8
  313.1 5.2 all-to-all-start.5
  318.3 3.1 slice.9
  321.4 47.0 %all-to-all-done.5 = f32[4096,1,128]{2,1,0:T(1,128)S(1)} async-done(((f32[4096,1,128]{2,1,0:T(1,128)}), f32[4096,1,128]{2,1,0:T(1,128)S(1)}, u32[]{:S(2)}, u32[]{:S(2)}) %all-to-all-start.5) | async-done | bytes 2097184 | tf_op jit(solution)/shard_map/all_to_all | solution.py:138
  368.4 56.9 %all_to_all.105 = f32[4096,1,128]{2,1,0:T(1,128)} all-to-all(f32[4096,1,128]{2,1,0:T(1,128)} %bitcast.109), channel_id=1, replica_groups=mesh['pipe'=4,'ctx'=32,'dp'=4] {'ctx'}, dimensions={0} | all-to-all | bytes 4194304 | tf_op jit(solution)/shard_map/all_to_all | solution.py:139
  425.2 5.9 all-to-all-start.4
  433.0 48.2 %all-to-all-done.4 = f32[4096,1,128]{2,1,0:T(1,128)} async-done(((f32[4096,1,128]{2,1,0:T(1,128)}), f32[4096,1,128]{2,1,0:T(1,128)}, u32[]{:S(2)}, u32[]{:S(2)}) %all-to-all-start.4) | async-done | bytes 2097184 | tf_op jit(solution)/shard_map/all_to_all | solution.py:137
  481.2 1.8 convert_element_type.50
  484.7 545.3 %psum.7 = f32[5120]{0:T(1024)S(1)} all-reduce(f32[5120]{0:T(1024)S(1)} %pad_maximum_fusion), channel_id=1, replica_groups=mesh['pipe'=4,'ctx'=32,'dp'=4] {'ctx','dp'}, use_global_device_ids=true, to_apply=%region_12.13 | all-reduce | flops 5120 | bytes 40960 | tf_op jit(solution)/shard_map/psum | solution.py:155
  1032.0 2.3 copy.50
  (129 shorter events, 84.4 us)
Async XLA Ops:
  0.6 12.8 %copy-start = (bf16[1,1,128,512]{3,2,1,0:T(8,128)(2,1)S(1)}, bf16[1,1,128,512]{3,2,1,0:T(8,128)(2,1)}, u32[]{:S(2)}) copy-start(bf16[1,1,128,512]{3,2,1,0:T(8,128)(2,1)} %param.9) | copy-start | bytes 393220
  2.9 38.6 %all-to-all-start.1 = ((bf16[128,32,128]{2,0,1:T(8,128)(2,1)}), bf16[128,32,128]{2,0,1:T(8,128)(2,1)S(1)}, u32[]{:S(2)}, u32[]{:S(2)}) async-start(bf16[128,32,128]{2,0,1:T(8,128)(2,1)} %bitcast.9), calls=%async_computation.1 | async-start | bytes 2097152 | tf_op jit(solution)/shard_map/all_to_all | solution.py:114
  42.7 69.6 %all-to-all-start.3 = ((bf16[128,32,128]{2,0,1:T(8,128)(2,1)}), bf16[128,32,128]{2,0,1:T(8,128)(2,1)S(1)}, u32[]{:S(2)}, u32[]{:S(2)}) async-start(bf16[128,32,128]{2,0,1:T(8,128)(2,1)} %bitcast.17), calls=%async_computation.3 | async-start | bytes 2097152 | tf_op jit(solution)/shard_map/all_to_all | solution.py:115
  47.0 64.0 %collective-permute-start = (bf16[1,1,128,4096]{3,2,1,0:T(8,128)(2,1)}, bf16[1,1,128,4096]{3,2,1,0:T(8,128)(2,1)S(1)}, u32[]{:S(2)}, u32[]{:S(2)}) collective-permute-start(bf16[1,1,128,4096]{3,2,1,0:T(8,128)(2,1)} %param.10), channel_id=1, source_target_pairs={{0,384},{128,0},{256,128},{384,256},{1,385},{129,1},{257,129},{385... | collective-permute-start | bytes 3145736 | tf_op jit(solution)/shard_map/ppermute | solution.py:17
  112.3 34.6 %all-to-all-start.2 = ((bf16[128,32,128]{0,2,1:T(8,128)(2,1)}), bf16[128,32,128]{0,2,1:T(8,128)(2,1)S(1)}, u32[]{:S(2)}, u32[]{:S(2)}) async-start(bf16[128,32,128]{0,2,1:T(8,128)(2,1)} %bitcast.112), calls=%async_computation.2 | async-start | bytes 2097152 | tf_op jit(solution)/shard_map/all_to_all | solution.py:116
  120.3 31.6 %copy-start.1 = (s32[1,4096]{1,0:T(1,128)S(1)}, s32[1,4096]{1,0:T(1,128)}, u32[]{:S(2)}) copy-start(s32[1,4096]{1,0:T(1,128)} %param.11) | copy-start | bytes 49156
  146.9 33.0 %all-to-all-start = ((bf16[128,32,128]{2,0,1:T(8,128)(2,1)}), bf16[128,32,128]{2,0,1:T(8,128)(2,1)}, u32[]{:S(2)}, u32[]{:S(2)}) async-start(bf16[128,32,128]{2,0,1:T(8,128)(2,1)} %copy.41), calls=%async_computation | async-start | bytes 2097152 | tf_op jit(solution)/shard_map/all_to_all | solution.py:113
  313.1 55.3 %all-to-all-start.5 = ((f32[4096,1,128]{2,1,0:T(1,128)}), f32[4096,1,128]{2,1,0:T(1,128)S(1)}, u32[]{:S(2)}, u32[]{:S(2)}) async-start(f32[4096,1,128]{2,1,0:T(1,128)} %bitcast.108), calls=%async_computation.5 | async-start | bytes 4194304 | tf_op jit(solution)/shard_map/all_to_all | solution.py:138
  425.2 56.0 %all-to-all-start.4 = ((f32[4096,1,128]{2,1,0:T(1,128)}), f32[4096,1,128]{2,1,0:T(1,128)}, u32[]{:S(2)}, u32[]{:S(2)}) async-start(f32[4096,1,128]{2,1,0:T(1,128)} %bitcast.116), calls=%async_computation.4 | async-start | bytes 4194304 | tf_op jit(solution)/shard_map/all_to_all | solution.py:137
where the time goes:
time: 1050 us; the launch traced here: 1040 us
  blocking collectives  602 us (57%)
  waiting for transfers between devices  227 us (22%)
  matrix products  76.1 us (7%)
  local copies, waits for them, and re-layouts  57 us (5%)
  starting transfers between devices  47.3 us (5%)
  other arithmetic  23 us (2%)
    psum x1, blocking collectives, body(): offset_overall = lax.psum(offset_parts, ('ctx', 'dp'))  545 us
    all_to_all x1, blocking collectives, body(): lax.all_to_all(content_derivative, 'ctx', split_axis=0, concat_axis=1, ti...  56.9 us
    ppermute x1, waiting for transfers between devices, passed_along(): return lax.ppermute(value, axis, pairs)  54.2 us
    all_to_all x1, waiting for transfers between devices, body(): lax.all_to_all(asker_derivative, 'ctx', split_axis=0, concat_axis=1, tile...  48.2 us
    all_to_all x1, waiting for transfers between devices, body(): lax.all_to_all(lookup_derivative, 'ctx', split_axis=0, concat_axis=1, til...  47 us
    all_to_all x1, waiting for transfers between devices, body(): lax.all_to_all(key_widened, 'ctx', split_axis=1, concat_axis=0, tiled=True)  28 us
    all_to_all x1, waiting for transfers between devices, body(): lax.all_to_all(cot_tok, 'ctx', split_axis=1, concat_axis=0, tiled=True)  25.2 us
    all_to_all x1, waiting for transfers between devices, body(): lax.all_to_all(query_tok, 'ctx', split_axis=1, concat_axis=0, tiled=True)  24.2 us
  transfers between devices with their start and end apart: 7, of which 6 were waited for; matrix products, arithmetic and copies ran while one was open for 1% of the time, Pallas kernels for 0%

commit v1 on v0

--- a/solution.py
+++ b/solution.py
@@ -152,7 +152,9 @@
     offset_parts = jnp.concatenate(
         [jnp.sum(query_flat, axis=0), jnp.sum(key_flattened, axis=0), jnp.sum(value_flat, axis=0)]
     )
-    offset_overall = lax.psum(offset_parts, ("ctx", "dp"))
+    pipe_idx = lax.axis_index("pipe")
+    slots = jnp.zeros((lax.axis_size("pipe"), offset_parts.shape[0]), jnp.float32).at[pipe_idx].set(offset_parts)
+    offset_overall = lax.psum(slots, ("pipe", "ctx", "dp"))[pipe_idx]
     bias_scaled = offset_overall / math.sqrt(lax.axis_size("dp") * shard_length * ctx_size)
     query_grad = query_flat.astype(jnp.bfloat16)[None, None]
     key_grad = key_flattened.astype(jnp.bfloat16)[None, None]

time: 1050 us -> 763 us (0.73)
  blocking collectives: 602 us -> 56.1 us
  waiting for transfers between devices: 227 us -> 479 us
  between operations: 0.82 us -> 14.3 us
    psum x1 -> x0, blocking collectives: 545 us -> none  [body(): offset_overall = lax.psum(offset_parts, ('ctx', 'dp'))]
    psum x0 -> x1, waiting for transfers between devices: none -> 251 us  [body(): offset_overall = lax.psum(slots, ('pipe', 'ctx', 'dp'))[pipe_idx]]
  transfers between devices with their start and end apart: 7 -> 8, of which waited for: 6 -> 7; matrix products, arithmetic and copies ran while one was open for 1% -> 3% of each run, Pallas kernels for 0% -> 0%
where the time goes in v1:
time: 763 us; the launch traced here: 760 us
  waiting for transfers between devices  479 us (63%)
  matrix products  76.2 us (10%)
  local copies, waits for them, and re-layouts  56.1 us (7%)
  blocking collectives  56.1 us (7%)
  starting transfers between devices  48.2 us (6%)
  other arithmetic  25.3 us (3%)
  between operations  14.3 us (2%)
    psum x1, waiting for transfers between devices, body(): offset_overall = lax.psum(slots, ('pipe', 'ctx', 'dp'))[pipe_idx]  251 us
    all_to_all x1, blocking collectives, body(): lax.all_to_all(content_derivative, 'ctx', split_axis=0, concat_axis=1, ti...  56.1 us
    ppermute x1, waiting for transfers between devices, passed_along(): return lax.ppermute(value, axis, pairs)  54.2 us
    all_to_all x1, waiting for transfers between devices, body(): lax.all_to_all(lookup_derivative, 'ctx', split_axis=0, concat_axis=1, til...  48.6 us
    all_to_all x1, waiting for transfers between devices, body(): lax.all_to_all(asker_derivative, 'ctx', split_axis=0, concat_axis=1, tile...  47.4 us
    all_to_all x1, waiting for transfers between devices, body(): lax.all_to_all(key_widened, 'ctx', split_axis=1, concat_axis=0, tiled=True)  28 us
    all_to_all x1, waiting for transfers between devices, body(): lax.all_to_all(cot_tok, 'ctx', split_axis=1, concat_axis=0, tiled=True)  25.2 us
    all_to_all x1, waiting for transfers between devices, body(): lax.all_to_all(query_tok, 'ctx', split_axis=1, concat_axis=0, tiled=True)  24.3 us
  transfers between devices with their start and end apart: 8, of which 7 were waited for; matrix products, arithmetic and copies ran while one was open for 3% of the time, Pallas kernels for 0%

profile of v1, /device:TPU:1, one launch (start us, length us, event | category | flops | bytes accessed | tf_op | source)
XLA Modules:
  0.0 760.0 jit_solution(13099326957965084261)
XLA Ops:
  9.4 10.6 %all-to-all-start.1 = ((bf16[128,32,128]{2,0,1:T(8,128)(2,1)}), bf16[128,32,128]{2,0,1:T(8,128)(2,1)S(1)}, u32[]{:S(2)}, u32[]{:S(2)}) async-start(bf16[128,32,128]{2,0,1:T(8,128)(2,1)} %bitcast.9), calls=%async_computation.1 | async-start | bytes 2097152 | tf_op jit(solution)/shard_map/all_to_all | solution.py:114
  20.0 28.0 %all-to-all-done.1 = bf16[128,32,128]{2,0,1:T(8,128)(2,1)S(1)} async-done(((bf16[128,32,128]{2,0,1:T(8,128)(2,1)}), bf16[128,32,128]{2,0,1:T(8,128)(2,1)S(1)}, u32[]{:S(2)}, u32[]{:S(2)}) %all-to-all-start.1) | async-done | bytes 1048608 | tf_op jit(solution)/shard_map/all_to_all | solution.py:114
  49.2 4.3 all-to-all-start.3
  53.6 9.8 %collective-permute-start = (bf16[1,1,128,4096]{3,2,1,0:T(8,128)(2,1)}, bf16[1,1,128,4096]{3,2,1,0:T(8,128)(2,1)S(1)}, u32[]{:S(2)}, u32[]{:S(2)}) collective-permute-start(bf16[1,1,128,4096]{3,2,1,0:T(8,128)(2,1)} %param.12), channel_id=1, source_target_pairs={{0,384},{128,0},{256,128},{384,256},{1,385},{129,1},{257,129},{385... | collective-permute-start | bytes 3145736 | tf_op jit(solution)/shard_map/ppermute | solution.py:17
  63.3 54.2 %collective-permute-done = bf16[1,1,128,4096]{3,2,1,0:T(8,128)(2,1)S(1)} collective-permute-done((bf16[1,1,128,4096]{3,2,1,0:T(8,128)(2,1)}, bf16[1,1,128,4096]{3,2,1,0:T(8,128)(2,1)S(1)}, u32[]{:S(2)}, u32[]{:S(2)}) %collective-permute-start) | collective-permute-done | bytes 1048608 | tf_op jit(solution)/shard_map/ppermute | solution.py:17
  118.9 6.5 all-to-all-start.2
  128.2 25.2 %all-to-all-done.2 = bf16[128,32,128]{0,2,1:T(8,128)(2,1)S(1)} async-done(((bf16[128,32,128]{0,2,1:T(8,128)(2,1)}), bf16[128,32,128]{0,2,1:T(8,128)(2,1)S(1)}, u32[]{:S(2)}, u32[]{:S(2)}) %all-to-all-start.2) | async-done | bytes 1048608 | tf_op jit(solution)/shard_map/all_to_all | solution.py:116
  153.5 5.0 all-to-all-start
  162.2 24.3 %all-to-all-done = bf16[128,32,128]{2,0,1:T(8,128)(2,1)} async-done(((bf16[128,32,128]{2,0,1:T(8,128)(2,1)}), bf16[128,32,128]{2,0,1:T(8,128)(2,1)}, u32[]{:S(2)}, u32[]{:S(2)}) %all-to-all-start) | async-done | bytes 1048608 | tf_op jit(solution)/shard_map/all_to_all | solution.py:113
  190.1 126.4 %while.26 = (s32[]{:T(128)}, f32[4608,128]{1,0:T(8,128)}, f32[4608,128]{1,0:T(8,128)}, f32[8,1,512,128]{3,2,1,0:T(8,128)}, s32[8]{0:T(128)}, /*index=5*/s32[4096...) while((s32[]{:T(128)}, f32[4608,128]{1,0:T(8,128)}, ...), condition=%wide.region_4.5_spmd, body=%wide.region_0.4_spmd.sunk | while | flops 820444160 | bytes 22487344 | solution.py:88
  193.5 1.8 fusion.55
  199.1 2.4 fusion.59
  201.5 2.3 fusion.60
  203.8 2.1 fusion.61
  214.9 2.4 fusion.59
  217.3 2.3 fusion.60
  219.6 2.1 fusion.61
  225.1 1.7 fusion.55
  230.7 2.4 fusion.59
  233.1 2.3 fusion.60
  235.4 2.1 fusion.61
  240.9 1.7 fusion.55
  246.5 2.4 fusion.59
  248.9 2.3 fusion.60
  251.2 2.1 fusion.61
  256.7 1.7 fusion.55
  262.3 2.4 fusion.59
  264.7 2.3 fusion.60
  267.0 2.1 fusion.61
  278.1 2.4 fusion.59
  280.5 2.3 fusion.60
  282.9 2.1 fusion.61
  293.9 2.4 fusion.59
  296.3 2.3 fusion.60
  298.7 2.1 fusion.61
  304.1 1.7 fusion.55
  309.7 2.4 fusion.59
  312.1 2.3 fusion.60
  314.5 2.1 fusion.61
  316.5 3.1 slice.22
  319.7 6.0 all-to-all-start.5
  327.1 48.6 %all-to-all-done.5 = f32[4096,1,128]{2,1,0:T(1,128)} async-done(((f32[4096,1,128]{2,1,0:T(1,128)}), f32[4096,1,128]{2,1,0:T(1,128)}, u32[]{:S(2)}, u32[]{:S(2)}) %all-to-all-start.5) | async-done | bytes 2097184 | tf_op jit(solution)/shard_map/all_to_all | solution.py:138
  375.7 56.1 %all_to_all.105 = f32[4096,1,128]{2,1,0:T(1,128)S(1)} all-to-all(f32[4096,1,128]{2,1,0:T(1,128)} %bitcast.107), channel_id=1, replica_groups=mesh['pipe'=4,'ctx'=32,'dp'=4] {'ctx'}, dimensions={0} | all-to-all | bytes 4194304 | tf_op jit(solution)/shard_map/all_to_all | solution.py:139
  431.9 6.0 all-to-all-start.4
  440.6 47.4 %all-to-all-done.4 = f32[4096,1,128]{2,1,0:T(1,128)} async-done(((f32[4096,1,128]{2,1,0:T(1,128)}), f32[4096,1,128]{2,1,0:T(1,128)}, u32[]{:S(2)}, u32[]{:S(2)}) %all-to-all-start.4) | async-done | bytes 2097184 | tf_op jit(solution)/shard_map/all_to_all | solution.py:137
  491.4 1.8 convert_element_type.50
  494.5 2.3 copy.50
  500.4 251.3 %all-reduce.5.cloned.1.call-done = f32[4,5120]{1,0:T(4,128)} async-done(((f32[4,5120]{1,0:T(4,128)}), f32[4,5120]{1,0:T(4,128)}) %all-reduce.5.cloned.1.call-update) | async-done | bytes 81936 | tf_op jit(solution)/shard_map/psum | solution.py:157
  (140 shorter events, 87.2 us)
Async XLA Ops:
  7.2 12.8 %copy-start.2 = (bf16[1,1,128,512]{3,2,1,0:T(8,128)(2,1)S(1)}, bf16[1,1,128,512]{3,2,1,0:T(8,128)(2,1)}, u32[]{:S(2)}) copy-start(bf16[1,1,128,512]{3,2,1,0:T(8,128)(2,1)} %param.11) | copy-start | bytes 393220
  9.4 38.6 %all-to-all-start.1 = ((bf16[128,32,128]{2,0,1:T(8,128)(2,1)}), bf16[128,32,128]{2,0,1:T(8,128)(2,1)S(1)}, u32[]{:S(2)}, u32[]{:S(2)}) async-start(bf16[128,32,128]{2,0,1:T(8,128)(2,1)} %bitcast.9), calls=%async_computation.1 | async-start | bytes 2097152 | tf_op jit(solution)/shard_map/all_to_all | solution.py:114
  49.2 69.6 %all-to-all-start.3 = ((bf16[128,32,128]{2,0,1:T(8,128)(2,1)}), bf16[128,32,128]{2,0,1:T(8,128)(2,1)S(1)}, u32[]{:S(2)}, u32[]{:S(2)}) async-start(bf16[128,32,128]{2,0,1:T(8,128)(2,1)} %bitcast.17), calls=%async_computation.3 | async-start | bytes 2097152 | tf_op jit(solution)/shard_map/all_to_all | solution.py:115
  53.6 64.0 %collective-permute-start = (bf16[1,1,128,4096]{3,2,1,0:T(8,128)(2,1)}, bf16[1,1,128,4096]{3,2,1,0:T(8,128)(2,1)S(1)}, u32[]{:S(2)}, u32[]{:S(2)}) collective-permute-start(bf16[1,1,128,4096]{3,2,1,0:T(8,128)(2,1)} %param.12), channel_id=1, source_target_pairs={{0,384},{128,0},{256,128},{384,256},{1,385},{129,1},{257,129},{385... | collective-permute-start | bytes 3145736 | tf_op jit(solution)/shard_map/ppermute | solution.py:17
  118.9 34.6 %all-to-all-start.2 = ((bf16[128,32,128]{0,2,1:T(8,128)(2,1)}), bf16[128,32,128]{0,2,1:T(8,128)(2,1)S(1)}, u32[]{:S(2)}, u32[]{:S(2)}) async-start(bf16[128,32,128]{0,2,1:T(8,128)(2,1)} %bitcast.110), calls=%async_computation.2 | async-start | bytes 2097152 | tf_op jit(solution)/shard_map/all_to_all | solution.py:116
  126.8 31.6 %copy-start.3 = (s32[1,4096]{1,0:T(1,128)S(1)}, s32[1,4096]{1,0:T(1,128)}, u32[]{:S(2)}) copy-start(s32[1,4096]{1,0:T(1,128)} %param.13) | copy-start | bytes 49156
  153.5 33.0 %all-to-all-start = ((bf16[128,32,128]{2,0,1:T(8,128)(2,1)}), bf16[128,32,128]{2,0,1:T(8,128)(2,1)}, u32[]{:S(2)}, u32[]{:S(2)}) async-start(bf16[128,32,128]{2,0,1:T(8,128)(2,1)} %copy.41), calls=%async_computation | async-start | bytes 2097152 | tf_op jit(solution)/shard_map/all_to_all | solution.py:113
  319.7 6.0 copy-start
  319.7 56.1 %all-to-all-start.5 = ((f32[4096,1,128]{2,1,0:T(1,128)}), f32[4096,1,128]{2,1,0:T(1,128)}, u32[]{:S(2)}, u32[]{:S(2)}) async-start(f32[4096,1,128]{2,1,0:T(1,128)} %bitcast.106), calls=%async_computation.5 | async-start | bytes 4194304 | tf_op jit(solution)/shard_map/all_to_all | solution.py:138
  431.9 6.1 copy-start.4
  431.9 56.1 %all-to-all-start.4 = ((f32[4096,1,128]{2,1,0:T(1,128)}), f32[4096,1,128]{2,1,0:T(1,128)}, u32[]{:S(2)}, u32[]{:S(2)}) async-start(f32[4096,1,128]{2,1,0:T(1,128)} %bitcast.114), calls=%async_computation.4 | async-start | bytes 4194304 | tf_op jit(solution)/shard_map/all_to_all | solution.py:137
  437.9 313.8 %all-reduce.5.cloned.1.call-start = ((), (), s32[]{:S(2)}) async-start(), calls=%async_computation.7 | async-start | bytes 163840 | tf_op jit(solution)/shard_map/psum | solution.py:157
  490.7 0.6 copy-start.1
Sparse Core Ops, SparseCore 0:
  491.5 260.1 all-reduce.4

commit v2 on v0

v2 whole, which is shorter than its diff:
```python
import math

import jax
import jax.numpy as jnp
from jax import lax
from jax.sharding import PartitionSpec as P

ASKER_STREAMS = 32
SHARED_GROUPS = 4
FEATURE_SIZE = 128
QUERY_PER_KEY = 8
DOC_MOST = 512


def passed_along(value, axis, steps):
    count = lax.axis_size(axis)
    pairs = [(source, (source + steps) % count) for source in range(count)]
    return lax.ppermute(value, axis, pairs)


def shifted(value, axis, steps):
    count = lax.axis_size(axis)
    pairs = [(source, source + steps) for source in range(count) if 0 <= source + steps < count]
    return lax.ppermute(value, axis, pairs)


def butterfly_sum(value, axis):
    count = lax.axis_size(axis)
    if count & (count - 1):
        return lax.psum(value, axis)
    stride = 1
    while stride < count:
        pairs = [(source, source ^ stride) for source in range(count)]
        value = value + lax.ppermute(value, axis, pairs)
        stride *= 2
    return value


def attend_group(query_g, key_g, value_g, cot_g, visible, scaling):
    scores = (
        jnp.einsum("qhd,kd->hqk", query_g, key_g, preferred_element_type=jnp.float32) * scaling
    )
    scores = jnp.where(visible[None], scores, -1e30)
    row_max = jnp.max(scores, axis=-1, keepdims=True)
    weights = jnp.where(visible[None], jnp.exp(scores - row_max), 0.0)
    probs = weights / jnp.sum(weights, axis=-1, keepdims=True)
    probs_b = probs.astype(jnp.bfloat16)
    attn_out = jnp.einsum("hqk,kd->qhd", probs_b, value_g, preferred_element_type=jnp.float32)
    dot_out = jnp.sum(cot_g.astype(jnp.float32) * attn_out, axis=-1).T[:, :, None]
    grad_prob = jnp.einsum("qhd,kd->hqk", cot_g, value_g, preferred_element_type=jnp.float32)
    grad_score = (probs * (grad_prob - dot_out) * scaling).astype(jnp.bfloat16)
    asker = jnp.einsum("hqk,kd->qhd", grad_score, key_g, preferred_element_type=jnp.float32)
    lookup = jnp.einsum("hqk,qhd->kd", grad_score, query_g, preferred_element_type=jnp.float32)
    content = jnp.einsum("hqk,qhd->kd", probs_b, cot_g, preferred_element_type=jnp.float32)
    return asker, lookup, content


def body(queries, key_input, value_input, incoming, segments):
    shard_length = queries.shape[2]
    ctx_size = lax.axis_size("ctx")
    reach = min(-(-(DOC_MOST - 1) // shard_length), ctx_size - 1)
    window = (reach + 1) * shard_length
    width = SHARED_GROUPS * FEATURE_SIZE
    scaling = 1.0 / math.sqrt(FEATURE_SIZE)
    here = lax.axis_index("ctx")
    anchor = here * shard_length

    handed = passed_along(incoming, "pipe", -1)
    kv_own = jnp.concatenate([key_input[0, 0], value_input[0, 0]], axis=1)
    kv_window = jnp.concatenate(
        [shifted(kv_own, "ctx", steps) for steps in range(reach, 0, -1)] + [kv_own], axis=0
    )

    doc_ids = segments[0]
    doc_pad = jnp.concatenate([jnp.full((reach * shard_length,), -1, jnp.int32), doc_ids])
    key_doc = lax.dynamic_slice_in_dim(doc_pad, anchor, window, 0)
    query_doc = lax.dynamic_slice_in_dim(doc_ids, anchor, shard_length, 0)
    query_pos = jnp.arange(shard_length, dtype=jnp.int32) + reach * shard_length
    key_pos = jnp.arange(window, dtype=jnp.int32)
    visible = (query_doc[:, None] == key_doc[None, :]) & (key_pos[None, :] <= query_pos[:, None])

    query_tok = queries[0, 0].reshape(shard_length, ASKER_STREAMS, FEATURE_SIZE)
    cot_tok = handed[0, 0].reshape(shard_length, ASKER_STREAMS, FEATURE_SIZE)
    askers, lookups, contents = [], [], []
    for group in range(SHARED_GROUPS):
        heads = slice(group * QUERY_PER_KEY, (group + 1) * QUERY_PER_KEY)
        cols = slice(group * FEATURE_SIZE, (group + 1) * FEATURE_SIZE)
        vcols = slice(width + group * FEATURE_SIZE, width + (group + 1) * FEATURE_SIZE)
        asker, lookup, content = attend_group(
            query_tok[:, heads],
            kv_window[:, cols],
            kv_window[:, vcols],
            cot_tok[:, heads],
            visible,
            scaling,
        )
        askers.append(asker)
        lookups.append(lookup)
        contents.append(content)
    query_flat = jnp.concatenate(askers, axis=1).reshape(shard_length, ASKER_STREAMS * FEATURE_SIZE)
    grad_window = jnp.concatenate(lookups + contents, axis=1)

    offset_parts = jnp.concatenate([jnp.sum(query_flat, axis=0), jnp.sum(grad_window, axis=0)])
    offset_overall = butterfly_sum(butterfly_sum(offset_parts, "ctx"), "dp")
    bias_scaled = offset_overall / math.sqrt(lax.axis_size("dp") * shard_length * ctx_size)

    grad_own = grad_window[reach * shard_length :]
    for block in range(reach):
        steps = reach - block
        grad_own = grad_own + shifted(
            grad_window[block * shard_length : (block + 1) * shard_length], "ctx", -steps
        )

    query_grad = query_flat.astype(jnp.bfloat16)[None, None]
    key_grad = grad_own[:, :width].astype(jnp.bfloat16)[None, None]
    value_grad = grad_own[:, width:].astype(jnp.bfloat16)[None, None]
    return (query_grad, key_grad, value_grad, bias_scaled[None])


def solution(mesh):
    return jax.shard_map(
        body,
        mesh=mesh,
        in_specs=(
            P("pipe", "dp", "ctx", None),
            P("pipe", "dp", "ctx", None),
            P("pipe", "dp", "ctx", None),
            P("pipe", "dp", "ctx", None),
            P("dp", None),
        ),
        out_specs=(
            P("pipe", "dp", "ctx", None),
            P("pipe", "dp", "ctx", None),
            P("pipe", "dp", "ctx", None),
            P("pipe", None),
        ),
        check_vma=False,
    )
```

time: 1050 us -> 194 us (0.18)
  the two profiles are of different devices: /device:TPU:1 before, /device:TPU:16 now
where the time goes in v2:
time: 194 us; the launch traced here: 192 us
  waiting for transfers between devices  74.7 us (39%)
  starting transfers between devices  55.1 us (28%)
  matrix products  37.1 us (19%)
  local copies, waits for them, and re-layouts  17.5 us (9%)
  other arithmetic  6.87 us (4%)
    ppermute x7, waiting for transfers between devices, butterfly_sum(): value = value + lax.ppermute(value, axis, pairs)  44.1 us
    ppermute x1, waiting for transfers between devices, passed_along(): return lax.ppermute(value, axis, pairs)  30.5 us
    ppermute x8, starting transfers between devices, shifted(): return lax.ppermute(value, axis, pairs)  24.6 us
    ppermute x7, starting transfers between devices, butterfly_sum(): value = value + lax.ppermute(value, axis, pairs)  20.4 us
    unnamed x50, local copies, waits for them, and re-layouts  16 us
    sub x4, matrix products, attend_group(): weights = jnp.where(visible[None], jnp.exp(scores - row_max), 0.0)  10.5 us
    ppermute x1, starting transfers between devices, passed_along(): return lax.ppermute(value, axis, pairs)  10.2 us
    dot_general x4, matrix products, attend_group(): jnp.einsum('hqk,kd->qhd', probs_b, value_g, preferred_element_type=jnp.fl...  6.79 us
  transfers between devices with their start and end apart: 16, of which 6 were waited for; matrix products, arithmetic and copies ran while one was open for 11% of the time, Pallas kernels for 0%

profile of v2, /device:TPU:16, one launch (start us, length us, event | category | flops | bytes accessed | tf_op | source)
XLA Modules:
  0.0 192.5 jit_solution(3757138448450579708)
XLA Ops:
  1.7 1.9 collective-permute-start.3
  3.7 4.3 %collective-permute-start.2 = (bf16[128,1024]{1,0:T(8,128)(2,1)S(1)}, bf16[128,1024]{1,0:T(8,128)(2,1)S(1)}, u32[]{:S(2)}, u32[]{:S(2)}) collective-permute-start(bf16[128,1024]{1,0:T(8,128)(2,1)S(1)} %pad_maximum_fusion.1), channel_id=1, source_target_pairs={{0,8},{4,12},{8,16},{12,20},{16,24},{20,28},{24,32},{28,36},{32,40... | collective-permute-start | bytes 786440 | tf_op jit(solution)/shard_map/ppermute | solution.py:24
  8.0 4.4 %collective-permute-start.1 = (bf16[128,1024]{1,0:T(8,128)(2,1)S(1)}, bf16[128,1024]{1,0:T(8,128)(2,1)}, u32[]{:S(2)}, u32[]{:S(2)}) collective-permute-start(bf16[128,1024]{1,0:T(8,128)(2,1)S(1)} %pad_maximum_fusion.1), channel_id=1, source_target_pairs={{0,12},{4,16},{8,20},{12,24},{16,28},{20,32},{24,36},{28,40},{32,4... | collective-permute-start | bytes 786440 | tf_op jit(solution)/shard_map/ppermute | solution.py:24
  12.3 4.7 %collective-permute-start = (bf16[128,1024]{1,0:T(8,128)(2,1)S(1)}, bf16[128,1024]{1,0:T(8,128)(2,1)}, u32[]{:S(2)}, u32[]{:S(2)}) collective-permute-start(bf16[128,1024]{1,0:T(8,128)(2,1)S(1)} %pad_maximum_fusion.1), channel_id=1, source_target_pairs={{0,16},{4,20},{8,24},{12,28},{16,32},{20,36},{24,40},{28,44},{32,4... | collective-permute-start | bytes 786440 | tf_op jit(solution)/shard_map/ppermute | solution.py:24
  17.0 2.3 %copy.50 = bf16[1,1,128,4096]{2,3,1,0:T(8,128)(2,1)} copy(bf16[1,1,128,4096]{3,2,1,0:T(8,128)(2,1)} %param.8) | data formatting | bytes 2097152 | tf_op args[3]
  19.3 10.2 %collective-permute-start.4 = (bf16[1,1,128,4096]{2,3,1,0:T(8,128)(2,1)}, bf16[1,1,128,4096]{2,3,1,0:T(8,128)(2,1)}, u32[]{:S(2)}, u32[]{:S(2)}) collective-permute-start(bf16[1,1,128,4096]{2,3,1,0:T(8,128)(2,1)} %copy.50), channel_id=1, source_target_pairs={{0,384},{128,0},{256,128},{384,256},{1,385},{129,1},{257,129},{385... | collective-permute-start | bytes 3145736 | tf_op jit(solution)/shard_map/ppermute | solution.py:18
  32.8 2.6 %fusion.123 = (f32[8,128]{1,0:T(8,128)S(1)}, f32[8,128,640]{1,2,0:T(8,128)}) fusion(pred[128,640]{0,1:T(8,128)(4,1)S(1)} %fusion.50, bf16[128,32,128]{0,2,1:T(8,128)(2,1)S(1)} %bitcast.207, bf16[640,1024]{1,0:T(8,128)(2,1)S(1)} %constant_dynamic-update-slice_fusion), kind=kOutput, calls=%fused_computation.153 | convolution fusion | flops 171049600 | bytes 3215360 | tf_op jit(solution)/shard_map/sub | solution.py:45
  35.4 2.7 %fusion.117 = (f32[8,128]{1,0:T(8,128)S(1)}, f32[8,128,640]{1,2,0:T(8,128)}) fusion(pred[128,640]{0,1:T(8,128)(4,1)S(1)} %fusion.50, bf16[128,32,128]{0,2,1:T(8,128)(2,1)S(1)} %bitcast.208, bf16[640,1024]{1,0:T(8,128)(2,1)S(1)} %constant_dynamic-update-slice_fusion), kind=kOutput, calls=%fused_computation.151 | convolution fusion | flops 171049600 | bytes 3215360 | tf_op jit(solution)/shard_map/sub | solution.py:45
  38.0 2.6 %fusion.120 = (f32[8,128]{1,0:T(8,128)S(1)}, f32[8,128,640]{1,2,0:T(8,128)}) fusion(pred[128,640]{0,1:T(8,128)(4,1)S(1)} %fusion.50, bf16[128,32,128]{0,2,1:T(8,128)(2,1)S(1)} %bitcast.209, bf16[640,1024]{1,0:T(8,128)(2,1)S(1)} %constant_dynamic-update-slice_fusion), kind=kOutput, calls=%fused_computation.152 | convolution fusion | flops 171049600 | bytes 3215360 | tf_op jit(solution)/shard_map/sub | solution.py:45
  40.6 2.6 %fusion.114 = (f32[8,128]{1,0:T(8,128)S(1)}, f32[8,128,640]{1,2,0:T(8,128)}) fusion(pred[128,640]{0,1:T(8,128)(4,1)S(1)} %fusion.50, bf16[128,32,128]{0,2,1:T(8,128)(2,1)S(1)} %bitcast.210, bf16[640,1024]{1,0:T(8,128)(2,1)S(1)} %constant_dynamic-update-slice_fusion), kind=kOutput, calls=%fused_computation.150 | convolution fusion | flops 171049600 | bytes 3215360 | tf_op jit(solution)/shard_map/sub | solution.py:45
  43.3 30.5 %collective-permute-done.4 = bf16[1,1,128,4096]{2,3,1,0:T(8,128)(2,1)} collective-permute-done((bf16[1,1,128,4096]{2,3,1,0:T(8,128)(2,1)}, bf16[1,1,128,4096]{2,3,1,0:T(8,128)(2,1)}, u32[]{:S(2)}, u32[]{:S(2)}) %collective-permute-start.4) | collective-permute-done | bytes 1048608 | tf_op jit(solution)/shard_map/ppermute | solution.py:18
  73.8 2.1 %fusion.113 = (bf16[128,8,128]{0,2,1:T(8,128)(2,1)S(1)}, bf16[128,8,128]{0,2,1:T(8,128)(2,1)}, bf16[128,8,128]{0,2,1:T(8,128)(2,1)}, bf16[128,8,128]{0,2,1:T(8,128)(2,1)S(1)}) fusion(bf16[128,32,128]{0,2,1:T(8,128)(2,1)} %bitcast.9), kind=kLoop, calls=%fused_computation.149 | loop fusion | bytes 2097152
  76.1 2.6 %multiply_reduce_fusion.3 = f32[128,8]{0,1:T(8,128)S(1)} fusion(bf16[128,8,128]{2,0,1:T(8,128)(2,1)S(1)} %copy.142, bf16[640,1024]{1,0:T(8,128)(2,1)S(1)} %constant_dynamic-update-slice_fusion, f32[8,128,640]{1,2,0:T(8,128)} %get-tuple-element.29, f32[8,128]{1,0:T(8,128)S(1)} %get-tuple-element.28), kind=kOutput, calls=%fused_computation.87 | convolution fusion | flops 169475072 | bytes 3055616 | tf_op jit(solution)/shard_map/hqk,kd->qhd/dot_general | solution.py:48
  78.7 1.6 fusion.15
  80.7 1.5 fusion.41
  82.2 1.8 copy.146
  84.0 1.8 copy.144
  86.6 2.7 %multiply_reduce_fusion.1 = f32[128,8]{0,1:T(8,128)S(1)} fusion(bf16[128,8,128]{2,0,1:T(8,128)(2,1)} %copy.146, bf16[640,1024]{1,0:T(8,128)(2,1)} %copy-done.6, f32[8,128,640]{1,2,0:T(8,128)} %get-tuple-element.25, f32[8,128]{1,0:T(8,128)S(1)} %get-tuple-element.24), kind=kOutput, calls=%fused_computation.85 | convolution fusion | flops 169475072 | bytes 3055616 | tf_op jit(solution)/shard_map/hqk,kd->qhd/dot_general | solution.py:48
  89.7 1.7 fusion.9
  91.4 1.2 convolution_bitcast_fusion.2
  93.4 1.7 fusion.12
  95.1 1.2 convolution_bitcast_fusion.4
  98.1 1.6 fusion.6
  99.7 1.4 convolution_bitcast_fusion
  101.6 1.5 fusion.37
  103.1 1.5 fusion.36
  104.6 1.5 fusion.35
  106.1 1.5 fusion.34
  107.9 2.0 %fusion.32 = f32[32,128]{1,0:T(8,128)S(1)} fusion(f32[128,8,128]{0,2,1:T(8,128)} %convolution_bitcast_fusion, f32[128,8,128]{0,2,1:T(8,128)} %convolution_bitcast_fusion.2, f32[128,8,128]{0,2,1:T(8,128)} %convolution_bitcast_fusion.4, f32[128,8,128]{0,2,1:T(8,128)S(1)} %convolution_bitcast_fusion.6), kind=kLoop, calls=%fused_computation.57 | loop fusion | flops 2093056 | bytes 2113536 | tf_op jit(solution)/shard_map/reduce_sum | solution.py:103
  109.9 2.1 %collective-permute-start.9 = (f32[5120]{0:T(1024)S(1)}, f32[5120]{0:T(1024)S(1)}, u32[]{:S(2)}, u32[]{:S(2)}) collective-permute-start(f32[5120]{0:T(1024)S(1)} %pad_maximum_fusion.2), channel_id=1, source_target_pairs={{0,4},{4,0},{8,12},{12,8},{16,20},{20,16},{24,28},{28,24},{32,36},... | collective-permute-start | bytes 61448 | tf_op jit(solution)/shard_map/ppermute | solution.py:34
  112.0 1.3 fusion.112
  113.3 1.9 collective-permute-start.5
  115.2 1.9 collective-permute-start.8
  117.1 3.5 %collective-permute-start.7 = (f32[128,1024]{0,1:T(8,128)}, f32[128,1024]{0,1:T(8,128)}, u32[]{:S(2)}, u32[]{:S(2)}) collective-permute-start(f32[128,1024]{0,1:T(8,128)} %get-tuple-element.14), channel_id=1, source_target_pairs={{8,0},{12,4},{16,8},{20,12},{24,16},{28,20},{32,24},{36,28},{40,32... | collective-permute-start | bytes 1572872 | tf_op jit(solution)/shard_map/ppermute | solution.py:24
  120.7 1.9 collective-permute-start.6
  122.6 2.5 %collective-permute-start.10 = (f32[5120]{0:T(1024)S(1)}, f32[5120]{0:T(1024)S(1)}, u32[]{:S(2)}, u32[]{:S(2)}) collective-permute-start(f32[5120]{0:T(1024)S(1)} %fusion.95), channel_id=1, source_target_pairs={{0,8},{4,12},{8,0},{12,4},{16,24},{20,28},{24,16},{28,20},{32,40},... | collective-permute-start | bytes 61448 | tf_op jit(solution)/shard_map/ppermute | solution.py:34
  125.1 17.4 %collective-permute-done.10 = f32[5120]{0:T(1024)S(1)} collective-permute-done((f32[5120]{0:T(1024)S(1)}, f32[5120]{0:T(1024)S(1)}, u32[]{:S(2)}, u32[]{:S(2)}) %collective-permute-start.10) | collective-permute-done | bytes 20512 | tf_op jit(solution)/shard_map/ppermute | solution.py:34
  142.5 3.4 %collective-permute-start.11 = (f32[5120]{0:T(1024)S(1)}, f32[5120]{0:T(1024)S(1)}, u32[]{:S(2)}, u32[]{:S(2)}) collective-permute-start(f32[5120]{0:T(1024)S(1)} %add.60), channel_id=1, source_target_pairs={{0,16},{4,20},{8,24},{12,28},{16,0},{20,4},{24,8},{28,12},{32,48},... | collective-permute-start | bytes 61448 | tf_op jit(solution)/shard_map/ppermute | solution.py:34
  145.9 12.6 %collective-permute-done.11 = f32[5120]{0:T(1024)S(1)} collective-permute-done((f32[5120]{0:T(1024)S(1)}, f32[5120]{0:T(1024)S(1)}, u32[]{:S(2)}, u32[]{:S(2)}) %collective-permute-start.11) | collective-permute-done | bytes 20512 | tf_op jit(solution)/shard_map/ppermute | solution.py:34
  158.5 1.9 collective-permute-start.12
  160.4 4.6 %collective-permute-done.12 = f32[5120]{0:T(1024)S(1)} collective-permute-done((f32[5120]{0:T(1024)S(1)}, f32[5120]{0:T(1024)S(1)}, u32[]{:S(2)}, u32[]{:S(2)}) %collective-permute-start.12) | collective-permute-done | bytes 20512 | tf_op jit(solution)/shard_map/ppermute | solution.py:34
  165.0 2.3 %collective-permute-start.13 = (f32[5120]{0:T(1024)S(1)}, f32[5120]{0:T(1024)S(1)}, u32[]{:S(2)}, u32[]{:S(2)}) collective-permute-start(f32[5120]{0:T(1024)S(1)} %add.62), channel_id=1, source_target_pairs={{0,64},{4,68},{8,72},{12,76},{16,80},{20,84},{24,88},{28,92},{32,9... | collective-permute-start | bytes 61448 | tf_op jit(solution)/shard_map/ppermute | solution.py:34
  167.4 7.3 %collective-permute-done.13 = f32[5120]{0:T(1024)S(1)} collective-permute-done((f32[5120]{0:T(1024)S(1)}, f32[5120]{0:T(1024)S(1)}, u32[]{:S(2)}, u32[]{:S(2)}) %collective-permute-start.13) | collective-permute-done | bytes 20512 | tf_op jit(solution)/shard_map/ppermute | solution.py:34
  174.6 3.4 %collective-permute-start.14 = (f32[5120]{0:T(1024)S(1)}, f32[5120]{0:T(1024)S(1)}, u32[]{:S(2)}, u32[]{:S(2)}) collective-permute-start(f32[5120]{0:T(1024)S(1)} %add.63), channel_id=1, source_target_pairs={{0,1},{1,0},{2,3},{3,2},{4,5},{5,4},{6,7},{7,6},{8,9},{9,8},{10,11... | collective-permute-start | bytes 61448 | tf_op jit(solution)/shard_map/ppermute | solution.py:34
  178.0 2.3 %collective-permute-done.14 = f32[5120]{0:T(1024)S(1)} collective-permute-done((f32[5120]{0:T(1024)S(1)}, f32[5120]{0:T(1024)S(1)}, u32[]{:S(2)}, u32[]{:S(2)}) %collective-permute-start.14) | collective-permute-done | bytes 20512 | tf_op jit(solution)/shard_map/ppermute | solution.py:34
  180.3 4.9 %collective-permute-start.15 = (f32[5120]{0:T(1024)S(1)}, f32[5120]{0:T(1024)S(1)}, u32[]{:S(2)}, u32[]{:S(2)}) collective-permute-start(f32[5120]{0:T(1024)S(1)} %add.64), channel_id=1, source_target_pairs={{0,2},{1,3},{2,0},{3,1},{4,6},{5,7},{6,4},{7,5},{8,10},{9,11},{10,... | collective-permute-start | bytes 61448 | tf_op jit(solution)/shard_map/ppermute | solution.py:34
  186.4 2.3 %copy.94 = bf16[1,1,128,4096]{3,2,1,0:T(8,128)(2,1)} copy(bf16[1,1,128,4096]{2,3,1,0:T(8,128)(2,1)} %bitcast.206) | data formatting | bytes 2097152
  189.3 1.6 fusion.49
  (78 shorter events, 12.8 us)
Async XLA Ops:
  0.6 28.9 %copy-start.12 = (s32[1,4096]{1,0:T(1,128)S(1)}, s32[1,4096]{1,0:T(1,128)}, u32[]{:S(2)}) copy-start(s32[1,4096]{1,0:T(1,128)} %param.9) | copy-start | bytes 49156
  0.6 29.1 %copy-start.5 = (bf16[1,1,128,4096]{3,2,1,0:T(8,128)(2,1)S(1)}, bf16[1,1,128,4096]{3,2,1,0:T(8,128)(2,1)}, u32[]{:S(2)}) copy-start(bf16[1,1,128,4096]{3,2,1,0:T(8,128)(2,1)} %param.5) | copy-start | bytes 3145732
  1.7 30.9 %collective-permute-start.3 = (bf16[128,1024]{1,0:T(8,128)(2,1)S(1)}, bf16[128,1024]{1,0:T(8,128)(2,1)S(1)}, u32[]{:S(2)}, u32[]{:S(2)}) collective-permute-start(bf16[128,1024]{1,0:T(8,128)(2,1)S(1)} %pad_maximum_fusion.1), channel_id=1, source_target_pairs={{0,4},{4,8},{8,12},{12,16},{16,20},{20,24},{24,28},{28,32},{32,36}... | collective-permute-start | bytes 786440 | tf_op jit(solution)/shard_map/ppermute | solution.py:24
  3.7 29.0 %collective-permute-start.2 = (bf16[128,1024]{1,0:T(8,128)(2,1)S(1)}, bf16[128,1024]{1,0:T(8,128)(2,1)S(1)}, u32[]{:S(2)}, u32[]{:S(2)}) collective-permute-start(bf16[128,1024]{1,0:T(8,128)(2,1)S(1)} %pad_maximum_fusion.1), channel_id=1, source_target_pairs={{0,8},{4,12},{8,16},{12,20},{16,24},{20,28},{24,32},{28,36},{32,40... | collective-permute-start | bytes 786440 | tf_op jit(solution)/shard_map/ppermute | solution.py:24
  8.0 23.7 %collective-permute-start.1 = (bf16[128,1024]{1,0:T(8,128)(2,1)S(1)}, bf16[128,1024]{1,0:T(8,128)(2,1)}, u32[]{:S(2)}, u32[]{:S(2)}) collective-permute-start(bf16[128,1024]{1,0:T(8,128)(2,1)S(1)} %pad_maximum_fusion.1), channel_id=1, source_target_pairs={{0,12},{4,16},{8,20},{12,24},{16,28},{20,32},{24,36},{28,40},{32,4... | collective-permute-start | bytes 786440 | tf_op jit(solution)/shard_map/ppermute | solution.py:24
  12.3 18.1 %collective-permute-start = (bf16[128,1024]{1,0:T(8,128)(2,1)S(1)}, bf16[128,1024]{1,0:T(8,128)(2,1)}, u32[]{:S(2)}, u32[]{:S(2)}) collective-permute-start(bf16[128,1024]{1,0:T(8,128)(2,1)S(1)} %pad_maximum_fusion.1), channel_id=1, source_target_pairs={{0,16},{4,20},{8,24},{12,28},{16,32},{20,36},{24,40},{28,44},{32,4... | collective-permute-start | bytes 786440 | tf_op jit(solution)/shard_map/ppermute | solution.py:24
  19.3 13.4 %copy-start.8 = (bf16[1,1,128,512]{3,2,1,0:T(8,128)(2,1)S(1)}, bf16[1,1,128,512]{3,2,1,0:T(8,128)(2,1)}, u32[]{:S(2)}) copy-start(bf16[1,1,128,512]{3,2,1,0:T(8,128)(2,1)} %param.7) | copy-start | bytes 393220
  19.3 13.4 %copy-start.9 = (bf16[1,1,128,512]{3,2,1,0:T(8,128)(2,1)S(1)}, bf16[1,1,128,512]{3,2,1,0:T(8,128)(2,1)}, u32[]{:S(2)}) copy-start(bf16[1,1,128,512]{3,2,1,0:T(8,128)(2,1)} %param.6) | copy-start | bytes 393220
  19.3 54.5 %collective-permute-start.4 = (bf16[1,1,128,4096]{2,3,1,0:T(8,128)(2,1)}, bf16[1,1,128,4096]{2,3,1,0:T(8,128)(2,1)}, u32[]{:S(2)}, u32[]{:S(2)}) collective-permute-start(bf16[1,1,128,4096]{2,3,1,0:T(8,128)(2,1)} %copy.50), channel_id=1, source_target_pairs={{0,384},{128,0},{256,128},{384,256},{1,385},{129,1},{257,129},{385... | collective-permute-start | bytes 3145736 | tf_op jit(solution)/shard_map/ppermute | solution.py:18
  30.4 10.2 %copy-start.3 = (bf16[1,1,128,4096]{2,3,1,0:T(8,128)(2,1)}, bf16[1,1,128,4096]{2,3,1,0:T(8,128)(2,1)S(1)}, u32[]{:S(2)}) copy-start(bf16[1,1,128,4096]{2,3,1,0:T(8,128)(2,1)S(1)} %copy.48) | copy-start | bytes 3145732
  32.7 47.5 %copy-start.6 = (bf16[640,1024]{1,0:T(8,128)(2,1)}, bf16[640,1024]{1,0:T(8,128)(2,1)S(1)}, u32[]{:S(2)}) copy-start(bf16[640,1024]{1,0:T(8,128)(2,1)S(1)} %constant_dynamic-update-slice_fusion) | copy-start | bytes 3932164
  76.0 2.6 %copy-start.15 = (f32[8,128,640]{1,2,0:T(8,128)S(1)}, f32[8,128,640]{1,2,0:T(8,128)}, u32[]{:S(2)}) copy-start(f32[8,128,640]{1,2,0:T(8,128)} %get-tuple-element.29) | copy-start | bytes 7864324
  86.6 2.7 %copy-start.7 = (bf16[640,1024]{1,0:T(8,128)(2,1)S(1)}, bf16[640,1024]{1,0:T(8,128)(2,1)}, u32[]{:S(2)}) copy-start(bf16[640,1024]{1,0:T(8,128)(2,1)} %copy-done.6) | copy-start | bytes 3932164
  86.6 3.1 %copy-start.13 = (f32[8,128,640]{1,2,0:T(8,128)S(1)}, f32[8,128,640]{1,2,0:T(8,128)}, u32[]{:S(2)}) copy-start(f32[8,128,640]{1,2,0:T(8,128)} %get-tuple-element.25) | copy-start | bytes 7864324
  89.7 2.9 %copy-start.11 = (bf16[128,8,128]{2,0,1:T(8,128)(2,1)S(1)}, bf16[128,8,128]{2,0,1:T(8,128)(2,1)}, u32[]{:S(2)}) copy-start(bf16[128,8,128]{2,0,1:T(8,128)(2,1)} %copy.144) | copy-start | bytes 786436
  89.7 2.9 %copy-start.17 = (f32[8,128,640]{1,2,0:T(8,128)S(1)}, f32[8,128,640]{1,2,0:T(8,128)}, u32[]{:S(2)}) copy-start(f32[8,128,640]{1,2,0:T(8,128)} %get-tuple-element.27) | copy-start | bytes 7864324
  93.4 2.9 %copy-start.4 = (bf16[1,1,128,4096]{2,3,1,0:T(8,128)(2,1)S(1)}, bf16[1,1,128,4096]{2,3,1,0:T(8,128)(2,1)}, u32[]{:S(2)}) copy-start(bf16[1,1,128,4096]{2,3,1,0:T(8,128)(2,1)} %copy-done.3) | copy-start | bytes 3145732
  95.0 2.3 %copy-start.10 = (bf16[128,8,128]{2,0,1:T(8,128)(2,1)S(1)}, bf16[128,8,128]{2,0,1:T(8,128)(2,1)}, u32[]{:S(2)}) copy-start(bf16[128,8,128]{2,0,1:T(8,128)(2,1)} %copy.148) | copy-start | bytes 786436
  95.1 2.3 %copy-start.14 = (f32[8,128,640]{1,2,0:T(8,128)S(1)}, f32[8,128,640]{1,2,0:T(8,128)}, u32[]{:S(2)}) copy-start(f32[8,128,640]{1,2,0:T(8,128)} %get-tuple-element.23) | copy-start | bytes 7864324
  99.7 1.9 %copy-start.16 = (f32[8,128,640]{1,2,0:T(8,128)S(1)}, f32[8,128,640]{1,2,0:T(8,128)}, u32[]{:S(2)}) copy-start(f32[8,128,640]{1,2,0:T(8,128)} %get-tuple-element.29) | copy-start | bytes 7864324
  109.9 75.4 %copy-start = (f32[128,8,128]{0,2,1:T(8,128)S(1)}, f32[128,8,128]{0,2,1:T(8,128)}, u32[]{:S(2)}) copy-start(f32[128,8,128]{0,2,1:T(8,128)} %convolution_bitcast_fusion.2) | copy-start | bytes 1572868
  109.9 75.4 %copy-start.1 = (f32[128,8,128]{0,2,1:T(8,128)S(1)}, f32[128,8,128]{0,2,1:T(8,128)}, u32[]{:S(2)}) copy-start(f32[128,8,128]{0,2,1:T(8,128)} %convolution_bitcast_fusion.4) | copy-start | bytes 1572868
  109.9 75.4 %copy-start.2 = (f32[128,8,128]{0,2,1:T(8,128)S(1)}, f32[128,8,128]{0,2,1:T(8,128)}, u32[]{:S(2)}) copy-start(f32[128,8,128]{0,2,1:T(8,128)} %convolution_bitcast_fusion) | copy-start | bytes 1572868
  109.9 12.7 %collective-permute-start.9 = (f32[5120]{0:T(1024)S(1)}, f32[5120]{0:T(1024)S(1)}, u32[]{:S(2)}, u32[]{:S(2)}) collective-permute-start(f32[5120]{0:T(1024)S(1)} %pad_maximum_fusion.2), channel_id=1, source_target_pairs={{0,4},{4,0},{8,12},{12,8},{16,20},{20,16},{24,28},{28,24},{32,36},... | collective-permute-start | bytes 61448 | tf_op jit(solution)/shard_map/ppermute | solution.py:34
  113.3 76.0 %collective-permute-start.5 = (f32[128,1024]{0,1:T(8,128)}, f32[128,1024]{0,1:T(8,128)}, u32[]{:S(2)}, u32[]{:S(2)}) collective-permute-start(f32[128,1024]{0,1:T(8,128)} %get-tuple-element.12), channel_id=1, source_target_pairs={{16,0},{20,4},{24,8},{28,12},{32,16},{36,20},{40,24},{44,28},{48,3... | collective-permute-start | bytes 1572872 | tf_op jit(solution)/shard_map/ppermute | solution.py:24
  115.2 74.1 %collective-permute-start.8 = (f32[128,1024]{0,1:T(8,128)}, f32[128,1024]{0,1:T(8,128)}, u32[]{:S(2)}, u32[]{:S(2)}) collective-permute-start(f32[128,1024]{0,1:T(8,128)} %get-tuple-element.13), channel_id=1, source_target_pairs={{4,0},{8,4},{12,8},{16,12},{20,16},{24,20},{28,24},{32,28},{36,32}... | collective-permute-start | bytes 1572872 | tf_op jit(solution)/shard_map/ppermute | solution.py:24
  117.1 72.1 %collective-permute-start.7 = (f32[128,1024]{0,1:T(8,128)}, f32[128,1024]{0,1:T(8,128)}, u32[]{:S(2)}, u32[]{:S(2)}) collective-permute-start(f32[128,1024]{0,1:T(8,128)} %get-tuple-element.14), channel_id=1, source_target_pairs={{8,0},{12,4},{16,8},{20,12},{24,16},{28,20},{32,24},{36,28},{40,32... | collective-permute-start | bytes 1572872 | tf_op jit(solution)/shard_map/ppermute | solution.py:24
  120.7 68.6 %collective-permute-start.6 = (f32[128,1024]{0,1:T(8,128)}, f32[128,1024]{0,1:T(8,128)}, u32[]{:S(2)}, u32[]{:S(2)}) collective-permute-start(f32[128,1024]{0,1:T(8,128)} %get-tuple-element.15), channel_id=1, source_target_pairs={{12,0},{16,4},{20,8},{24,12},{28,16},{32,20},{36,24},{40,28},{44,3... | collective-permute-start | bytes 1572872 | tf_op jit(solution)/shard_map/ppermute | solution.py:24
  122.6 19.9 %collective-permute-start.10 = (f32[5120]{0:T(1024)S(1)}, f32[5120]{0:T(1024)S(1)}, u32[]{:S(2)}, u32[]{:S(2)}) collective-permute-start(f32[5120]{0:T(1024)S(1)} %fusion.95), channel_id=1, source_target_pairs={{0,8},{4,12},{8,0},{12,4},{16,24},{20,28},{24,16},{28,20},{32,40},... | collective-permute-start | bytes 61448 | tf_op jit(solution)/shard_map/ppermute | solution.py:34
  142.5 15.9 %collective-permute-start.11 = (f32[5120]{0:T(1024)S(1)}, f32[5120]{0:T(1024)S(1)}, u32[]{:S(2)}, u32[]{:S(2)}) collective-permute-start(f32[5120]{0:T(1024)S(1)} %add.60), channel_id=1, source_target_pairs={{0,16},{4,20},{8,24},{12,28},{16,0},{20,4},{24,8},{28,12},{32,48},... | collective-permute-start | bytes 61448 | tf_op jit(solution)/shard_map/ppermute | solution.py:34
  158.5 6.6 %collective-permute-start.12 = (f32[5120]{0:T(1024)S(1)}, f32[5120]{0:T(1024)S(1)}, u32[]{:S(2)}, u32[]{:S(2)}) collective-permute-start(f32[5120]{0:T(1024)S(1)} %add.61), channel_id=1, source_target_pairs={{0,32},{4,36},{8,40},{12,44},{16,48},{20,52},{24,56},{28,60},{32,0... | collective-permute-start | bytes 61448 | tf_op jit(solution)/shard_map/ppermute | solution.py:34
  165.0 9.6 %collective-permute-start.13 = (f32[5120]{0:T(1024)S(1)}, f32[5120]{0:T(1024)S(1)}, u32[]{:S(2)}, u32[]{:S(2)}) collective-permute-start(f32[5120]{0:T(1024)S(1)} %add.62), channel_id=1, source_target_pairs={{0,64},{4,68},{8,72},{12,76},{16,80},{20,84},{24,88},{28,92},{32,9... | collective-permute-start | bytes 61448 | tf_op jit(solution)/shard_map/ppermute | solution.py:34
  174.6 5.7 %collective-permute-start.14 = (f32[5120]{0:T(1024)S(1)}, f32[5120]{0:T(1024)S(1)}, u32[]{:S(2)}, u32[]{:S(2)}) collective-permute-start(f32[5120]{0:T(1024)S(1)} %add.63), channel_id=1, source_target_pairs={{0,1},{1,0},{2,3},{3,2},{4,5},{5,4},{6,7},{7,6},{8,9},{9,8},{10,11... | collective-permute-start | bytes 61448 | tf_op jit(solution)/shard_map/ppermute | solution.py:34
  180.3 8.4 %collective-permute-start.15 = (f32[5120]{0:T(1024)S(1)}, f32[5120]{0:T(1024)S(1)}, u32[]{:S(2)}, u32[]{:S(2)}) collective-permute-start(f32[5120]{0:T(1024)S(1)} %add.64), channel_id=1, source_target_pairs={{0,2},{1,3},{2,0},{3,1},{4,6},{5,7},{6,4},{7,5},{8,10},{9,11},{10,... | collective-permute-start | bytes 61448 | tf_op jit(solution)/shard_map/ppermute | solution.py:34

commit v3 on v2

--- a/solution.py
+++ b/solution.py
@@ -24,15 +24,31 @@
     return lax.ppermute(value, axis, pairs)
 
 
-def butterfly_sum(value, axis):
+def radix_rounds(count):
+    rounds, stride = [], 1
+    while stride < count:
+        radix = 4 if count % (stride * 4) == 0 else 2
+        rounds.append((stride, radix))
+        stride *= radix
+    return rounds
+
+
+def group_sum(value, axis):
     count = lax.axis_size(axis)
     if count & (count - 1):
         return lax.psum(value, axis)
-    stride = 1
-    while stride < count:
-        pairs = [(source, source ^ stride) for source in range(count)]
-        value = value + lax.ppermute(value, axis, pairs)
-        stride *= 2
+    here = lax.axis_index(axis)
+    for stride, radix in radix_rounds(count):
+        got = [value] + [
+            lax.ppermute(value, axis, [(i, i ^ (t * stride)) for i in range(count)])
+            for t in range(1, radix)
+        ]
+        stack = jnp.stack(got)
+        spot = (here // stride) % radix
+        ordered = jnp.take(stack, spot ^ jnp.arange(radix), axis=0)
+        while ordered.shape[0] > 1:
+            ordered = ordered[0::2] + ordered[1::2]
+        value = ordered[0]
     return value
 
 
@@ -65,7 +81,11 @@
     here = lax.axis_index("ctx")
     anchor = here * shard_length
 
-    handed = passed_along(incoming, "pipe", -1)
+    group_cols = QUERY_PER_KEY * FEATURE_SIZE
+    cot_groups = [
+        passed_along(incoming[0, 0, :, g * group_cols : (g + 1) * group_cols], "pipe", -1)
+        for g in range(SHARED_GROUPS)
+    ]
     kv_own = jnp.concatenate([key_input[0, 0], value_input[0, 0]], axis=1)
     kv_window = jnp.concatenate(
         [shifted(kv_own, "ctx", steps) for steps in range(reach, 0, -1)] + [kv_own], axis=0
@@ -80,7 +100,6 @@
     visible = (query_doc[:, None] == key_doc[None, :]) & (key_pos[None, :] <= query_pos[:, None])
 
     query_tok = queries[0, 0].reshape(shard_length, ASKER_STREAMS, FEATURE_SIZE)
-    cot_tok = handed[0, 0].reshape(shard_length, ASKER_STREAMS, FEATURE_SIZE)
     askers, lookups, contents = [], [], []
     for group in range(SHARED_GROUPS):
         heads = slice(group * QUERY_PER_KEY, (group + 1) * QUERY_PER_KEY)
@@ -90,7 +109,7 @@
             query_tok[:, heads],
             kv_window[:, cols],
             kv_window[:, vcols],
-            cot_tok[:, heads],
+            cot_groups[group].reshape(shard_length, QUERY_PER_KEY, FEATURE_SIZE),
             visible,
             scaling,
         )
@@ -101,7 +120,7 @@
     grad_window = jnp.concatenate(lookups + contents, axis=1)
 
     offset_parts = jnp.concatenate([jnp.sum(query_flat, axis=0), jnp.sum(grad_window, axis=0)])
-    offset_overall = butterfly_sum(butterfly_sum(offset_parts, "ctx"), "dp")
+    offset_overall = group_sum(group_sum(offset_parts, "ctx"), "dp")
     bias_scaled = offset_overall / math.sqrt(lax.axis_size("dp") * shard_length * ctx_size)
 
     grad_own = grad_window[reach * shard_length :]

time: 194 us -> 192 us (0.990)
  the two profiles are of different devices: /device:TPU:16 before, /device:TPU:1 now
where the time goes in v3:
time: 192 us; the launch traced here: 191 us
  starting transfers between devices  84.5 us (44%)
  waiting for transfers between devices  45.7 us (24%)
  matrix products  30.8 us (16%)
  local copies, waits for them, and re-layouts  18.3 us (10%)
  other arithmetic  9.75 us (5%)
    ppermute x10, starting transfers between devices, group_sum(): lax.ppermute(value, axis, [(i, i ^ t * stride) for i in range(count)])  45.2 us
    ppermute x8, waiting for transfers between devices, shifted(): return lax.ppermute(value, axis, pairs)  33.3 us
    ppermute x8, starting transfers between devices, shifted(): return lax.ppermute(value, axis, pairs)  23.6 us
    ppermute x4, starting transfers between devices, passed_along(): return lax.ppermute(value, axis, pairs)  15.8 us
    unnamed x44, local copies, waits for them, and re-layouts  12.4 us
    sub x4, matrix products, attend_group(): weights = jnp.where(visible[None], jnp.exp(scores - row_max), 0.0)  10.4 us
    ppermute x10, waiting for transfers between devices, group_sum(): lax.ppermute(value, axis, [(i, i ^ t * stride) for i in range(count)])  6.65 us
    ppermute x4, waiting for transfers between devices, passed_along(): return lax.ppermute(value, axis, pairs)  5.76 us
  transfers between devices with their start and end apart: 22, of which 9 were waited for; matrix products, arithmetic and copies ran while one was open for 20% of the time, Pallas kernels for 0%

profile of v3, /device:TPU:1, one launch (start us, length us, event | category | flops | bytes accessed | tf_op | source)
XLA Modules:
  0.0 190.7 jit_solution(15268191184051333848)
XLA Ops:
  0.7 1.8 pad_maximum_fusion.1
  2.4 5.4 %collective-permute-start.3 = (bf16[128,1024]{1,0:T(8,128)(2,1)}, bf16[128,1024]{1,0:T(8,128)(2,1)}, u32[]{:S(2)}, u32[]{:S(2)}) collective-permute-start(bf16[128,1024]{1,0:T(8,128)(2,1)} %pad_maximum_fusion.1), channel_id=1, source_target_pairs={{0,4},{4,8},{8,12},{12,16},{16,20},{20,24},{24,28},{28,32},{32,36}... | collective-permute-start | bytes 786440 | tf_op jit(solution)/shard_map/ppermute | solution.py:24
  7.8 3.0 %collective-permute-start.2 = (bf16[128,1024]{1,0:T(8,128)(2,1)}, bf16[128,1024]{1,0:T(8,128)(2,1)}, u32[]{:S(2)}, u32[]{:S(2)}) collective-permute-start(bf16[128,1024]{1,0:T(8,128)(2,1)} %pad_maximum_fusion.1), channel_id=1, source_target_pairs={{0,8},{4,12},{8,16},{12,20},{16,24},{20,28},{24,32},{28,36},{32,40... | collective-permute-start | bytes 786440 | tf_op jit(solution)/shard_map/ppermute | solution.py:24
  10.8 3.1 %collective-permute-start.1 = (bf16[128,1024]{1,0:T(8,128)(2,1)}, bf16[128,1024]{1,0:T(8,128)(2,1)}, u32[]{:S(2)}, u32[]{:S(2)}) collective-permute-start(bf16[128,1024]{1,0:T(8,128)(2,1)} %pad_maximum_fusion.1), channel_id=1, source_target_pairs={{0,12},{4,16},{8,20},{12,24},{16,28},{20,32},{24,36},{28,40},{32,4... | collective-permute-start | bytes 786440 | tf_op jit(solution)/shard_map/ppermute | solution.py:24
  13.9 3.2 %collective-permute-start = (bf16[128,1024]{1,0:T(8,128)(2,1)}, bf16[128,1024]{1,0:T(8,128)(2,1)}, u32[]{:S(2)}, u32[]{:S(2)}) collective-permute-start(bf16[128,1024]{1,0:T(8,128)(2,1)} %pad_maximum_fusion.1), channel_id=1, source_target_pairs={{0,16},{4,20},{8,24},{12,28},{16,32},{20,36},{24,40},{28,44},{32,4... | collective-permute-start | bytes 786440 | tf_op jit(solution)/shard_map/ppermute | solution.py:24
  17.1 1.3 fusion.106
  18.6 9.8 %collective-permute-start.7 = (bf16[128,1024]{0,1:T(8,128)(2,1)S(1)}, bf16[128,1024]{0,1:T(8,128)(2,1)}, u32[]{:S(2)}, u32[]{:S(2)}) collective-permute-start(bf16[128,1024]{0,1:T(8,128)(2,1)S(1)} %bitcast.249), channel_id=1, source_target_pairs={{0,384},{128,0},{256,128},{384,256},{1,385},{129,1},{257,129},{385... | collective-permute-start | bytes 786440 | tf_op jit(solution)/shard_map/ppermute | solution.py:18
  32.2 2.2 %collective-permute-start.5 = (bf16[128,1024]{0,1:T(8,128)(2,1)}, bf16[128,1024]{0,1:T(8,128)(2,1)}, u32[]{:S(2)}, u32[]{:S(2)}) collective-permute-start(bf16[128,1024]{0,1:T(8,128)(2,1)} %bitcast.20), channel_id=1, source_target_pairs={{0,384},{128,0},{256,128},{384,256},{1,385},{129,1},{257,129},{385... | collective-permute-start | bytes 786440 | tf_op jit(solution)/shard_map/ppermute | solution.py:18
  35.4 1.9 %collective-permute-start.6 = (bf16[128,1024]{0,1:T(8,128)(2,1)}, bf16[128,1024]{0,1:T(8,128)(2,1)S(1)}, u32[]{:S(2)}, u32[]{:S(2)}) collective-permute-start(bf16[128,1024]{0,1:T(8,128)(2,1)} %bitcast.31), channel_id=1, source_target_pairs={{0,384},{128,0},{256,128},{384,256},{1,385},{129,1},{257,129},{385... | collective-permute-start | bytes 786440 | tf_op jit(solution)/shard_map/ppermute | solution.py:18
  38.3 1.9 %collective-permute-start.4 = (bf16[128,1024]{0,1:T(8,128)(2,1)}, bf16[128,1024]{0,1:T(8,128)(2,1)S(1)}, u32[]{:S(2)}, u32[]{:S(2)}) collective-permute-start(bf16[128,1024]{0,1:T(8,128)(2,1)} %bitcast.250), channel_id=1, source_target_pairs={{0,384},{128,0},{256,128},{384,256},{1,385},{129,1},{257,129},{385... | collective-permute-start | bytes 786440 | tf_op jit(solution)/shard_map/ppermute | solution.py:18
  42.2 2.6 %fusion.116 = (f32[8,128]{1,0:T(8,128)S(1)}, f32[8,128,640]{1,2,0:T(8,128)}) fusion(pred[128,640]{0,1:T(8,128)(4,1)S(1)} %fusion.50, bf16[128,32,128]{0,2,1:T(8,128)(2,1)S(1)} %bitcast.237, bf16[640,1024]{1,0:T(8,128)(2,1)S(1)} %constant_dynamic-update-slice_fusion), kind=kOutput, calls=%fused_computation.174 | convolution fusion | flops 171049600 | bytes 3215360 | tf_op jit(solution)/shard_map/sub | solution.py:61
  44.9 2.6 %fusion.110 = (f32[8,128]{1,0:T(8,128)S(1)}, f32[8,128,640]{1,2,0:T(8,128)}) fusion(pred[128,640]{0,1:T(8,128)(4,1)S(1)} %fusion.50, bf16[128,32,128]{0,2,1:T(8,128)(2,1)S(1)} %bitcast.238, bf16[640,1024]{1,0:T(8,128)(2,1)S(1)} %constant_dynamic-update-slice_fusion), kind=kOutput, calls=%fused_computation.172 | convolution fusion | flops 171049600 | bytes 3215360 | tf_op jit(solution)/shard_map/sub | solution.py:61
  47.5 2.6 %fusion.113 = (f32[8,128]{1,0:T(8,128)S(1)}, f32[8,128,640]{1,2,0:T(8,128)}) fusion(pred[128,640]{0,1:T(8,128)(4,1)S(1)} %fusion.50, bf16[128,32,128]{0,2,1:T(8,128)(2,1)S(1)} %bitcast.239, bf16[640,1024]{1,0:T(8,128)(2,1)S(1)} %constant_dynamic-update-slice_fusion), kind=kOutput, calls=%fused_computation.173 | convolution fusion | flops 171049600 | bytes 3215360 | tf_op jit(solution)/shard_map/sub | solution.py:61
  50.1 2.6 %fusion.107 = (f32[8,128]{1,0:T(8,128)S(1)}, f32[8,128,640]{1,2,0:T(8,128)}) fusion(pred[128,640]{0,1:T(8,128)(4,1)S(1)} %fusion.50, bf16[128,32,128]{0,2,1:T(8,128)(2,1)S(1)} %bitcast.240, bf16[640,1024]{1,0:T(8,128)(2,1)S(1)} %constant_dynamic-update-slice_fusion), kind=kOutput, calls=%fused_computation.171 | convolution fusion | flops 171049600 | bytes 3215360 | tf_op jit(solution)/shard_map/sub | solution.py:61
  52.7 5.8 %collective-permute-done.4 = bf16[128,1024]{0,1:T(8,128)(2,1)S(1)} collective-permute-done((bf16[128,1024]{0,1:T(8,128)(2,1)}, bf16[128,1024]{0,1:T(8,128)(2,1)S(1)}, u32[]{:S(2)}, u32[]{:S(2)}) %collective-permute-start.4) | collective-permute-done | bytes 262176 | tf_op jit(solution)/shard_map/ppermute | solution.py:18
  58.4 2.3 %multiply_reduce_fusion.3 = f32[128,8]{0,1:T(8,128)S(1)} fusion(bf16[128,8,128]{0,2,1:T(8,128)(2,1)S(1)} %bitcast.274, bf16[640,1024]{1,0:T(8,128)(2,1)S(1)} %constant_dynamic-update-slice_fusion, f32[8,128,640]{1,2,0:T(8,128)} %get-tuple-element.30, f32[8,128]{1,0:T(8,128)S(1)} %get-tuple-element.29), kind=kOutput, calls=%fused_computation.91 | convolution fusion | flops 169475072 | bytes 3055616 | tf_op jit(solution)/shard_map/hqk,kd->qhd/dot_general | solution.py:64
  63.9 1.2 convolution_bitcast_fusion.2
  65.9 1.6 multiply_reduce_fusion.2
  67.5 1.6 fusion.12
  69.1 1.2 convolution_bitcast_fusion.4
  71.4 1.4 multiply_reduce_fusion
  72.8 1.6 fusion.6
  76.6 1.5 fusion.36
  78.8 1.5 fusion.34
  80.5 2.1 %fusion.32 = f32[32,128]{1,0:T(8,128)S(1)} fusion(f32[128,8,128]{0,2,1:T(8,128)} %convolution_bitcast_fusion, f32[128,8,128]{0,2,1:T(8,128)} %convolution_bitcast_fusion.2, f32[128,8,128]{0,2,1:T(8,128)} %convolution_bitcast_fusion.4, f32[128,8,128]{0,2,1:T(8,128)S(1)} %convolution_bitcast_fusion.6), kind=kLoop, calls=%fused_computation.61 | loop fusion | flops 2093056 | bytes 2113536 | tf_op jit(solution)/shard_map/reduce_sum | solution.py:122
  82.7 18.0 %collective-permute-start.14 = (f32[5120]{0:T(1024)S(1)}, f32[5120]{0:T(1024)S(1)}, u32[]{:S(2)}, u32[]{:S(2)}) collective-permute-start(f32[5120]{0:T(1024)S(1)} %pad_maximum_fusion.6), channel_id=1, source_target_pairs={{0,12},{4,8},{8,4},{12,0},{16,28},{20,24},{24,20},{28,16},{32,44},... | collective-permute-start | bytes 61448 | tf_op jit(solution)/shard_map/ppermute | solution.py:43
  100.7 3.0 %collective-permute-start.13 = (f32[5120]{0:T(1024)S(1)}, f32[5120]{0:T(1024)S(1)}, u32[]{:S(2)}, u32[]{:S(2)}) collective-permute-start(f32[5120]{0:T(1024)S(1)} %pad_maximum_fusion.6), channel_id=1, source_target_pairs={{0,8},{4,12},{8,0},{12,4},{16,24},{20,28},{24,16},{28,20},{32,40},... | collective-permute-start | bytes 61448 | tf_op jit(solution)/shard_map/ppermute | solution.py:43
  103.7 1.9 %collective-permute-start.12 = (f32[5120]{0:T(1024)S(1)}, f32[5120]{0:T(1024)S(1)}, u32[]{:S(2)}, u32[]{:S(2)}) collective-permute-start(f32[5120]{0:T(1024)S(1)} %pad_maximum_fusion.6), channel_id=1, source_target_pairs={{0,4},{4,0},{8,12},{12,8},{16,20},{20,16},{24,28},{28,24},{32,36},... | collective-permute-start | bytes 61448 | tf_op jit(solution)/shard_map/ppermute | solution.py:43
  107.9 4.8 %collective-permute-start.17 = (f32[5120]{0:T(1024)S(1)}, f32[5120]{0:T(1024)S(1)}, u32[]{:S(2)}, u32[]{:S(2)}) collective-permute-start(f32[5120]{0:T(1024)S(1)} %bitcast.255), channel_id=1, source_target_pairs={{0,48},{4,52},{8,56},{12,60},{16,32},{20,36},{24,40},{28,44},{32,1... | collective-permute-start | bytes 61448 | tf_op jit(solution)/shard_map/ppermute | solution.py:43
  112.7 1.9 %collective-permute-start.16 = (f32[5120]{0:T(1024)S(1)}, f32[5120]{0:T(1024)S(1)}, u32[]{:S(2)}, u32[]{:S(2)}) collective-permute-start(f32[5120]{0:T(1024)S(1)} %bitcast.256), channel_id=1, source_target_pairs={{0,32},{4,36},{8,40},{12,44},{16,48},{20,52},{24,56},{28,60},{32,0... | collective-permute-start | bytes 61448 | tf_op jit(solution)/shard_map/ppermute | solution.py:43
  114.7 2.5 %collective-permute-start.15 = (f32[5120]{0:T(1024)S(1)}, f32[5120]{0:T(1024)S(1)}, u32[]{:S(2)}, u32[]{:S(2)}) collective-permute-start(f32[5120]{0:T(1024)S(1)} %bitcast.257), channel_id=1, source_target_pairs={{0,16},{4,20},{8,24},{12,28},{16,0},{20,4},{24,8},{28,12},{32,48},... | collective-permute-start | bytes 61448 | tf_op jit(solution)/shard_map/ppermute | solution.py:43
  120.6 4.0 %collective-permute-start.18 = (f32[5120]{0:T(1024)S(1)}, f32[5120]{0:T(1024)S(1)}, u32[]{:S(2)}, u32[]{:S(2)}) collective-permute-start(f32[5120]{0:T(1024)S(1)} %bitcast.258), channel_id=1, source_target_pairs={{0,64},{4,68},{8,72},{12,76},{16,80},{20,84},{24,88},{28,92},{32,9... | collective-permute-start | bytes 61448 | tf_op jit(solution)/shard_map/ppermute | solution.py:43
  124.5 1.4 fusion.105
  125.9 3.3 %collective-permute-done.18 = f32[5120]{0:T(1024)S(1)} collective-permute-done((f32[5120]{0:T(1024)S(1)}, f32[5120]{0:T(1024)S(1)}, u32[]{:S(2)}, u32[]{:S(2)}) %collective-permute-start.18) | collective-permute-done | bytes 20512 | tf_op jit(solution)/shard_map/ppermute | solution.py:43
  129.9 4.4 %collective-permute-start.21 = (f32[5120]{0:T(1024)S(1)}, f32[5120]{0:T(1024)S(1)}, u32[]{:S(2)}, u32[]{:S(2)}) collective-permute-start(f32[5120]{0:T(1024)S(1)} %bitcast.252), channel_id=1, source_target_pairs={{0,3},{1,2},{2,1},{3,0},{4,7},{5,6},{6,5},{7,4},{8,11},{9,10},{10,... | collective-permute-start | bytes 61448 | tf_op jit(solution)/shard_map/ppermute | solution.py:43
  134.3 2.4 %collective-permute-start.20 = (f32[5120]{0:T(1024)S(1)}, f32[5120]{0:T(1024)S(1)}, u32[]{:S(2)}, u32[]{:S(2)}) collective-permute-start(f32[5120]{0:T(1024)S(1)} %bitcast.253), channel_id=1, source_target_pairs={{0,2},{1,3},{2,0},{3,1},{4,6},{5,7},{6,4},{7,5},{8,10},{9,11},{10,... | collective-permute-start | bytes 61448 | tf_op jit(solution)/shard_map/ppermute | solution.py:43
  136.8 2.2 %collective-permute-start.19 = (f32[5120]{0:T(1024)S(1)}, f32[5120]{0:T(1024)S(1)}, u32[]{:S(2)}, u32[]{:S(2)}) collective-permute-start(f32[5120]{0:T(1024)S(1)} %bitcast.254), channel_id=1, source_target_pairs={{0,1},{1,0},{2,3},{3,2},{4,5},{5,4},{6,7},{7,6},{8,9},{9,8},{10,11... | collective-permute-start | bytes 61448 | tf_op jit(solution)/shard_map/ppermute | solution.py:43
  139.0 2.5 %fusion.33 = bf16[128,32,128]{0,2,1:T(8,128)(2,1)} fusion(f32[128,8,128]{0,2,1:T(8,128)} %convolution_bitcast_fusion, f32[128,8,128]{0,2,1:T(8,128)} %convolution_bitcast_fusion.2, f32[128,8,128]{0,2,1:T(8,128)} %convolution_bitcast_fusion.4, f32[128,8,128]{0,2,1:T(8,128)S(1)} %convolution_bitcast_fusion.6), kind=kLoop, calls=%fused_computation.62 | loop fusion | flops 1572864 | bytes 3145728 | tf_op jit(solution)/shard_map/convert_element_type | solution.py:133
  141.4 2.3 %copy.89 = bf16[1,1,128,4096]{3,2,1,0:T(8,128)(2,1)} copy(bf16[1,1,128,4096]{2,3,1,0:T(8,128)(2,1)} %bitcast.236) | data formatting | bytes 2097152
  143.7 1.3 collective-permute-start.8
  145.0 5.0 %collective-permute-start.11 = (f32[128,1024]{0,1:T(8,128)}, f32[128,1024]{0,1:T(8,128)}, u32[]{:S(2)}, u32[]{:S(2)}) collective-permute-start(f32[128,1024]{0,1:T(8,128)} %get-tuple-element.14), channel_id=1, source_target_pairs={{4,0},{8,4},{12,8},{16,12},{20,16},{24,20},{28,24},{32,28},{36,32}... | collective-permute-start | bytes 1572872 | tf_op jit(solution)/shard_map/ppermute | solution.py:24
  150.0 1.3 collective-permute-start.10
  151.3 1.3 collective-permute-start.9
  154.3 1.9 collective-permute-done.8
  156.2 4.0 %collective-permute-done.11 = f32[128,1024]{0,1:T(8,128)} collective-permute-done((f32[128,1024]{0,1:T(8,128)}, f32[128,1024]{0,1:T(8,128)}, u32[]{:S(2)}, u32[]{:S(2)}) %collective-permute-start.11) | collective-permute-done | bytes 524320 | tf_op jit(solution)/shard_map/ppermute | solution.py:24
  160.1 6.0 %collective-permute-done.10 = f32[128,1024]{0,1:T(8,128)} collective-permute-done((f32[128,1024]{0,1:T(8,128)}, f32[128,1024]{0,1:T(8,128)}, u32[]{:S(2)}, u32[]{:S(2)}) %collective-permute-start.10) | collective-permute-done | bytes 524320 | tf_op jit(solution)/shard_map/ppermute | solution.py:24
  166.2 21.5 %collective-permute-done.9 = f32[128,1024]{0,1:T(8,128)} collective-permute-done((f32[128,1024]{0,1:T(8,128)}, f32[128,1024]{0,1:T(8,128)}, u32[]{:S(2)}, u32[]{:S(2)}) %collective-permute-start.9) | collective-permute-done | bytes 524320 | tf_op jit(solution)/shard_map/ppermute | solution.py:24
  187.6 1.5 fusion.49
  (115 shorter events, 25.1 us)
Async XLA Ops:
  0.6 27.9 %copy-start.7 = (s32[1,4096]{1,0:T(1,128)S(1)}, s32[1,4096]{1,0:T(1,128)}, u32[]{:S(2)}) copy-start(s32[1,4096]{1,0:T(1,128)} %param.11) | copy-start | bytes 49156
  0.6 28.2 %copy-start.2 = (bf16[1,1,128,4096]{3,2,1,0:T(8,128)(2,1)S(1)}, bf16[1,1,128,4096]{3,2,1,0:T(8,128)(2,1)}, u32[]{:S(2)}) copy-start(bf16[1,1,128,4096]{3,2,1,0:T(8,128)(2,1)} %param.7) | copy-start | bytes 3145732
  2.4 38.8 %collective-permute-start.3 = (bf16[128,1024]{1,0:T(8,128)(2,1)}, bf16[128,1024]{1,0:T(8,128)(2,1)}, u32[]{:S(2)}, u32[]{:S(2)}) collective-permute-start(bf16[128,1024]{1,0:T(8,128)(2,1)} %pad_maximum_fusion.1), channel_id=1, source_target_pairs={{0,4},{4,8},{8,12},{12,16},{16,20},{20,24},{24,28},{28,32},{32,36}... | collective-permute-start | bytes 786440 | tf_op jit(solution)/shard_map/ppermute | solution.py:24
  7.8 30.5 %collective-permute-start.2 = (bf16[128,1024]{1,0:T(8,128)(2,1)}, bf16[128,1024]{1,0:T(8,128)(2,1)}, u32[]{:S(2)}, u32[]{:S(2)}) collective-permute-start(bf16[128,1024]{1,0:T(8,128)(2,1)} %pad_maximum_fusion.1), channel_id=1, source_target_pairs={{0,8},{4,12},{8,16},{12,20},{16,24},{20,28},{24,32},{28,36},{32,40... | collective-permute-start | bytes 786440 | tf_op jit(solution)/shard_map/ppermute | solution.py:24
  10.8 24.6 %collective-permute-start.1 = (bf16[128,1024]{1,0:T(8,128)(2,1)}, bf16[128,1024]{1,0:T(8,128)(2,1)}, u32[]{:S(2)}, u32[]{:S(2)}) collective-permute-start(bf16[128,1024]{1,0:T(8,128)(2,1)} %pad_maximum_fusion.1), channel_id=1, source_target_pairs={{0,12},{4,16},{8,20},{12,24},{16,28},{20,32},{24,36},{28,40},{32,4... | collective-permute-start | bytes 786440 | tf_op jit(solution)/shard_map/ppermute | solution.py:24
  13.9 18.3 %collective-permute-start = (bf16[128,1024]{1,0:T(8,128)(2,1)}, bf16[128,1024]{1,0:T(8,128)(2,1)}, u32[]{:S(2)}, u32[]{:S(2)}) collective-permute-start(bf16[128,1024]{1,0:T(8,128)(2,1)} %pad_maximum_fusion.1), channel_id=1, source_target_pairs={{0,16},{4,20},{8,24},{12,28},{16,32},{20,36},{24,40},{28,44},{32,4... | collective-permute-start | bytes 786440 | tf_op jit(solution)/shard_map/ppermute | solution.py:24
  18.6 52.8 %collective-permute-start.7 = (bf16[128,1024]{0,1:T(8,128)(2,1)S(1)}, bf16[128,1024]{0,1:T(8,128)(2,1)}, u32[]{:S(2)}, u32[]{:S(2)}) collective-permute-start(bf16[128,1024]{0,1:T(8,128)(2,1)S(1)} %bitcast.249), channel_id=1, source_target_pairs={{0,384},{128,0},{256,128},{384,256},{1,385},{129,1},{257,129},{385... | collective-permute-start | bytes 786440 | tf_op jit(solution)/shard_map/ppermute | solution.py:18
  28.9 13.3 %copy-start.5 = (bf16[1,1,128,512]{3,2,1,0:T(8,128)(2,1)S(1)}, bf16[1,1,128,512]{3,2,1,0:T(8,128)(2,1)}, u32[]{:S(2)}) copy-start(bf16[1,1,128,512]{3,2,1,0:T(8,128)(2,1)} %param.9) | copy-start | bytes 393220
  28.9 13.3 %copy-start.6 = (bf16[1,1,128,512]{3,2,1,0:T(8,128)(2,1)S(1)}, bf16[1,1,128,512]{3,2,1,0:T(8,128)(2,1)}, u32[]{:S(2)}) copy-start(bf16[1,1,128,512]{3,2,1,0:T(8,128)(2,1)} %param.8) | copy-start | bytes 393220
  29.6 20.5 %copy-start = (bf16[1,1,128,4096]{2,3,1,0:T(8,128)(2,1)}, bf16[1,1,128,4096]{2,3,1,0:T(8,128)(2,1)S(1)}, u32[]{:S(2)}) copy-start(bf16[1,1,128,4096]{2,3,1,0:T(8,128)(2,1)S(1)} %copy.48) | copy-start | bytes 3145732
  32.2 33.4 %collective-permute-start.5 = (bf16[128,1024]{0,1:T(8,128)(2,1)}, bf16[128,1024]{0,1:T(8,128)(2,1)}, u32[]{:S(2)}, u32[]{:S(2)}) collective-permute-start(bf16[128,1024]{0,1:T(8,128)(2,1)} %bitcast.20), channel_id=1, source_target_pairs={{0,384},{128,0},{256,128},{384,256},{1,385},{129,1},{257,129},{385... | collective-permute-start | bytes 786440 | tf_op jit(solution)/shard_map/ppermute | solution.py:18
  35.4 26.7 %collective-permute-start.6 = (bf16[128,1024]{0,1:T(8,128)(2,1)}, bf16[128,1024]{0,1:T(8,128)(2,1)S(1)}, u32[]{:S(2)}, u32[]{:S(2)}) collective-permute-start(bf16[128,1024]{0,1:T(8,128)(2,1)} %bitcast.31), channel_id=1, source_target_pairs={{0,384},{128,0},{256,128},{384,256},{1,385},{129,1},{257,129},{385... | collective-permute-start | bytes 786440 | tf_op jit(solution)/shard_map/ppermute | solution.py:18
  38.3 20.1 %collective-permute-start.4 = (bf16[128,1024]{0,1:T(8,128)(2,1)}, bf16[128,1024]{0,1:T(8,128)(2,1)S(1)}, u32[]{:S(2)}, u32[]{:S(2)}) collective-permute-start(bf16[128,1024]{0,1:T(8,128)(2,1)} %bitcast.250), channel_id=1, source_target_pairs={{0,384},{128,0},{256,128},{384,256},{1,385},{129,1},{257,129},{385... | collective-permute-start | bytes 786440 | tf_op jit(solution)/shard_map/ppermute | solution.py:18
  42.2 21.7 %copy-start.3 = (bf16[640,1024]{1,0:T(8,128)(2,1)}, bf16[640,1024]{1,0:T(8,128)(2,1)S(1)}, u32[]{:S(2)}) copy-start(bf16[640,1024]{1,0:T(8,128)(2,1)S(1)} %constant_dynamic-update-slice_fusion) | copy-start | bytes 3932164
  58.4 2.3 %copy-start.10 = (bf16[128,1024]{0,1:T(8,128)(2,1)}, bf16[128,1024]{0,1:T(8,128)(2,1)S(1)}, u32[]{:S(2)}) copy-start(bf16[128,1024]{0,1:T(8,128)(2,1)S(1)} %collective-permute-done.4) | copy-start | bytes 786436
  58.4 2.6 %copy-start.14 = (f32[8,128,640]{1,2,0:T(8,128)S(1)}, f32[8,128,640]{1,2,0:T(8,128)}, u32[]{:S(2)}) copy-start(f32[8,128,640]{1,2,0:T(8,128)} %get-tuple-element.30) | copy-start | bytes 7864324
  61.1 1.7 copy-start.12
  62.1 1.1 copy-start.8
  63.2 1.9 copy-start.1
  63.9 2.0 %copy-start.15 = (f32[8,128,640]{1,2,0:T(8,128)S(1)}, f32[8,128,640]{1,2,0:T(8,128)}, u32[]{:S(2)}) copy-start(f32[8,128,640]{1,2,0:T(8,128)} %get-tuple-element.28) | copy-start | bytes 7864324
  65.9 1.6 copy-start.4
  69.1 2.3 %copy-start.13 = (f32[8,128,640]{1,2,0:T(8,128)S(1)}, f32[8,128,640]{1,2,0:T(8,128)}, u32[]{:S(2)}) copy-start(f32[8,128,640]{1,2,0:T(8,128)} %get-tuple-element.24) | copy-start | bytes 7864324
  74.3 1.8 copy-start.11
  76.6 1.6 copy-start.9
  82.7 23.0 %collective-permute-start.14 = (f32[5120]{0:T(1024)S(1)}, f32[5120]{0:T(1024)S(1)}, u32[]{:S(2)}, u32[]{:S(2)}) collective-permute-start(f32[5120]{0:T(1024)S(1)} %pad_maximum_fusion.6), channel_id=1, source_target_pairs={{0,12},{4,8},{8,4},{12,0},{16,28},{20,24},{24,20},{28,16},{32,44},... | collective-permute-start | bytes 61448 | tf_op jit(solution)/shard_map/ppermute | solution.py:43
  100.7 5.0 %collective-permute-start.13 = (f32[5120]{0:T(1024)S(1)}, f32[5120]{0:T(1024)S(1)}, u32[]{:S(2)}, u32[]{:S(2)}) collective-permute-start(f32[5120]{0:T(1024)S(1)} %pad_maximum_fusion.6), channel_id=1, source_target_pairs={{0,8},{4,12},{8,0},{12,4},{16,24},{20,28},{24,16},{28,20},{32,40},... | collective-permute-start | bytes 61448 | tf_op jit(solution)/shard_map/ppermute | solution.py:43
  103.7 3.1 %collective-permute-start.12 = (f32[5120]{0:T(1024)S(1)}, f32[5120]{0:T(1024)S(1)}, u32[]{:S(2)}, u32[]{:S(2)}) collective-permute-start(f32[5120]{0:T(1024)S(1)} %pad_maximum_fusion.6), channel_id=1, source_target_pairs={{0,4},{4,0},{8,12},{12,8},{16,20},{20,16},{24,28},{28,24},{32,36},... | collective-permute-start | bytes 61448 | tf_op jit(solution)/shard_map/ppermute | solution.py:43
  107.9 9.3 %collective-permute-start.17 = (f32[5120]{0:T(1024)S(1)}, f32[5120]{0:T(1024)S(1)}, u32[]{:S(2)}, u32[]{:S(2)}) collective-permute-start(f32[5120]{0:T(1024)S(1)} %bitcast.255), channel_id=1, source_target_pairs={{0,48},{4,52},{8,56},{12,60},{16,32},{20,36},{24,40},{28,44},{32,1... | collective-permute-start | bytes 61448 | tf_op jit(solution)/shard_map/ppermute | solution.py:43
  112.7 5.5 %collective-permute-start.16 = (f32[5120]{0:T(1024)S(1)}, f32[5120]{0:T(1024)S(1)}, u32[]{:S(2)}, u32[]{:S(2)}) collective-permute-start(f32[5120]{0:T(1024)S(1)} %bitcast.256), channel_id=1, source_target_pairs={{0,32},{4,36},{8,40},{12,44},{16,48},{20,52},{24,56},{28,60},{32,0... | collective-permute-start | bytes 61448 | tf_op jit(solution)/shard_map/ppermute | solution.py:43
  114.7 4.8 %collective-permute-start.15 = (f32[5120]{0:T(1024)S(1)}, f32[5120]{0:T(1024)S(1)}, u32[]{:S(2)}, u32[]{:S(2)}) collective-permute-start(f32[5120]{0:T(1024)S(1)} %bitcast.257), channel_id=1, source_target_pairs={{0,16},{4,20},{8,24},{12,28},{16,0},{20,4},{24,8},{28,12},{32,48},... | collective-permute-start | bytes 61448 | tf_op jit(solution)/shard_map/ppermute | solution.py:43
  120.6 8.6 %collective-permute-start.18 = (f32[5120]{0:T(1024)S(1)}, f32[5120]{0:T(1024)S(1)}, u32[]{:S(2)}, u32[]{:S(2)}) collective-permute-start(f32[5120]{0:T(1024)S(1)} %bitcast.258), channel_id=1, source_target_pairs={{0,64},{4,68},{8,72},{12,76},{16,80},{20,84},{24,88},{28,92},{32,9... | collective-permute-start | bytes 61448 | tf_op jit(solution)/shard_map/ppermute | solution.py:43
  129.9 20.1 %collective-permute-start.21 = (f32[5120]{0:T(1024)S(1)}, f32[5120]{0:T(1024)S(1)}, u32[]{:S(2)}, u32[]{:S(2)}) collective-permute-start(f32[5120]{0:T(1024)S(1)} %bitcast.252), channel_id=1, source_target_pairs={{0,3},{1,2},{2,1},{3,0},{4,7},{5,6},{6,5},{7,4},{8,11},{9,10},{10,... | collective-permute-start | bytes 61448 | tf_op jit(solution)/shard_map/ppermute | solution.py:43
  134.3 17.0 %collective-permute-start.20 = (f32[5120]{0:T(1024)S(1)}, f32[5120]{0:T(1024)S(1)}, u32[]{:S(2)}, u32[]{:S(2)}) collective-permute-start(f32[5120]{0:T(1024)S(1)} %bitcast.253), channel_id=1, source_target_pairs={{0,2},{1,3},{2,0},{3,1},{4,6},{5,7},{6,4},{7,5},{8,10},{9,11},{10,... | collective-permute-start | bytes 61448 | tf_op jit(solution)/shard_map/ppermute | solution.py:43
  136.8 15.8 %collective-permute-start.19 = (f32[5120]{0:T(1024)S(1)}, f32[5120]{0:T(1024)S(1)}, u32[]{:S(2)}, u32[]{:S(2)}) collective-permute-start(f32[5120]{0:T(1024)S(1)} %bitcast.254), channel_id=1, source_target_pairs={{0,1},{1,0},{2,3},{3,2},{4,5},{5,4},{6,7},{7,6},{8,9},{9,8},{10,11... | collective-permute-start | bytes 61448 | tf_op jit(solution)/shard_map/ppermute | solution.py:43
  143.7 12.5 %collective-permute-start.8 = (f32[128,1024]{0,1:T(8,128)}, f32[128,1024]{0,1:T(8,128)S(1)}, u32[]{:S(2)}, u32[]{:S(2)}) collective-permute-start(f32[128,1024]{0,1:T(8,128)} %get-tuple-element.13), channel_id=1, source_target_pairs={{16,0},{20,4},{24,8},{28,12},{32,16},{36,20},{40,24},{44,28},{48,3... | collective-permute-start | bytes 1572872 | tf_op jit(solution)/shard_map/ppermute | solution.py:24
  145.0 15.1 %collective-permute-start.11 = (f32[128,1024]{0,1:T(8,128)}, f32[128,1024]{0,1:T(8,128)}, u32[]{:S(2)}, u32[]{:S(2)}) collective-permute-start(f32[128,1024]{0,1:T(8,128)} %get-tuple-element.14), channel_id=1, source_target_pairs={{4,0},{8,4},{12,8},{16,12},{20,16},{24,20},{28,24},{32,28},{36,32}... | collective-permute-start | bytes 1572872 | tf_op jit(solution)/shard_map/ppermute | solution.py:24
  150.0 16.2 %collective-permute-start.10 = (f32[128,1024]{0,1:T(8,128)}, f32[128,1024]{0,1:T(8,128)}, u32[]{:S(2)}, u32[]{:S(2)}) collective-permute-start(f32[128,1024]{0,1:T(8,128)} %get-tuple-element.15), channel_id=1, source_target_pairs={{8,0},{12,4},{16,8},{20,12},{24,16},{28,20},{32,24},{36,28},{40,32... | collective-permute-start | bytes 1572872 | tf_op jit(solution)/shard_map/ppermute | solution.py:24
  151.3 36.3 %collective-permute-start.9 = (f32[128,1024]{0,1:T(8,128)}, f32[128,1024]{0,1:T(8,128)}, u32[]{:S(2)}, u32[]{:S(2)}) collective-permute-start(f32[128,1024]{0,1:T(8,128)} %get-tuple-element.16), channel_id=1, source_target_pairs={{12,0},{16,4},{20,8},{24,12},{28,16},{32,20},{36,24},{40,28},{44,3... | collective-permute-start | bytes 1572872 | tf_op jit(solution)/shard_map/ppermute | solution.py:24

commit v4 on v3

--- a/solution.py
+++ b/solution.py
@@ -4,6 +4,7 @@
 import jax.numpy as jnp
 from jax import lax
 from jax.sharding import PartitionSpec as P
+
 
 ASKER_STREAMS = 32
 SHARED_GROUPS = 4
@@ -71,7 +72,7 @@
     return asker, lookup, content
 
 
-def body(queries, key_input, value_input, incoming, segments):
+def body_inner(queries, key_input, value_input, incoming, segments):
     shard_length = queries.shape[2]
     ctx_size = lax.axis_size("ctx")
     reach = min(-(-(DOC_MOST - 1) // shard_length), ctx_size - 1)
@@ -120,15 +121,15 @@
     grad_window = jnp.concatenate(lookups + contents, axis=1)
 
     offset_parts = jnp.concatenate([jnp.sum(query_flat, axis=0), jnp.sum(grad_window, axis=0)])
-    offset_overall = group_sum(group_sum(offset_parts, "ctx"), "dp")
-    bias_scaled = offset_overall / math.sqrt(lax.axis_size("dp") * shard_length * ctx_size)
 
     grad_own = grad_window[reach * shard_length :]
     for block in range(reach):
         steps = reach - block
-        grad_own = grad_own + shifted(
-            grad_window[block * shard_length : (block + 1) * shard_length], "ctx", -steps
-        )
+        part = grad_window[block * shard_length : (block + 1) * shard_length]
+        grad_own = grad_own + shifted(part.astype(jnp.bfloat16), "ctx", -steps).astype(jnp.float32)
+
+    offset_overall = group_sum(group_sum(offset_parts, "ctx"), "dp")
+    bias_scaled = offset_overall / math.sqrt(lax.axis_size("dp") * shard_length * ctx_size)
 
     query_grad = query_flat.astype(jnp.bfloat16)[None, None]
     key_grad = grad_own[:, :width].astype(jnp.bfloat16)[None, None]
@@ -138,7 +139,7 @@
 
 def solution(mesh):
     return jax.shard_map(
-        body,
+        body_inner,
         mesh=mesh,
         in_specs=(
             P("pipe", "dp", "ctx", None),

time: 192 us -> 177 us (0.922)
  waiting for transfers between devices: 45.7 us -> 27.7 us
    ppermute x8, waiting for transfers between devices: 33.3 us -> 14.3 us  [shifted(): return lax.ppermute(value, axis, pairs)]
    convert_element_type x1, other arithmetic: 2.48 us -> 0.16 us  [body_inner(): query_grad = query_flat.astype(jnp.bfloat16)[None, None]]
    unnamed x44 -> x40, local copies, waits for them, and re-layouts: 12.4 us -> 12.2 us
  transfers between devices with their start and end apart: 22 -> 22, of which waited for: 9 -> 8; matrix products, arithmetic and copies ran while one was open for 20% -> 20% of each run, Pallas kernels for 0% -> 0%
where the time goes in v4:
time: 177 us; the launch traced here: 175 us
  starting transfers between devices  84.5 us (48%)
  matrix products  32.2 us (18%)
  waiting for transfers between devices  27.7 us (16%)
  local copies, waits for them, and re-layouts  20.2 us (11%)
  other arithmetic  9.2 us (5%)
    ppermute x10, starting transfers between devices, group_sum(): lax.ppermute(value, axis, [(i, i ^ t * stride) for i in range(count)])  45.3 us
    ppermute x8, starting transfers between devices, shifted(): return lax.ppermute(value, axis, pairs)  23.5 us
    ppermute x4, starting transfers between devices, passed_along(): return lax.ppermute(value, axis, pairs)  15.8 us
    ppermute x8, waiting for transfers between devices, shifted(): return lax.ppermute(value, axis, pairs)  14.3 us
    unnamed x40, local copies, waits for them, and re-layouts  12.2 us
    sub x4, matrix products, attend_group(): weights = jnp.where(visible[None], jnp.exp(scores - row_max), 0.0)  10.5 us
    ppermute x10, waiting for transfers between devices, group_sum(): lax.ppermute(value, axis, [(i, i ^ t * stride) for i in range(count)])  6.92 us
    ppermute x4, waiting for transfers between devices, passed_along(): return lax.ppermute(value, axis, pairs)  6.54 us
  transfers between devices with their start and end apart: 22, of which 8 were waited for; matrix products, arithmetic and copies ran while one was open for 20% of the time, Pallas kernels for 0%

profile of v4, /device:TPU:1, one launch (start us, length us, event | category | flops | bytes accessed | tf_op | source)
XLA Modules:
  0.0 175.5 jit_solution(7073183746186820065)
XLA Ops:
  0.7 1.8 %pad_maximum_fusion.1 = bf16[128,1024]{1,0:T(8,128)(2,1)} fusion(bf16[128,512]{1,0:T(8,128)(2,1)} %bitcast.245, bf16[128,512]{1,0:T(8,128)(2,1)} %bitcast.247), kind=kLoop, calls=%fused_computation.98 | loop fusion | flops 524288 | bytes 524288 | tf_op jit(solution)/shard_map/concatenate | solution.py:90
  2.4 5.4 %collective-permute-start.3 = (bf16[128,1024]{1,0:T(8,128)(2,1)}, bf16[128,1024]{1,0:T(8,128)(2,1)}, u32[]{:S(2)}, u32[]{:S(2)}) collective-permute-start(bf16[128,1024]{1,0:T(8,128)(2,1)} %pad_maximum_fusion.1), channel_id=1, source_target_pairs={{0,4},{4,8},{8,12},{12,16},{16,20},{20,24},{24,28},{28,32},{32,36}... | collective-permute-start | bytes 786440 | tf_op jit(solution)/shard_map/ppermute | solution.py:25
  7.8 3.0 %collective-permute-start.2 = (bf16[128,1024]{1,0:T(8,128)(2,1)}, bf16[128,1024]{1,0:T(8,128)(2,1)}, u32[]{:S(2)}, u32[]{:S(2)}) collective-permute-start(bf16[128,1024]{1,0:T(8,128)(2,1)} %pad_maximum_fusion.1), channel_id=1, source_target_pairs={{0,8},{4,12},{8,16},{12,20},{16,24},{20,28},{24,32},{28,36},{32,40... | collective-permute-start | bytes 786440 | tf_op jit(solution)/shard_map/ppermute | solution.py:25
  10.8 3.1 %collective-permute-start.1 = (bf16[128,1024]{1,0:T(8,128)(2,1)}, bf16[128,1024]{1,0:T(8,128)(2,1)}, u32[]{:S(2)}, u32[]{:S(2)}) collective-permute-start(bf16[128,1024]{1,0:T(8,128)(2,1)} %pad_maximum_fusion.1), channel_id=1, source_target_pairs={{0,12},{4,16},{8,20},{12,24},{16,28},{20,32},{24,36},{28,40},{32,4... | collective-permute-start | bytes 786440 | tf_op jit(solution)/shard_map/ppermute | solution.py:25
  13.9 3.2 %collective-permute-start = (bf16[128,1024]{1,0:T(8,128)(2,1)}, bf16[128,1024]{1,0:T(8,128)(2,1)}, u32[]{:S(2)}, u32[]{:S(2)}) collective-permute-start(bf16[128,1024]{1,0:T(8,128)(2,1)} %pad_maximum_fusion.1), channel_id=1, source_target_pairs={{0,16},{4,20},{8,24},{12,28},{16,32},{20,36},{24,40},{28,44},{32,4... | collective-permute-start | bytes 786440 | tf_op jit(solution)/shard_map/ppermute | solution.py:25
  17.1 1.3 fusion.107
  18.6 9.8 %collective-permute-start.7 = (bf16[128,1024]{0,1:T(8,128)(2,1)S(1)}, bf16[128,1024]{0,1:T(8,128)(2,1)}, u32[]{:S(2)}, u32[]{:S(2)}) collective-permute-start(bf16[128,1024]{0,1:T(8,128)(2,1)S(1)} %bitcast.249), channel_id=1, source_target_pairs={{0,384},{128,0},{256,128},{384,256},{1,385},{129,1},{257,129},{385... | collective-permute-start | bytes 786440 | tf_op jit(solution)/shard_map/ppermute | solution.py:19
  31.5 2.2 %collective-permute-start.5 = (bf16[128,1024]{0,1:T(8,128)(2,1)}, bf16[128,1024]{0,1:T(8,128)(2,1)}, u32[]{:S(2)}, u32[]{:S(2)}) collective-permute-start(bf16[128,1024]{0,1:T(8,128)(2,1)} %bitcast.20), channel_id=1, source_target_pairs={{0,384},{128,0},{256,128},{384,256},{1,385},{129,1},{257,129},{385... | collective-permute-start | bytes 786440 | tf_op jit(solution)/shard_map/ppermute | solution.py:19
  34.6 1.9 %collective-permute-start.6 = (bf16[128,1024]{0,1:T(8,128)(2,1)}, bf16[128,1024]{0,1:T(8,128)(2,1)}, u32[]{:S(2)}, u32[]{:S(2)}) collective-permute-start(bf16[128,1024]{0,1:T(8,128)(2,1)} %bitcast.31), channel_id=1, source_target_pairs={{0,384},{128,0},{256,128},{384,256},{1,385},{129,1},{257,129},{385... | collective-permute-start | bytes 786440 | tf_op jit(solution)/shard_map/ppermute | solution.py:19
  37.5 1.9 %collective-permute-start.4 = (bf16[128,1024]{0,1:T(8,128)(2,1)S(1)}, bf16[128,1024]{0,1:T(8,128)(2,1)S(1)}, u32[]{:S(2)}, u32[]{:S(2)}) collective-permute-start(bf16[128,1024]{0,1:T(8,128)(2,1)S(1)} %bitcast.250), channel_id=1, source_target_pairs={{0,384},{128,0},{256,128},{384,256},{1,385},{129,1},{257,129},{385... | collective-permute-start | bytes 786440 | tf_op jit(solution)/shard_map/ppermute | solution.py:19
  41.5 2.6 %fusion.108 = (f32[8,128]{1,0:T(8,128)S(1)}, f32[8,128,640]{1,2,0:T(8,128)}) fusion(pred[128,640]{0,1:T(8,128)(4,1)S(1)} %fusion.50, bf16[128,32,128]{0,2,1:T(8,128)(2,1)S(1)} %bitcast.237, bf16[640,1024]{1,0:T(8,128)(2,1)S(1)} %constant_dynamic-update-slice_fusion), kind=kOutput, calls=%fused_computation.172 | convolution fusion | flops 171049600 | bytes 3215360 | tf_op jit(solution)/shard_map/sub | solution.py:62
  44.1 2.6 %fusion.114 = (f32[8,128]{1,0:T(8,128)S(1)}, f32[8,128,640]{1,2,0:T(8,128)}) fusion(pred[128,640]{0,1:T(8,128)(4,1)S(1)} %fusion.50, bf16[128,32,128]{0,2,1:T(8,128)(2,1)S(1)} %bitcast.238, bf16[640,1024]{1,0:T(8,128)(2,1)S(1)} %constant_dynamic-update-slice_fusion), kind=kOutput, calls=%fused_computation.174 | convolution fusion | flops 171049600 | bytes 3215360 | tf_op jit(solution)/shard_map/sub | solution.py:62
  46.7 2.6 %fusion.111 = (f32[8,128]{1,0:T(8,128)S(1)}, f32[8,128,640]{1,2,0:T(8,128)}) fusion(pred[128,640]{0,1:T(8,128)(4,1)S(1)} %fusion.50, bf16[128,32,128]{0,2,1:T(8,128)(2,1)S(1)} %bitcast.239, bf16[640,1024]{1,0:T(8,128)(2,1)S(1)} %constant_dynamic-update-slice_fusion), kind=kOutput, calls=%fused_computation.173 | convolution fusion | flops 171049600 | bytes 3215360 | tf_op jit(solution)/shard_map/sub | solution.py:62
  49.3 2.6 %fusion.117 = (f32[8,128]{1,0:T(8,128)S(1)}, f32[8,128,640]{1,2,0:T(8,128)}) fusion(pred[128,640]{0,1:T(8,128)(4,1)S(1)} %fusion.50, bf16[128,32,128]{0,2,1:T(8,128)(2,1)S(1)} %bitcast.240, bf16[640,1024]{1,0:T(8,128)(2,1)S(1)} %constant_dynamic-update-slice_fusion), kind=kOutput, calls=%fused_computation.175 | convolution fusion | flops 171049600 | bytes 3215360 | tf_op jit(solution)/shard_map/sub | solution.py:62
  51.9 6.5 %collective-permute-done.4 = bf16[128,1024]{0,1:T(8,128)(2,1)S(1)} collective-permute-done((bf16[128,1024]{0,1:T(8,128)(2,1)S(1)}, bf16[128,1024]{0,1:T(8,128)(2,1)S(1)}, u32[]{:S(2)}, u32[]{:S(2)}) %collective-permute-start.4) | collective-permute-done | bytes 262176 | tf_op jit(solution)/shard_map/ppermute | solution.py:19
  58.5 2.3 %multiply_reduce_fusion.3 = f32[128,8]{0,1:T(8,128)S(1)} fusion(bf16[128,8,128]{0,2,1:T(8,128)(2,1)S(1)} %bitcast.271, bf16[640,1024]{1,0:T(8,128)(2,1)S(1)} %constant_dynamic-update-slice_fusion, f32[8,128,640]{1,2,0:T(8,128)} %get-tuple-element.26, f32[8,128]{1,0:T(8,128)S(1)} %get-tuple-element.25), kind=kOutput, calls=%fused_computation.91 | convolution fusion | flops 169475072 | bytes 3055616 | tf_op jit(solution)/shard_map/hqk,kd->qhd/dot_general | solution.py:65
  62.8 1.4 multiply_reduce_fusion.1
  64.2 1.7 fusion.9
  66.0 1.4 convolution_bitcast_fusion.2
  68.0 1.4 multiply_reduce_fusion.2
  69.4 1.6 fusion.12
  72.7 1.4 multiply_reduce_fusion
  74.1 1.6 fusion.6
  77.2 1.5 fusion.36
  78.7 1.5 fusion.35
  80.2 1.5 fusion.34
  81.7 1.5 copy-done
  84.3 17.3 %collective-permute-start.14 = (f32[5120]{0:T(1024)S(1)}, f32[5120]{0:T(1024)S(1)}, u32[]{:S(2)}, u32[]{:S(2)}) collective-permute-start(f32[5120]{0:T(1024)S(1)} %pad_maximum_fusion.6), channel_id=1, source_target_pairs={{0,12},{4,8},{8,4},{12,0},{16,28},{20,24},{24,20},{28,16},{32,44},... | collective-permute-start | bytes 61448 | tf_op jit(solution)/shard_map/ppermute | solution.py:44
  101.6 3.7 %collective-permute-start.13 = (f32[5120]{0:T(1024)S(1)}, f32[5120]{0:T(1024)S(1)}, u32[]{:S(2)}, u32[]{:S(2)}) collective-permute-start(f32[5120]{0:T(1024)S(1)} %pad_maximum_fusion.6), channel_id=1, source_target_pairs={{0,8},{4,12},{8,0},{12,4},{16,24},{20,28},{24,16},{28,20},{32,40},... | collective-permute-start | bytes 61448 | tf_op jit(solution)/shard_map/ppermute | solution.py:44
  105.2 1.9 %collective-permute-start.12 = (f32[5120]{0:T(1024)S(1)}, f32[5120]{0:T(1024)S(1)}, u32[]{:S(2)}, u32[]{:S(2)}) collective-permute-start(f32[5120]{0:T(1024)S(1)} %pad_maximum_fusion.6), channel_id=1, source_target_pairs={{0,4},{4,0},{8,12},{12,8},{16,20},{20,16},{24,28},{28,24},{32,36},... | collective-permute-start | bytes 61448 | tf_op jit(solution)/shard_map/ppermute | solution.py:44
  108.4 1.2 gather_fusion.1
  112.3 4.8 %collective-permute-start.17 = (f32[5120]{0:T(1024)S(1)}, f32[5120]{0:T(1024)S(1)}, u32[]{:S(2)}, u32[]{:S(2)}) collective-permute-start(f32[5120]{0:T(1024)S(1)} %bitcast.255), channel_id=1, source_target_pairs={{0,48},{4,52},{8,56},{12,60},{16,32},{20,36},{24,40},{28,44},{32,1... | collective-permute-start | bytes 61448 | tf_op jit(solution)/shard_map/ppermute | solution.py:44
  117.1 1.9 %collective-permute-start.16 = (f32[5120]{0:T(1024)S(1)}, f32[5120]{0:T(1024)S(1)}, u32[]{:S(2)}, u32[]{:S(2)}) collective-permute-start(f32[5120]{0:T(1024)S(1)} %bitcast.256), channel_id=1, source_target_pairs={{0,32},{4,36},{8,40},{12,44},{16,48},{20,52},{24,56},{28,60},{32,0... | collective-permute-start | bytes 61448 | tf_op jit(solution)/shard_map/ppermute | solution.py:44
  119.0 2.5 %collective-permute-start.15 = (f32[5120]{0:T(1024)S(1)}, f32[5120]{0:T(1024)S(1)}, u32[]{:S(2)}, u32[]{:S(2)}) collective-permute-start(f32[5120]{0:T(1024)S(1)} %bitcast.257), channel_id=1, source_target_pairs={{0,16},{4,20},{8,24},{12,28},{16,0},{20,4},{24,8},{28,12},{32,48},... | collective-permute-start | bytes 61448 | tf_op jit(solution)/shard_map/ppermute | solution.py:44
  122.7 1.2 collective-permute-done.15
  123.9 1.2 gather_fusion.2
  127.8 4.0 %collective-permute-start.18 = (f32[5120]{0:T(1024)S(1)}, f32[5120]{0:T(1024)S(1)}, u32[]{:S(2)}, u32[]{:S(2)}) collective-permute-start(f32[5120]{0:T(1024)S(1)} %bitcast.258), channel_id=1, source_target_pairs={{0,64},{4,68},{8,72},{12,76},{16,80},{20,84},{24,88},{28,92},{32,9... | collective-permute-start | bytes 61448 | tf_op jit(solution)/shard_map/ppermute | solution.py:44
  133.0 3.5 %collective-permute-done.18 = f32[5120]{0:T(1024)S(1)} collective-permute-done((f32[5120]{0:T(1024)S(1)}, f32[5120]{0:T(1024)S(1)}, u32[]{:S(2)}, u32[]{:S(2)}) %collective-permute-start.18) | collective-permute-done | bytes 20512 | tf_op jit(solution)/shard_map/ppermute | solution.py:44
  137.2 4.5 %collective-permute-start.21 = (f32[5120]{0:T(1024)S(1)}, f32[5120]{0:T(1024)S(1)}, u32[]{:S(2)}, u32[]{:S(2)}) collective-permute-start(f32[5120]{0:T(1024)S(1)} %bitcast.252), channel_id=1, source_target_pairs={{0,3},{1,2},{2,1},{3,0},{4,7},{5,6},{6,5},{7,4},{8,11},{9,10},{10,... | collective-permute-start | bytes 61448 | tf_op jit(solution)/shard_map/ppermute | solution.py:44
  141.7 2.4 %collective-permute-start.20 = (f32[5120]{0:T(1024)S(1)}, f32[5120]{0:T(1024)S(1)}, u32[]{:S(2)}, u32[]{:S(2)}) collective-permute-start(f32[5120]{0:T(1024)S(1)} %bitcast.253), channel_id=1, source_target_pairs={{0,2},{1,3},{2,0},{3,1},{4,6},{5,7},{6,4},{7,5},{8,10},{9,11},{10,... | collective-permute-start | bytes 61448 | tf_op jit(solution)/shard_map/ppermute | solution.py:44
  144.2 2.2 %collective-permute-start.19 = (f32[5120]{0:T(1024)S(1)}, f32[5120]{0:T(1024)S(1)}, u32[]{:S(2)}, u32[]{:S(2)}) collective-permute-start(f32[5120]{0:T(1024)S(1)} %bitcast.254), channel_id=1, source_target_pairs={{0,1},{1,0},{2,3},{3,2},{4,5},{5,4},{6,7},{7,6},{8,9},{9,8},{10,11... | collective-permute-start | bytes 61448 | tf_op jit(solution)/shard_map/ppermute | solution.py:44
  146.5 1.3 copy.89
  147.8 1.3 collective-permute-start.8
  149.1 5.0 %collective-permute-start.11 = (bf16[128,1024]{0,1:T(8,128)(2,1)}, bf16[128,1024]{0,1:T(8,128)(2,1)S(1)}, u32[]{:S(2)}, u32[]{:S(2)}) collective-permute-start(bf16[128,1024]{0,1:T(8,128)(2,1)} %get-tuple-element.16), channel_id=1, source_target_pairs={{4,0},{8,4},{12,8},{16,12},{20,16},{24,20},{28,24},{32,28},{36,32}... | collective-permute-start | bytes 786440 | tf_op jit(solution)/shard_map/ppermute | solution.py:25
  154.1 1.3 collective-permute-start.10
  155.4 1.3 collective-permute-start.9
  158.8 5.5 %collective-permute-done.10 = bf16[128,1024]{0,1:T(8,128)(2,1)S(1)} collective-permute-done((bf16[128,1024]{0,1:T(8,128)(2,1)}, bf16[128,1024]{0,1:T(8,128)(2,1)S(1)}, u32[]{:S(2)}, u32[]{:S(2)}) %collective-permute-start.10) | collective-permute-done | bytes 262176 | tf_op jit(solution)/shard_map/ppermute | solution.py:25
  164.2 8.5 %collective-permute-done.9 = bf16[128,1024]{0,1:T(8,128)(2,1)S(1)} collective-permute-done((bf16[128,1024]{0,1:T(8,128)(2,1)S(1)}, bf16[128,1024]{0,1:T(8,128)(2,1)S(1)}, u32[]{:S(2)}, u32[]{:S(2)}) %collective-permute-start.9) | collective-permute-done | bytes 262176 | tf_op jit(solution)/shard_map/ppermute | solution.py:25
  (111 shorter events, 28.2 us)
Async XLA Ops:
  0.6 27.9 %copy-start.7 = (s32[1,4096]{1,0:T(1,128)S(1)}, s32[1,4096]{1,0:T(1,128)}, u32[]{:S(2)}) copy-start(s32[1,4096]{1,0:T(1,128)} %param.11) | copy-start | bytes 49156
  0.6 28.2 %copy-start.1 = (bf16[1,1,128,4096]{3,2,1,0:T(8,128)(2,1)S(1)}, bf16[1,1,128,4096]{3,2,1,0:T(8,128)(2,1)}, u32[]{:S(2)}) copy-start(bf16[1,1,128,4096]{3,2,1,0:T(8,128)(2,1)} %param.7) | copy-start | bytes 3145732
  2.4 38.0 %collective-permute-start.3 = (bf16[128,1024]{1,0:T(8,128)(2,1)}, bf16[128,1024]{1,0:T(8,128)(2,1)}, u32[]{:S(2)}, u32[]{:S(2)}) collective-permute-start(bf16[128,1024]{1,0:T(8,128)(2,1)} %pad_maximum_fusion.1), channel_id=1, source_target_pairs={{0,4},{4,8},{8,12},{12,16},{16,20},{20,24},{24,28},{28,32},{32,36}... | collective-permute-start | bytes 786440 | tf_op jit(solution)/shard_map/ppermute | solution.py:25
  7.8 29.7 %collective-permute-start.2 = (bf16[128,1024]{1,0:T(8,128)(2,1)}, bf16[128,1024]{1,0:T(8,128)(2,1)}, u32[]{:S(2)}, u32[]{:S(2)}) collective-permute-start(bf16[128,1024]{1,0:T(8,128)(2,1)} %pad_maximum_fusion.1), channel_id=1, source_target_pairs={{0,8},{4,12},{8,16},{12,20},{16,24},{20,28},{24,32},{28,36},{32,40... | collective-permute-start | bytes 786440 | tf_op jit(solution)/shard_map/ppermute | solution.py:25
  10.8 23.8 %collective-permute-start.1 = (bf16[128,1024]{1,0:T(8,128)(2,1)}, bf16[128,1024]{1,0:T(8,128)(2,1)}, u32[]{:S(2)}, u32[]{:S(2)}) collective-permute-start(bf16[128,1024]{1,0:T(8,128)(2,1)} %pad_maximum_fusion.1), channel_id=1, source_target_pairs={{0,12},{4,16},{8,20},{12,24},{16,28},{20,32},{24,36},{28,40},{32,4... | collective-permute-start | bytes 786440 | tf_op jit(solution)/shard_map/ppermute | solution.py:25
  13.9 17.5 %collective-permute-start = (bf16[128,1024]{1,0:T(8,128)(2,1)}, bf16[128,1024]{1,0:T(8,128)(2,1)}, u32[]{:S(2)}, u32[]{:S(2)}) collective-permute-start(bf16[128,1024]{1,0:T(8,128)(2,1)} %pad_maximum_fusion.1), channel_id=1, source_target_pairs={{0,16},{4,20},{8,24},{12,28},{16,32},{20,36},{24,40},{28,44},{32,4... | collective-permute-start | bytes 786440 | tf_op jit(solution)/shard_map/ppermute | solution.py:25
  18.6 53.9 %collective-permute-start.7 = (bf16[128,1024]{0,1:T(8,128)(2,1)S(1)}, bf16[128,1024]{0,1:T(8,128)(2,1)}, u32[]{:S(2)}, u32[]{:S(2)}) collective-permute-start(bf16[128,1024]{0,1:T(8,128)(2,1)S(1)} %bitcast.249), channel_id=1, source_target_pairs={{0,384},{128,0},{256,128},{384,256},{1,385},{129,1},{257,129},{385... | collective-permute-start | bytes 786440 | tf_op jit(solution)/shard_map/ppermute | solution.py:19
  28.9 12.5 %copy-start.4 = (bf16[1,1,128,512]{3,2,1,0:T(8,128)(2,1)S(1)}, bf16[1,1,128,512]{3,2,1,0:T(8,128)(2,1)}, u32[]{:S(2)}) copy-start(bf16[1,1,128,512]{3,2,1,0:T(8,128)(2,1)} %param.9) | copy-start | bytes 393220
  28.9 12.5 %copy-start.5 = (bf16[1,1,128,512]{3,2,1,0:T(8,128)(2,1)S(1)}, bf16[1,1,128,512]{3,2,1,0:T(8,128)(2,1)}, u32[]{:S(2)}) copy-start(bf16[1,1,128,512]{3,2,1,0:T(8,128)(2,1)} %param.8) | copy-start | bytes 393220
  31.5 36.5 %collective-permute-start.5 = (bf16[128,1024]{0,1:T(8,128)(2,1)}, bf16[128,1024]{0,1:T(8,128)(2,1)}, u32[]{:S(2)}, u32[]{:S(2)}) collective-permute-start(bf16[128,1024]{0,1:T(8,128)(2,1)} %bitcast.20), channel_id=1, source_target_pairs={{0,384},{128,0},{256,128},{384,256},{1,385},{129,1},{257,129},{385... | collective-permute-start | bytes 786440 | tf_op jit(solution)/shard_map/ppermute | solution.py:19
  34.6 27.5 %collective-permute-start.6 = (bf16[128,1024]{0,1:T(8,128)(2,1)}, bf16[128,1024]{0,1:T(8,128)(2,1)}, u32[]{:S(2)}, u32[]{:S(2)}) collective-permute-start(bf16[128,1024]{0,1:T(8,128)(2,1)} %bitcast.31), channel_id=1, source_target_pairs={{0,384},{128,0},{256,128},{384,256},{1,385},{129,1},{257,129},{385... | collective-permute-start | bytes 786440 | tf_op jit(solution)/shard_map/ppermute | solution.py:19
  37.5 20.9 %collective-permute-start.4 = (bf16[128,1024]{0,1:T(8,128)(2,1)S(1)}, bf16[128,1024]{0,1:T(8,128)(2,1)S(1)}, u32[]{:S(2)}, u32[]{:S(2)}) collective-permute-start(bf16[128,1024]{0,1:T(8,128)(2,1)S(1)} %bitcast.250), channel_id=1, source_target_pairs={{0,384},{128,0},{256,128},{384,256},{1,385},{129,1},{257,129},{385... | collective-permute-start | bytes 786440 | tf_op jit(solution)/shard_map/ppermute | solution.py:19
  41.4 22.8 %copy-start.2 = (bf16[640,1024]{1,0:T(8,128)(2,1)}, bf16[640,1024]{1,0:T(8,128)(2,1)S(1)}, u32[]{:S(2)}) copy-start(bf16[640,1024]{1,0:T(8,128)(2,1)S(1)} %constant_dynamic-update-slice_fusion) | copy-start | bytes 3932164
  58.4 2.3 %copy-start.8 = (bf16[128,1024]{0,1:T(8,128)(2,1)}, bf16[128,1024]{0,1:T(8,128)(2,1)S(1)}, u32[]{:S(2)}) copy-start(bf16[128,1024]{0,1:T(8,128)(2,1)S(1)} %collective-permute-done.4) | copy-start | bytes 786436
  58.4 2.6 %copy-start.12 = (f32[8,128,640]{1,2,0:T(8,128)S(1)}, f32[8,128,640]{1,2,0:T(8,128)}, u32[]{:S(2)}) copy-start(f32[8,128,640]{1,2,0:T(8,128)} %get-tuple-element.26) | copy-start | bytes 7864324
  61.1 1.7 copy-start.10
  64.2 3.7 %copy-start.13 = (f32[8,128,640]{1,2,0:T(8,128)S(1)}, f32[8,128,640]{1,2,0:T(8,128)}, u32[]{:S(2)}) copy-start(f32[8,128,640]{1,2,0:T(8,128)} %get-tuple-element.28) | copy-start | bytes 7864324
  66.0 2.0 %copy-start.3 = (bf16[640,1024]{1,0:T(8,128)(2,1)S(1)}, bf16[640,1024]{1,0:T(8,128)(2,1)}, u32[]{:S(2)}) copy-start(bf16[640,1024]{1,0:T(8,128)(2,1)} %copy-done.2) | copy-start | bytes 3932164
  70.9 1.7 copy-start.11
  75.6 1.0 copy-start.9
  81.7 1.5 copy-start
  84.3 22.9 %collective-permute-start.14 = (f32[5120]{0:T(1024)S(1)}, f32[5120]{0:T(1024)S(1)}, u32[]{:S(2)}, u32[]{:S(2)}) collective-permute-start(f32[5120]{0:T(1024)S(1)} %pad_maximum_fusion.6), channel_id=1, source_target_pairs={{0,12},{4,8},{8,4},{12,0},{16,28},{20,24},{24,20},{28,16},{32,44},... | collective-permute-start | bytes 61448 | tf_op jit(solution)/shard_map/ppermute | solution.py:44
  101.6 5.6 %collective-permute-start.13 = (f32[5120]{0:T(1024)S(1)}, f32[5120]{0:T(1024)S(1)}, u32[]{:S(2)}, u32[]{:S(2)}) collective-permute-start(f32[5120]{0:T(1024)S(1)} %pad_maximum_fusion.6), channel_id=1, source_target_pairs={{0,8},{4,12},{8,0},{12,4},{16,24},{20,28},{24,16},{28,20},{32,40},... | collective-permute-start | bytes 61448 | tf_op jit(solution)/shard_map/ppermute | solution.py:44
  105.2 3.1 %collective-permute-start.12 = (f32[5120]{0:T(1024)S(1)}, f32[5120]{0:T(1024)S(1)}, u32[]{:S(2)}, u32[]{:S(2)}) collective-permute-start(f32[5120]{0:T(1024)S(1)} %pad_maximum_fusion.6), channel_id=1, source_target_pairs={{0,4},{4,0},{8,12},{12,8},{16,20},{20,16},{24,28},{28,24},{32,36},... | collective-permute-start | bytes 61448 | tf_op jit(solution)/shard_map/ppermute | solution.py:44
  112.3 9.3 %collective-permute-start.17 = (f32[5120]{0:T(1024)S(1)}, f32[5120]{0:T(1024)S(1)}, u32[]{:S(2)}, u32[]{:S(2)}) collective-permute-start(f32[5120]{0:T(1024)S(1)} %bitcast.255), channel_id=1, source_target_pairs={{0,48},{4,52},{8,56},{12,60},{16,32},{20,36},{24,40},{28,44},{32,1... | collective-permute-start | bytes 61448 | tf_op jit(solution)/shard_map/ppermute | solution.py:44
  117.1 5.6 %collective-permute-start.16 = (f32[5120]{0:T(1024)S(1)}, f32[5120]{0:T(1024)S(1)}, u32[]{:S(2)}, u32[]{:S(2)}) collective-permute-start(f32[5120]{0:T(1024)S(1)} %bitcast.256), channel_id=1, source_target_pairs={{0,32},{4,36},{8,40},{12,44},{16,48},{20,52},{24,56},{28,60},{32,0... | collective-permute-start | bytes 61448 | tf_op jit(solution)/shard_map/ppermute | solution.py:44
  119.0 4.8 %collective-permute-start.15 = (f32[5120]{0:T(1024)S(1)}, f32[5120]{0:T(1024)S(1)}, u32[]{:S(2)}, u32[]{:S(2)}) collective-permute-start(f32[5120]{0:T(1024)S(1)} %bitcast.257), channel_id=1, source_target_pairs={{0,16},{4,20},{8,24},{12,28},{16,0},{20,4},{24,8},{28,12},{32,48},... | collective-permute-start | bytes 61448 | tf_op jit(solution)/shard_map/ppermute | solution.py:44
  127.8 8.7 %collective-permute-start.18 = (f32[5120]{0:T(1024)S(1)}, f32[5120]{0:T(1024)S(1)}, u32[]{:S(2)}, u32[]{:S(2)}) collective-permute-start(f32[5120]{0:T(1024)S(1)} %bitcast.258), channel_id=1, source_target_pairs={{0,64},{4,68},{8,72},{12,76},{16,80},{20,84},{24,88},{28,92},{32,9... | collective-permute-start | bytes 61448 | tf_op jit(solution)/shard_map/ppermute | solution.py:44
  137.2 18.2 %copy-start.6 = (bf16[128,1024]{0,1:T(8,128)(2,1)S(1)}, bf16[128,1024]{0,1:T(8,128)(2,1)}, u32[]{:S(2)}) copy-start(bf16[128,1024]{0,1:T(8,128)(2,1)} %get-tuple-element.18) | copy-start | bytes 786436
  137.2 16.9 %collective-permute-start.21 = (f32[5120]{0:T(1024)S(1)}, f32[5120]{0:T(1024)S(1)}, u32[]{:S(2)}, u32[]{:S(2)}) collective-permute-start(f32[5120]{0:T(1024)S(1)} %bitcast.252), channel_id=1, source_target_pairs={{0,3},{1,2},{2,1},{3,0},{4,7},{5,6},{6,5},{7,4},{8,11},{9,10},{10,... | collective-permute-start | bytes 61448 | tf_op jit(solution)/shard_map/ppermute | solution.py:44
  141.7 13.7 %collective-permute-start.20 = (f32[5120]{0:T(1024)S(1)}, f32[5120]{0:T(1024)S(1)}, u32[]{:S(2)}, u32[]{:S(2)}) collective-permute-start(f32[5120]{0:T(1024)S(1)} %bitcast.253), channel_id=1, source_target_pairs={{0,2},{1,3},{2,0},{3,1},{4,6},{5,7},{6,4},{7,5},{8,10},{9,11},{10,... | collective-permute-start | bytes 61448 | tf_op jit(solution)/shard_map/ppermute | solution.py:44
  144.2 12.5 %collective-permute-start.19 = (f32[5120]{0:T(1024)S(1)}, f32[5120]{0:T(1024)S(1)}, u32[]{:S(2)}, u32[]{:S(2)}) collective-permute-start(f32[5120]{0:T(1024)S(1)} %bitcast.254), channel_id=1, source_target_pairs={{0,1},{1,0},{2,3},{3,2},{4,5},{5,4},{6,7},{7,6},{8,9},{9,8},{10,11... | collective-permute-start | bytes 61448 | tf_op jit(solution)/shard_map/ppermute | solution.py:44
  147.8 10.6 %collective-permute-start.8 = (bf16[128,1024]{0,1:T(8,128)(2,1)}, bf16[128,1024]{0,1:T(8,128)(2,1)S(1)}, u32[]{:S(2)}, u32[]{:S(2)}) collective-permute-start(bf16[128,1024]{0,1:T(8,128)(2,1)} %get-tuple-element.15), channel_id=1, source_target_pairs={{16,0},{20,4},{24,8},{28,12},{32,16},{36,20},{40,24},{44,28},{48,3... | collective-permute-start | bytes 786440 | tf_op jit(solution)/shard_map/ppermute | solution.py:25
  149.1 9.6 %collective-permute-start.11 = (bf16[128,1024]{0,1:T(8,128)(2,1)}, bf16[128,1024]{0,1:T(8,128)(2,1)S(1)}, u32[]{:S(2)}, u32[]{:S(2)}) collective-permute-start(bf16[128,1024]{0,1:T(8,128)(2,1)} %get-tuple-element.16), channel_id=1, source_target_pairs={{4,0},{8,4},{12,8},{16,12},{20,16},{24,20},{28,24},{32,28},{36,32}... | collective-permute-start | bytes 786440 | tf_op jit(solution)/shard_map/ppermute | solution.py:25
  154.1 10.1 %collective-permute-start.10 = (bf16[128,1024]{0,1:T(8,128)(2,1)}, bf16[128,1024]{0,1:T(8,128)(2,1)S(1)}, u32[]{:S(2)}, u32[]{:S(2)}) collective-permute-start(bf16[128,1024]{0,1:T(8,128)(2,1)} %get-tuple-element.17), channel_id=1, source_target_pairs={{8,0},{12,4},{16,8},{20,12},{24,16},{28,20},{32,24},{36,28},{40,32... | collective-permute-start | bytes 786440 | tf_op jit(solution)/shard_map/ppermute | solution.py:25
  155.4 17.3 %collective-permute-start.9 = (bf16[128,1024]{0,1:T(8,128)(2,1)S(1)}, bf16[128,1024]{0,1:T(8,128)(2,1)S(1)}, u32[]{:S(2)}, u32[]{:S(2)}) collective-permute-start(bf16[128,1024]{0,1:T(8,128)(2,1)S(1)} %copy-done.6), channel_id=1, source_target_pairs={{12,0},{16,4},{20,8},{24,12},{28,16},{32,20},{36,24},{40,28},{44,3... | collective-permute-start | bytes 786440 | tf_op jit(solution)/shard_map/ppermute | solution.py:25

commit v5 on v4

--- a/solution.py
+++ b/solution.py
@@ -51,6 +51,23 @@
             ordered = ordered[0::2] + ordered[1::2]
         value = ordered[0]
     return value
+
+
+def exchange_sum(value, axes):
+    count = 1
+    for axis in axes:
+        count *= lax.axis_size(axis)
+    if value.shape[0] % count:
+        return group_sum(group_sum(value, axes[0]), axes[1])
+    pieces = lax.all_to_all(value.reshape(count, -1), axes, 0, 0, tiled=True)
+    ordered = pieces
+    while ordered.shape[0] > 1:
+        if ordered.shape[0] % 2:
+            ordered = jnp.concatenate([ordered[:1] + ordered[1:2], ordered[2:]])
+        else:
+            ordered = ordered[0::2] + ordered[1::2]
+    mine = jnp.broadcast_to(ordered, (count, ordered.shape[1]))
+    return lax.all_to_all(mine, axes, 0, 0, tiled=True).reshape(-1)
 
 
 def attend_group(query_g, key_g, value_g, cot_g, visible, scaling):
@@ -128,7 +145,7 @@
         part = grad_window[block * shard_length : (block + 1) * shard_length]
         grad_own = grad_own + shifted(part.astype(jnp.bfloat16), "ctx", -steps).astype(jnp.float32)
 
-    offset_overall = group_sum(group_sum(offset_parts, "ctx"), "dp")
+    offset_overall = exchange_sum(offset_parts, ("ctx", "dp"))
     bias_scaled = offset_overall / math.sqrt(lax.axis_size("dp") * shard_length * ctx_size)
 
     query_grad = query_flat.astype(jnp.bfloat16)[None, None]

time: 177 us -> 149 us (0.84)
  waiting for transfers between devices: 27.7 us -> 16.3 us
  starting transfers between devices: 84.5 us -> 76.8 us
  other arithmetic: 9.2 us -> 4.87 us
  local copies, waits for them, and re-layouts: 20.2 us -> 16.9 us
    ppermute x10 -> x0, starting transfers between devices: 45.3 us -> none  [group_sum(): lax.ppermute(value, axis, [(i, i ^ t * stride) for i in range(count)])]
    all_to_all x0 -> x2, starting transfers between devices: none -> 39.7 us  [the longest x1 25.8 us: exchange_sum(): pieces = lax.all_to_all(value.reshape(count, -1), axes, 0, 0, tiled=True)]
    ppermute x8, waiting for transfers between devices: 14.3 us -> 0.02 us  [shifted(): return lax.ppermute(value, axis, pairs)]
    all_to_all x0 -> x2, waiting for transfers between devices: none -> 10.9 us  [the longest x1 8.6 us: exchange_sum(): return lax.all_to_all(mine, axes, 0, 0, tiled=True).reshape(-1)]
    ppermute x10 -> x0, waiting for transfers between devices: 6.92 us -> none  [group_sum(): lax.ppermute(value, axis, [(i, i ^ t * stride) for i in range(count)])]
    gather x4 -> x0, local copies, waits for them, and re-layouts: 3.6 us -> none  [group_sum(): ordered = jnp.take(stack, spot ^ jnp.arange(radix), axis=0)]
    ppermute x8, starting transfers between devices: 23.5 us -> 21.4 us  [shifted(): return lax.ppermute(value, axis, pairs)]
    select_n x8 -> x0, other arithmetic: 2.12 us -> none  [group_sum(): ordered = jnp.take(stack, spot ^ jnp.arange(radix), axis=0)]
  transfers between devices with their start and end apart: 22 -> 14, of which waited for: 8 -> 3; matrix products, arithmetic and copies ran while one was open for 20% -> 24% of each run, Pallas kernels for 0% -> 0%
where the time goes in v5:
time: 149 us; the launch traced here: 148 us
  starting transfers between devices  76.8 us (52%)
  matrix products  32.2 us (22%)
  local copies, waits for them, and re-layouts  16.9 us (11%)
  waiting for transfers between devices  16.3 us (11%)
  other arithmetic  4.87 us (3%)
    all_to_all x1, starting transfers between devices, exchange_sum(): pieces = lax.all_to_all(value.reshape(count, -1), axes, 0, 0, tiled=True)  25.8 us
    ppermute x8, starting transfers between devices, shifted(): return lax.ppermute(value, axis, pairs)  21.4 us
    ppermute x4, starting transfers between devices, passed_along(): return lax.ppermute(value, axis, pairs)  15.8 us
    all_to_all x1, starting transfers between devices, exchange_sum(): return lax.all_to_all(mine, axes, 0, 0, tiled=True).reshape(-1)  13.9 us
    unnamed x38, local copies, waits for them, and re-layouts  12.2 us
    sub x4, matrix products, attend_group(): weights = jnp.where(visible[None], jnp.exp(scores - row_max), 0.0)  10.5 us
    all_to_all x1, waiting for transfers between devices, exchange_sum(): return lax.all_to_all(mine, axes, 0, 0, tiled=True).reshape(-1)  8.6 us
    dot_general x4, matrix products, attend_group(): jnp.einsum('hqk,kd->qhd', probs_b, value_g, preferred_element_type=jnp.fl...  6.44 us
  transfers between devices with their start and end apart: 14, of which 3 were waited for; matrix products, arithmetic and copies ran while one was open for 24% of the time, Pallas kernels for 0%

profile of v5, /device:TPU:1, one launch (start us, length us, event | category | flops | bytes accessed | tf_op | source)
XLA Modules:
  0.0 148.4 jit_solution(3876386211689986363)
XLA Ops:
  0.7 1.8 %pad_maximum_fusion.1 = bf16[128,1024]{1,0:T(8,128)(2,1)} fusion(bf16[128,512]{1,0:T(8,128)(2,1)} %bitcast.233, bf16[128,512]{1,0:T(8,128)(2,1)} %bitcast.235), kind=kLoop, calls=%fused_computation.94 | loop fusion | flops 524288 | bytes 524288 | tf_op jit(solution)/shard_map/concatenate | solution.py:107
  2.4 5.4 %collective-permute-start.3 = (bf16[128,1024]{1,0:T(8,128)(2,1)}, bf16[128,1024]{1,0:T(8,128)(2,1)}, u32[]{:S(2)}, u32[]{:S(2)}) collective-permute-start(bf16[128,1024]{1,0:T(8,128)(2,1)} %pad_maximum_fusion.1), channel_id=1, source_target_pairs={{0,4},{4,8},{8,12},{12,16},{16,20},{20,24},{24,28},{28,32},{32,36}... | collective-permute-start | bytes 786440 | tf_op jit(solution)/shard_map/ppermute | solution.py:25
  7.8 3.0 %collective-permute-start.2 = (bf16[128,1024]{1,0:T(8,128)(2,1)}, bf16[128,1024]{1,0:T(8,128)(2,1)}, u32[]{:S(2)}, u32[]{:S(2)}) collective-permute-start(bf16[128,1024]{1,0:T(8,128)(2,1)} %pad_maximum_fusion.1), channel_id=1, source_target_pairs={{0,8},{4,12},{8,16},{12,20},{16,24},{20,28},{24,32},{28,36},{32,40... | collective-permute-start | bytes 786440 | tf_op jit(solution)/shard_map/ppermute | solution.py:25
  10.8 3.1 %collective-permute-start.1 = (bf16[128,1024]{1,0:T(8,128)(2,1)}, bf16[128,1024]{1,0:T(8,128)(2,1)}, u32[]{:S(2)}, u32[]{:S(2)}) collective-permute-start(bf16[128,1024]{1,0:T(8,128)(2,1)} %pad_maximum_fusion.1), channel_id=1, source_target_pairs={{0,12},{4,16},{8,20},{12,24},{16,28},{20,32},{24,36},{28,40},{32,4... | collective-permute-start | bytes 786440 | tf_op jit(solution)/shard_map/ppermute | solution.py:25
  13.9 3.2 %collective-permute-start = (bf16[128,1024]{1,0:T(8,128)(2,1)}, bf16[128,1024]{1,0:T(8,128)(2,1)}, u32[]{:S(2)}, u32[]{:S(2)}) collective-permute-start(bf16[128,1024]{1,0:T(8,128)(2,1)} %pad_maximum_fusion.1), channel_id=1, source_target_pairs={{0,16},{4,20},{8,24},{12,28},{16,32},{20,36},{24,40},{28,44},{32,4... | collective-permute-start | bytes 786440 | tf_op jit(solution)/shard_map/ppermute | solution.py:25
  17.2 1.3 fusion.105
  18.6 9.8 %collective-permute-start.7 = (bf16[128,1024]{0,1:T(8,128)(2,1)S(1)}, bf16[128,1024]{0,1:T(8,128)(2,1)}, u32[]{:S(2)}, u32[]{:S(2)}) collective-permute-start(bf16[128,1024]{0,1:T(8,128)(2,1)S(1)} %bitcast.237), channel_id=1, source_target_pairs={{0,384},{128,0},{256,128},{384,256},{1,385},{129,1},{257,129},{385... | collective-permute-start | bytes 786440 | tf_op jit(solution)/shard_map/ppermute | solution.py:19
  29.5 0.9 copy.182
  30.4 0.8 copy.180
  31.2 2.2 %collective-permute-start.5 = (bf16[128,1024]{0,1:T(8,128)(2,1)}, bf16[128,1024]{0,1:T(8,128)(2,1)}, u32[]{:S(2)}, u32[]{:S(2)}) collective-permute-start(bf16[128,1024]{0,1:T(8,128)(2,1)} %bitcast.20), channel_id=1, source_target_pairs={{0,384},{128,0},{256,128},{384,256},{1,385},{129,1},{257,129},{385... | collective-permute-start | bytes 786440 | tf_op jit(solution)/shard_map/ppermute | solution.py:19
  33.4 1.0 constant_dynamic-update-slice_fusion.4
  34.4 1.9 %collective-permute-start.6 = (bf16[128,1024]{0,1:T(8,128)(2,1)}, bf16[128,1024]{0,1:T(8,128)(2,1)}, u32[]{:S(2)}, u32[]{:S(2)}) collective-permute-start(bf16[128,1024]{0,1:T(8,128)(2,1)} %bitcast.31), channel_id=1, source_target_pairs={{0,384},{128,0},{256,128},{384,256},{1,385},{129,1},{257,129},{385... | collective-permute-start | bytes 786440 | tf_op jit(solution)/shard_map/ppermute | solution.py:19
  36.3 1.0 constant_dynamic-update-slice_fusion.3
  37.3 1.9 %collective-permute-start.4 = (bf16[128,1024]{0,1:T(8,128)(2,1)S(1)}, bf16[128,1024]{0,1:T(8,128)(2,1)S(1)}, u32[]{:S(2)}, u32[]{:S(2)}) collective-permute-start(bf16[128,1024]{0,1:T(8,128)(2,1)S(1)} %bitcast.238), channel_id=1, source_target_pairs={{0,384},{128,0},{256,128},{384,256},{1,385},{129,1},{257,129},{385... | collective-permute-start | bytes 786440 | tf_op jit(solution)/shard_map/ppermute | solution.py:19
  39.2 1.0 constant_dynamic-update-slice_fusion.2
  40.2 1.0 constant_dynamic-update-slice_fusion.1
  41.2 2.7 %fusion.106 = (f32[8,128]{1,0:T(8,128)S(1)}, f32[8,128,640]{1,2,0:T(8,128)}) fusion(pred[128,640]{0,1:T(8,128)(4,1)S(1)} %fusion.50, bf16[128,32,128]{0,2,1:T(8,128)(2,1)S(1)} %bitcast.225, bf16[640,1024]{1,0:T(8,128)(2,1)S(1)} %constant_dynamic-update-slice_fusion), kind=kOutput, calls=%fused_computation.143 | convolution fusion | flops 171049600 | bytes 3215360 | tf_op jit(solution)/shard_map/sub | solution.py:79
  43.9 2.6 %fusion.112 = (f32[8,128]{1,0:T(8,128)S(1)}, f32[8,128,640]{1,2,0:T(8,128)}) fusion(pred[128,640]{0,1:T(8,128)(4,1)S(1)} %fusion.50, bf16[128,32,128]{0,2,1:T(8,128)(2,1)S(1)} %bitcast.226, bf16[640,1024]{1,0:T(8,128)(2,1)S(1)} %constant_dynamic-update-slice_fusion), kind=kOutput, calls=%fused_computation.145 | convolution fusion | flops 171049600 | bytes 3215360 | tf_op jit(solution)/shard_map/sub | solution.py:79
  46.5 2.6 %fusion.109 = (f32[8,128]{1,0:T(8,128)S(1)}, f32[8,128,640]{1,2,0:T(8,128)}) fusion(pred[128,640]{0,1:T(8,128)(4,1)S(1)} %fusion.50, bf16[128,32,128]{0,2,1:T(8,128)(2,1)S(1)} %bitcast.227, bf16[640,1024]{1,0:T(8,128)(2,1)S(1)} %constant_dynamic-update-slice_fusion), kind=kOutput, calls=%fused_computation.144 | convolution fusion | flops 171049600 | bytes 3215360 | tf_op jit(solution)/shard_map/sub | solution.py:79
  49.1 2.6 %fusion.115 = (f32[8,128]{1,0:T(8,128)S(1)}, f32[8,128,640]{1,2,0:T(8,128)}) fusion(pred[128,640]{0,1:T(8,128)(4,1)S(1)} %fusion.50, bf16[128,32,128]{0,2,1:T(8,128)(2,1)S(1)} %bitcast.228, bf16[640,1024]{1,0:T(8,128)(2,1)S(1)} %constant_dynamic-update-slice_fusion), kind=kOutput, calls=%fused_computation.146 | convolution fusion | flops 171049600 | bytes 3215360 | tf_op jit(solution)/shard_map/sub | solution.py:79
  51.7 5.3 %collective-permute-done.4 = bf16[128,1024]{0,1:T(8,128)(2,1)S(1)} collective-permute-done((bf16[128,1024]{0,1:T(8,128)(2,1)S(1)}, bf16[128,1024]{0,1:T(8,128)(2,1)S(1)}, u32[]{:S(2)}, u32[]{:S(2)}) %collective-permute-start.4) | collective-permute-done | bytes 262176 | tf_op jit(solution)/shard_map/ppermute | solution.py:19
  57.0 2.3 %multiply_reduce_fusion.3 = f32[128,8]{0,1:T(8,128)S(1)} fusion(bf16[128,8,128]{0,2,1:T(8,128)(2,1)S(1)} %bitcast.243, bf16[640,1024]{1,0:T(8,128)(2,1)S(1)} %constant_dynamic-update-slice_fusion, f32[8,128,640]{1,2,0:T(8,128)} %get-tuple-element.29, f32[8,128]{1,0:T(8,128)S(1)} %get-tuple-element.28), kind=kOutput, calls=%fused_computation.87 | convolution fusion | flops 169475072 | bytes 3055616 | tf_op jit(solution)/shard_map/hqk,kd->qhd/dot_general | solution.py:82
  61.4 1.4 multiply_reduce_fusion.1
  62.8 1.7 %fusion.9 = bf16[8,128,640]{1,2,0:T(8,128)(2,1)S(1)} fusion(bf16[128,8,128]{0,2,1:T(8,128)(2,1)} %bitcast.32, f32[8,128]{1,0:T(8,128)S(1)} %bitcast.247, f32[8,128,640]{1,2,0:T(8,128)S(1)} %copy-done.9, f32[8,128]{1,0:T(8,128)S(1)} %get-tuple-element.32, bf16[640,1024]{1,0:T(8,128)(2,1)S(1)} %constant_dynamic-update-slice_fusion), kind=kOutput, calls=%fused_computation.12 | convolution fusion | flops 171048960 | bytes 4366336 | tf_op jit(solution)/shard_map/qhd,kd->hqk/dot_general | solution.py:84
  64.6 1.4 convolution_bitcast_fusion.2
  66.6 1.4 multiply_reduce_fusion.2
  67.9 1.6 %fusion.12 = bf16[8,128,640]{1,2,0:T(8,128)(2,1)S(1)} fusion(bf16[128,8,128]{0,2,1:T(8,128)(2,1)} %bitcast.21, f32[8,128]{1,0:T(8,128)S(1)} %bitcast.248, f32[8,128,640]{1,2,0:T(8,128)S(1)} %copy-done.12, f32[8,128]{1,0:T(8,128)S(1)} %get-tuple-element.30, bf16[640,1024]{1,0:T(8,128)(2,1)S(1)} %copy-done.3), kind=kOutput, calls=%fused_computation.17 | convolution fusion | flops 171048960 | bytes 4366336 | tf_op jit(solution)/shard_map/qhd,kd->hqk/dot_general | solution.py:84
  71.3 1.4 multiply_reduce_fusion
  72.6 1.6 %fusion.6 = bf16[8,128,640]{1,2,0:T(8,128)(2,1)S(1)} fusion(bf16[128,8,128]{0,2,1:T(8,128)(2,1)} %bitcast.43, f32[8,128]{1,0:T(8,128)S(1)} %bitcast.249, f32[8,128,640]{1,2,0:T(8,128)S(1)} %copy-done.10, f32[8,128]{1,0:T(8,128)S(1)} %get-tuple-element.34, bf16[640,1024]{1,0:T(8,128)(2,1)S(1)} %copy-done.3), kind=kOutput, calls=%fused_computation.7 | convolution fusion | flops 171048960 | bytes 4366336 | tf_op jit(solution)/shard_map/qhd,kd->hqk/dot_general | solution.py:84
  75.7 1.5 %fusion.36 = f32[640,1024]{0,1:T(8,128)S(1)} fusion(f32[640,1024]{0,1:T(8,128)S(1)} %fusion.37, bf16[128,8,128]{0,2,1:T(8,128)(2,1)} %bitcast.21, f32[8,128,640]{1,2,0:T(8,128)S(1)} %copy-done.12, f32[8,128]{1,0:T(8,128)S(1)} %get-tuple-element.30), kind=kOutput, calls=%fused_computation.64 | convolution fusion | flops 169082880 | bytes 3215360 | tf_op jit(solution)/shard_map/hqk,qhd->kd/dot_general | solution.py:88
  77.3 1.5 %fusion.35 = f32[640,1024]{0,1:T(8,128)S(1)} fusion(f32[640,1024]{0,1:T(8,128)S(1)} %fusion.36, bf16[128,8,128]{0,2,1:T(8,128)(2,1)} %bitcast.32, f32[8,128,640]{1,2,0:T(8,128)S(1)} %copy-done.9, f32[8,128]{1,0:T(8,128)S(1)} %get-tuple-element.32), kind=kOutput, calls=%fused_computation.62 | convolution fusion | flops 169082880 | bytes 3215360 | tf_op jit(solution)/shard_map/hqk,qhd->kd/dot_general | solution.py:88
  78.8 1.5 %fusion.34 = f32[640,1024]{0,1:T(8,128)S(1)} fusion(f32[640,1024]{0,1:T(8,128)S(1)} %fusion.35, bf16[128,8,128]{0,2,1:T(8,128)(2,1)} %bitcast.43, f32[8,128,640]{1,2,0:T(8,128)S(1)} %copy-done.10, f32[8,128]{1,0:T(8,128)S(1)} %get-tuple-element.34), kind=kOutput, calls=%fused_computation.60 | convolution fusion | flops 169082880 | bytes 3215360 | tf_op jit(solution)/shard_map/hqk,qhd->kd/dot_general | solution.py:88
  80.3 1.5 %copy-done = f32[640,1024]{0,1:T(8,128)} copy-done((f32[640,1024]{0,1:T(8,128)}, f32[640,1024]{0,1:T(8,128)S(1)}, u32[]{:S(2)}) %copy-start) | copy-done | bytes 2621464
  82.1 0.8 fusion.32
  83.6 25.8 %all-to-all-start = ((f32[128,1,40]{2,1,0:T(1,128)}), f32[128,1,40]{2,1,0:T(1,128)S(1)}, u32[]{:S(2)}, u32[]{:S(2)}) async-start(f32[128,1,40]{2,1,0:T(1,128)} %bitcast.61), calls=%async_computation | async-start | bytes 131072 | tf_op jit(solution)/shard_map/all_to_all | solution.py:62
  109.4 1.1 fusion.104
  110.4 1.3 collective-permute-start.8
  111.7 2.8 %collective-permute-start.11 = (bf16[128,1024]{0,1:T(8,128)(2,1)}, bf16[128,1024]{0,1:T(8,128)(2,1)}, u32[]{:S(2)}, u32[]{:S(2)}) collective-permute-start(bf16[128,1024]{0,1:T(8,128)(2,1)} %get-tuple-element.19), channel_id=1, source_target_pairs={{4,0},{8,4},{12,8},{16,12},{20,16},{24,20},{28,24},{32,28},{36,32}... | collective-permute-start | bytes 786440 | tf_op jit(solution)/shard_map/ppermute | solution.py:25
  114.5 1.3 collective-permute-start.10
  115.8 1.3 collective-permute-start.9
  117.1 2.3 %all-to-all-done = f32[128,1,40]{2,1,0:T(1,128)S(1)} async-done(((f32[128,1,40]{2,1,0:T(1,128)}), f32[128,1,40]{2,1,0:T(1,128)S(1)}, u32[]{:S(2)}, u32[]{:S(2)}) %all-to-all-start) | async-done | bytes 20512 | tf_op jit(solution)/shard_map/all_to_all | solution.py:62
  120.4 13.9 %all-to-all-start.1 = ((f32[128,1,40]{2,1,0:T(1,128)}), f32[128,1,40]{2,1,0:T(1,128)S(1)}, u32[]{:S(2)}, u32[]{:S(2)}) async-start(f32[128,1,40]{2,1,0:T(1,128)} %broadcast_in_dim.85), calls=%async_computation.1 | async-start | bytes 131072 | tf_op jit(solution)/shard_map/all_to_all | solution.py:70
  134.5 1.3 copy.134
  135.9 8.6 %all-to-all-done.1 = f32[128,1,40]{2,1,0:T(1,128)S(1)} async-done(((f32[128,1,40]{2,1,0:T(1,128)}), f32[128,1,40]{2,1,0:T(1,128)S(1)}, u32[]{:S(2)}, u32[]{:S(2)}) %all-to-all-start.1) | async-done | bytes 20512 | tf_op jit(solution)/shard_map/all_to_all | solution.py:70
  144.6 0.7 div.50
  145.4 1.4 fusion.49
  146.9 0.8 copy.136
  147.6 0.8 copy.135
  (79 shorter events, 9.4 us)
Async XLA Ops:
  0.6 27.8 %copy-start.6 = (s32[1,4096]{1,0:T(1,128)S(1)}, s32[1,4096]{1,0:T(1,128)}, u32[]{:S(2)}) copy-start(s32[1,4096]{1,0:T(1,128)} %param.9) | copy-start | bytes 49156
  0.6 28.0 %copy-start.1 = (bf16[1,1,128,4096]{3,2,1,0:T(8,128)(2,1)S(1)}, bf16[1,1,128,4096]{3,2,1,0:T(8,128)(2,1)}, u32[]{:S(2)}) copy-start(bf16[1,1,128,4096]{3,2,1,0:T(8,128)(2,1)} %param.5) | copy-start | bytes 3145732
  2.4 37.7 %collective-permute-start.3 = (bf16[128,1024]{1,0:T(8,128)(2,1)}, bf16[128,1024]{1,0:T(8,128)(2,1)}, u32[]{:S(2)}, u32[]{:S(2)}) collective-permute-start(bf16[128,1024]{1,0:T(8,128)(2,1)} %pad_maximum_fusion.1), channel_id=1, source_target_pairs={{0,4},{4,8},{8,12},{12,16},{16,20},{20,24},{24,28},{28,32},{32,36}... | collective-permute-start | bytes 786440 | tf_op jit(solution)/shard_map/ppermute | solution.py:25
  7.8 29.5 %collective-permute-start.2 = (bf16[128,1024]{1,0:T(8,128)(2,1)}, bf16[128,1024]{1,0:T(8,128)(2,1)}, u32[]{:S(2)}, u32[]{:S(2)}) collective-permute-start(bf16[128,1024]{1,0:T(8,128)(2,1)} %pad_maximum_fusion.1), channel_id=1, source_target_pairs={{0,8},{4,12},{8,16},{12,20},{16,24},{20,28},{24,32},{28,36},{32,40... | collective-permute-start | bytes 786440 | tf_op jit(solution)/shard_map/ppermute | solution.py:25
  10.8 23.5 %collective-permute-start.1 = (bf16[128,1024]{1,0:T(8,128)(2,1)}, bf16[128,1024]{1,0:T(8,128)(2,1)}, u32[]{:S(2)}, u32[]{:S(2)}) collective-permute-start(bf16[128,1024]{1,0:T(8,128)(2,1)} %pad_maximum_fusion.1), channel_id=1, source_target_pairs={{0,12},{4,16},{8,20},{12,24},{16,28},{20,32},{24,36},{28,40},{32,4... | collective-permute-start | bytes 786440 | tf_op jit(solution)/shard_map/ppermute | solution.py:25
  13.9 17.3 %collective-permute-start = (bf16[128,1024]{1,0:T(8,128)(2,1)}, bf16[128,1024]{1,0:T(8,128)(2,1)}, u32[]{:S(2)}, u32[]{:S(2)}) collective-permute-start(bf16[128,1024]{1,0:T(8,128)(2,1)} %pad_maximum_fusion.1), channel_id=1, source_target_pairs={{0,16},{4,20},{8,24},{12,28},{16,32},{20,36},{24,40},{28,44},{32,4... | collective-permute-start | bytes 786440 | tf_op jit(solution)/shard_map/ppermute | solution.py:25
  18.6 52.4 %collective-permute-start.7 = (bf16[128,1024]{0,1:T(8,128)(2,1)S(1)}, bf16[128,1024]{0,1:T(8,128)(2,1)}, u32[]{:S(2)}, u32[]{:S(2)}) collective-permute-start(bf16[128,1024]{0,1:T(8,128)(2,1)S(1)} %bitcast.237), channel_id=1, source_target_pairs={{0,384},{128,0},{256,128},{384,256},{1,385},{129,1},{257,129},{385... | collective-permute-start | bytes 786440 | tf_op jit(solution)/shard_map/ppermute | solution.py:19
  28.6 12.5 %copy-start.4 = (bf16[1,1,128,512]{3,2,1,0:T(8,128)(2,1)S(1)}, bf16[1,1,128,512]{3,2,1,0:T(8,128)(2,1)}, u32[]{:S(2)}) copy-start(bf16[1,1,128,512]{3,2,1,0:T(8,128)(2,1)} %param.7) | copy-start | bytes 393220
  28.7 12.5 %copy-start.5 = (bf16[1,1,128,512]{3,2,1,0:T(8,128)(2,1)S(1)}, bf16[1,1,128,512]{3,2,1,0:T(8,128)(2,1)}, u32[]{:S(2)}) copy-start(bf16[1,1,128,512]{3,2,1,0:T(8,128)(2,1)} %param.6) | copy-start | bytes 393220
  31.2 35.3 %collective-permute-start.5 = (bf16[128,1024]{0,1:T(8,128)(2,1)}, bf16[128,1024]{0,1:T(8,128)(2,1)}, u32[]{:S(2)}, u32[]{:S(2)}) collective-permute-start(bf16[128,1024]{0,1:T(8,128)(2,1)} %bitcast.20), channel_id=1, source_target_pairs={{0,384},{128,0},{256,128},{384,256},{1,385},{129,1},{257,129},{385... | collective-permute-start | bytes 786440 | tf_op jit(solution)/shard_map/ppermute | solution.py:19
  34.4 26.3 %collective-permute-start.6 = (bf16[128,1024]{0,1:T(8,128)(2,1)}, bf16[128,1024]{0,1:T(8,128)(2,1)}, u32[]{:S(2)}, u32[]{:S(2)}) collective-permute-start(bf16[128,1024]{0,1:T(8,128)(2,1)} %bitcast.31), channel_id=1, source_target_pairs={{0,384},{128,0},{256,128},{384,256},{1,385},{129,1},{257,129},{385... | collective-permute-start | bytes 786440 | tf_op jit(solution)/shard_map/ppermute | solution.py:19
  37.3 19.8 %collective-permute-start.4 = (bf16[128,1024]{0,1:T(8,128)(2,1)S(1)}, bf16[128,1024]{0,1:T(8,128)(2,1)S(1)}, u32[]{:S(2)}, u32[]{:S(2)}) collective-permute-start(bf16[128,1024]{0,1:T(8,128)(2,1)S(1)} %bitcast.238), channel_id=1, source_target_pairs={{0,384},{128,0},{256,128},{384,256},{1,385},{129,1},{257,129},{385... | collective-permute-start | bytes 786440 | tf_op jit(solution)/shard_map/ppermute | solution.py:19
  41.2 21.6 %copy-start.2 = (bf16[640,1024]{1,0:T(8,128)(2,1)}, bf16[640,1024]{1,0:T(8,128)(2,1)S(1)}, u32[]{:S(2)}) copy-start(bf16[640,1024]{1,0:T(8,128)(2,1)S(1)} %constant_dynamic-update-slice_fusion) | copy-start | bytes 3932164
  57.0 2.3 %copy-start.7 = (bf16[128,1024]{0,1:T(8,128)(2,1)}, bf16[128,1024]{0,1:T(8,128)(2,1)S(1)}, u32[]{:S(2)}) copy-start(bf16[128,1024]{0,1:T(8,128)(2,1)S(1)} %collective-permute-done.4) | copy-start | bytes 786436
  57.0 2.6 %copy-start.11 = (f32[8,128,640]{1,2,0:T(8,128)S(1)}, f32[8,128,640]{1,2,0:T(8,128)}, u32[]{:S(2)}) copy-start(f32[8,128,640]{1,2,0:T(8,128)} %get-tuple-element.29) | copy-start | bytes 7864324
  59.7 1.7 %copy-start.9 = (f32[8,128,640]{1,2,0:T(8,128)S(1)}, f32[8,128,640]{1,2,0:T(8,128)}, u32[]{:S(2)}) copy-start(f32[8,128,640]{1,2,0:T(8,128)} %get-tuple-element.33) | copy-start | bytes 7864324
  62.8 3.7 %copy-start.12 = (f32[8,128,640]{1,2,0:T(8,128)S(1)}, f32[8,128,640]{1,2,0:T(8,128)}, u32[]{:S(2)}) copy-start(f32[8,128,640]{1,2,0:T(8,128)} %get-tuple-element.31) | copy-start | bytes 7864324
  64.5 2.0 %copy-start.3 = (bf16[640,1024]{1,0:T(8,128)(2,1)S(1)}, bf16[640,1024]{1,0:T(8,128)(2,1)}, u32[]{:S(2)}) copy-start(bf16[640,1024]{1,0:T(8,128)(2,1)} %copy-done.2) | copy-start | bytes 3932164
  69.5 1.7 %copy-start.10 = (f32[8,128,640]{1,2,0:T(8,128)S(1)}, f32[8,128,640]{1,2,0:T(8,128)}, u32[]{:S(2)}) copy-start(f32[8,128,640]{1,2,0:T(8,128)} %get-tuple-element.35) | copy-start | bytes 7864324
  74.2 1.0 copy-start.8
  80.3 1.5 %copy-start = (f32[640,1024]{0,1:T(8,128)}, f32[640,1024]{0,1:T(8,128)S(1)}, u32[]{:S(2)}) copy-start(f32[640,1024]{0,1:T(8,128)S(1)} %fusion.34) | copy-start | bytes 7864324
  83.6 35.9 %all-to-all-start = ((f32[128,1,40]{2,1,0:T(1,128)}), f32[128,1,40]{2,1,0:T(1,128)S(1)}, u32[]{:S(2)}, u32[]{:S(2)}) async-start(f32[128,1,40]{2,1,0:T(1,128)} %bitcast.61), calls=%async_computation | async-start | bytes 131072 | tf_op jit(solution)/shard_map/all_to_all | solution.py:62
  110.4 34.9 %collective-permute-start.8 = (bf16[128,1024]{0,1:T(8,128)(2,1)}, bf16[128,1024]{0,1:T(8,128)(2,1)S(1)}, u32[]{:S(2)}, u32[]{:S(2)}) collective-permute-start(bf16[128,1024]{0,1:T(8,128)(2,1)} %get-tuple-element.18), channel_id=1, source_target_pairs={{16,0},{20,4},{24,8},{28,12},{32,16},{36,20},{40,24},{44,28},{48,3... | collective-permute-start | bytes 786440 | tf_op jit(solution)/shard_map/ppermute | solution.py:25
  111.7 33.6 %collective-permute-start.11 = (bf16[128,1024]{0,1:T(8,128)(2,1)}, bf16[128,1024]{0,1:T(8,128)(2,1)}, u32[]{:S(2)}, u32[]{:S(2)}) collective-permute-start(bf16[128,1024]{0,1:T(8,128)(2,1)} %get-tuple-element.19), channel_id=1, source_target_pairs={{4,0},{8,4},{12,8},{16,12},{20,16},{24,20},{28,24},{32,28},{36,32}... | collective-permute-start | bytes 786440 | tf_op jit(solution)/shard_map/ppermute | solution.py:25
  114.5 30.8 %collective-permute-start.10 = (bf16[128,1024]{0,1:T(8,128)(2,1)}, bf16[128,1024]{0,1:T(8,128)(2,1)}, u32[]{:S(2)}, u32[]{:S(2)}) collective-permute-start(bf16[128,1024]{0,1:T(8,128)(2,1)} %get-tuple-element.20), channel_id=1, source_target_pairs={{8,0},{12,4},{16,8},{20,12},{24,16},{28,20},{32,24},{36,28},{40,32... | collective-permute-start | bytes 786440 | tf_op jit(solution)/shard_map/ppermute | solution.py:25
  115.8 29.5 %collective-permute-start.9 = (bf16[128,1024]{0,1:T(8,128)(2,1)}, bf16[128,1024]{0,1:T(8,128)(2,1)}, u32[]{:S(2)}, u32[]{:S(2)}) collective-permute-start(bf16[128,1024]{0,1:T(8,128)(2,1)} %get-tuple-element.21), channel_id=1, source_target_pairs={{12,0},{16,4},{20,8},{24,12},{28,16},{32,20},{36,24},{40,28},{44,3... | collective-permute-start | bytes 786440 | tf_op jit(solution)/shard_map/ppermute | solution.py:25
  120.4 24.0 %all-to-all-start.1 = ((f32[128,1,40]{2,1,0:T(1,128)}), f32[128,1,40]{2,1,0:T(1,128)S(1)}, u32[]{:S(2)}, u32[]{:S(2)}) async-start(f32[128,1,40]{2,1,0:T(1,128)} %broadcast_in_dim.85), calls=%async_computation.1 | async-start | bytes 131072 | tf_op jit(solution)/shard_map/all_to_all | solution.py:70

commit v6 on v5

--- a/solution.py
+++ b/solution.py
@@ -100,10 +100,11 @@
     anchor = here * shard_length
 
     group_cols = QUERY_PER_KEY * FEATURE_SIZE
-    cot_groups = [
-        passed_along(incoming[0, 0, :, g * group_cols : (g + 1) * group_cols], "pipe", -1)
-        for g in range(SHARED_GROUPS)
-    ]
+    cot_groups = []
+    for g in range(SHARED_GROUPS):
+        cot_groups.append(
+            passed_along(incoming[0, 0, :, g * group_cols : (g + 1) * group_cols], "pipe", -1)
+        )
     kv_own = jnp.concatenate([key_input[0, 0], value_input[0, 0]], axis=1)
     kv_window = jnp.concatenate(
         [shifted(kv_own, "ctx", steps) for steps in range(reach, 0, -1)] + [kv_own], axis=0

time: 149 us -> 149 us (level)
  no operation moved by 1% of the time
where the time goes in v6:
time: 149 us; the launch traced here: 148 us
  starting transfers between devices  76.8 us (52%)
  matrix products  32.2 us (22%)
  local copies, waits for them, and re-layouts  16.9 us (11%)
  waiting for transfers between devices  16.3 us (11%)
  other arithmetic  4.87 us (3%)
    all_to_all x1, starting transfers between devices, exchange_sum(): pieces = lax.all_to_all(value.reshape(count, -1), axes, 0, 0, tiled=True)  25.8 us
    ppermute x8, starting transfers between devices, shifted(): return lax.ppermute(value, axis, pairs)  21.4 us
    ppermute x4, starting transfers between devices, passed_along(): return lax.ppermute(value, axis, pairs)  15.8 us
    all_to_all x1, starting transfers between devices, exchange_sum(): return lax.all_to_all(mine, axes, 0, 0, tiled=True).reshape(-1)  13.9 us
    unnamed x38, local copies, waits for them, and re-layouts  12.2 us
    sub x4, matrix products, attend_group(): weights = jnp.where(visible[None], jnp.exp(scores - row_max), 0.0)  10.5 us
    all_to_all x1, waiting for transfers between devices, exchange_sum(): return lax.all_to_all(mine, axes, 0, 0, tiled=True).reshape(-1)  8.6 us
    dot_general x4, matrix products, attend_group(): jnp.einsum('hqk,kd->qhd', probs_b, value_g, preferred_element_type=jnp.fl...  6.44 us
  transfers between devices with their start and end apart: 14, of which 3 were waited for; matrix products, arithmetic and copies ran while one was open for 24% of the time, Pallas kernels for 0%

profile of v6, /device:TPU:1, one launch (start us, length us, event | category | flops | bytes accessed | tf_op | source)
XLA Modules:
  0.0 148.4 jit_solution(3876386211689986363)
XLA Ops:
  0.7 1.8 %pad_maximum_fusion.1 = bf16[128,1024]{1,0:T(8,128)(2,1)} fusion(bf16[128,512]{1,0:T(8,128)(2,1)} %bitcast.233, bf16[128,512]{1,0:T(8,128)(2,1)} %bitcast.235), kind=kLoop, calls=%fused_computation.94 | loop fusion | flops 524288 | bytes 524288 | tf_op jit(solution)/shard_map/concatenate | solution.py:108
  2.4 5.4 %collective-permute-start.3 = (bf16[128,1024]{1,0:T(8,128)(2,1)}, bf16[128,1024]{1,0:T(8,128)(2,1)}, u32[]{:S(2)}, u32[]{:S(2)}) collective-permute-start(bf16[128,1024]{1,0:T(8,128)(2,1)} %pad_maximum_fusion.1), channel_id=1, source_target_pairs={{0,4},{4,8},{8,12},{12,16},{16,20},{20,24},{24,28},{28,32},{32,36}... | collective-permute-start | bytes 786440 | tf_op jit(solution)/shard_map/ppermute | solution.py:25
  7.8 3.0 %collective-permute-start.2 = (bf16[128,1024]{1,0:T(8,128)(2,1)}, bf16[128,1024]{1,0:T(8,128)(2,1)}, u32[]{:S(2)}, u32[]{:S(2)}) collective-permute-start(bf16[128,1024]{1,0:T(8,128)(2,1)} %pad_maximum_fusion.1), channel_id=1, source_target_pairs={{0,8},{4,12},{8,16},{12,20},{16,24},{20,28},{24,32},{28,36},{32,40... | collective-permute-start | bytes 786440 | tf_op jit(solution)/shard_map/ppermute | solution.py:25
  10.8 3.1 %collective-permute-start.1 = (bf16[128,1024]{1,0:T(8,128)(2,1)}, bf16[128,1024]{1,0:T(8,128)(2,1)}, u32[]{:S(2)}, u32[]{:S(2)}) collective-permute-start(bf16[128,1024]{1,0:T(8,128)(2,1)} %pad_maximum_fusion.1), channel_id=1, source_target_pairs={{0,12},{4,16},{8,20},{12,24},{16,28},{20,32},{24,36},{28,40},{32,4... | collective-permute-start | bytes 786440 | tf_op jit(solution)/shard_map/ppermute | solution.py:25
  13.9 3.2 %collective-permute-start = (bf16[128,1024]{1,0:T(8,128)(2,1)}, bf16[128,1024]{1,0:T(8,128)(2,1)}, u32[]{:S(2)}, u32[]{:S(2)}) collective-permute-start(bf16[128,1024]{1,0:T(8,128)(2,1)} %pad_maximum_fusion.1), channel_id=1, source_target_pairs={{0,16},{4,20},{8,24},{12,28},{16,32},{20,36},{24,40},{28,44},{32,4... | collective-permute-start | bytes 786440 | tf_op jit(solution)/shard_map/ppermute | solution.py:25
  17.2 1.3 fusion.105
  18.6 9.8 %collective-permute-start.7 = (bf16[128,1024]{0,1:T(8,128)(2,1)S(1)}, bf16[128,1024]{0,1:T(8,128)(2,1)}, u32[]{:S(2)}, u32[]{:S(2)}) collective-permute-start(bf16[128,1024]{0,1:T(8,128)(2,1)S(1)} %bitcast.237), channel_id=1, source_target_pairs={{0,384},{128,0},{256,128},{384,256},{1,385},{129,1},{257,129},{385... | collective-permute-start | bytes 786440 | tf_op jit(solution)/shard_map/ppermute | solution.py:19
  29.5 0.9 copy.182
  30.4 0.8 copy.180
  31.2 2.2 %collective-permute-start.5 = (bf16[128,1024]{0,1:T(8,128)(2,1)}, bf16[128,1024]{0,1:T(8,128)(2,1)}, u32[]{:S(2)}, u32[]{:S(2)}) collective-permute-start(bf16[128,1024]{0,1:T(8,128)(2,1)} %bitcast.20), channel_id=1, source_target_pairs={{0,384},{128,0},{256,128},{384,256},{1,385},{129,1},{257,129},{385... | collective-permute-start | bytes 786440 | tf_op jit(solution)/shard_map/ppermute | solution.py:19
  33.4 1.0 constant_dynamic-update-slice_fusion.4
  34.4 1.9 %collective-permute-start.6 = (bf16[128,1024]{0,1:T(8,128)(2,1)}, bf16[128,1024]{0,1:T(8,128)(2,1)}, u32[]{:S(2)}, u32[]{:S(2)}) collective-permute-start(bf16[128,1024]{0,1:T(8,128)(2,1)} %bitcast.31), channel_id=1, source_target_pairs={{0,384},{128,0},{256,128},{384,256},{1,385},{129,1},{257,129},{385... | collective-permute-start | bytes 786440 | tf_op jit(solution)/shard_map/ppermute | solution.py:19
  36.3 1.0 constant_dynamic-update-slice_fusion.3
  37.3 1.9 %collective-permute-start.4 = (bf16[128,1024]{0,1:T(8,128)(2,1)S(1)}, bf16[128,1024]{0,1:T(8,128)(2,1)S(1)}, u32[]{:S(2)}, u32[]{:S(2)}) collective-permute-start(bf16[128,1024]{0,1:T(8,128)(2,1)S(1)} %bitcast.238), channel_id=1, source_target_pairs={{0,384},{128,0},{256,128},{384,256},{1,385},{129,1},{257,129},{385... | collective-permute-start | bytes 786440 | tf_op jit(solution)/shard_map/ppermute | solution.py:19
  39.2 1.0 constant_dynamic-update-slice_fusion.2
  40.2 1.0 constant_dynamic-update-slice_fusion.1
  41.2 2.7 %fusion.106 = (f32[8,128]{1,0:T(8,128)S(1)}, f32[8,128,640]{1,2,0:T(8,128)}) fusion(pred[128,640]{0,1:T(8,128)(4,1)S(1)} %fusion.50, bf16[128,32,128]{0,2,1:T(8,128)(2,1)S(1)} %bitcast.225, bf16[640,1024]{1,0:T(8,128)(2,1)S(1)} %constant_dynamic-update-slice_fusion), kind=kOutput, calls=%fused_computation.143 | convolution fusion | flops 171049600 | bytes 3215360 | tf_op jit(solution)/shard_map/sub | solution.py:79
  43.9 2.6 %fusion.112 = (f32[8,128]{1,0:T(8,128)S(1)}, f32[8,128,640]{1,2,0:T(8,128)}) fusion(pred[128,640]{0,1:T(8,128)(4,1)S(1)} %fusion.50, bf16[128,32,128]{0,2,1:T(8,128)(2,1)S(1)} %bitcast.226, bf16[640,1024]{1,0:T(8,128)(2,1)S(1)} %constant_dynamic-update-slice_fusion), kind=kOutput, calls=%fused_computation.145 | convolution fusion | flops 171049600 | bytes 3215360 | tf_op jit(solution)/shard_map/sub | solution.py:79
  46.5 2.6 %fusion.109 = (f32[8,128]{1,0:T(8,128)S(1)}, f32[8,128,640]{1,2,0:T(8,128)}) fusion(pred[128,640]{0,1:T(8,128)(4,1)S(1)} %fusion.50, bf16[128,32,128]{0,2,1:T(8,128)(2,1)S(1)} %bitcast.227, bf16[640,1024]{1,0:T(8,128)(2,1)S(1)} %constant_dynamic-update-slice_fusion), kind=kOutput, calls=%fused_computation.144 | convolution fusion | flops 171049600 | bytes 3215360 | tf_op jit(solution)/shard_map/sub | solution.py:79
  49.1 2.6 %fusion.115 = (f32[8,128]{1,0:T(8,128)S(1)}, f32[8,128,640]{1,2,0:T(8,128)}) fusion(pred[128,640]{0,1:T(8,128)(4,1)S(1)} %fusion.50, bf16[128,32,128]{0,2,1:T(8,128)(2,1)S(1)} %bitcast.228, bf16[640,1024]{1,0:T(8,128)(2,1)S(1)} %constant_dynamic-update-slice_fusion), kind=kOutput, calls=%fused_computation.146 | convolution fusion | flops 171049600 | bytes 3215360 | tf_op jit(solution)/shard_map/sub | solution.py:79
  51.7 5.3 %collective-permute-done.4 = bf16[128,1024]{0,1:T(8,128)(2,1)S(1)} collective-permute-done((bf16[128,1024]{0,1:T(8,128)(2,1)S(1)}, bf16[128,1024]{0,1:T(8,128)(2,1)S(1)}, u32[]{:S(2)}, u32[]{:S(2)}) %collective-permute-start.4) | collective-permute-done | bytes 262176 | tf_op jit(solution)/shard_map/ppermute | solution.py:19
  57.0 2.3 %multiply_reduce_fusion.3 = f32[128,8]{0,1:T(8,128)S(1)} fusion(bf16[128,8,128]{0,2,1:T(8,128)(2,1)S(1)} %bitcast.243, bf16[640,1024]{1,0:T(8,128)(2,1)S(1)} %constant_dynamic-update-slice_fusion, f32[8,128,640]{1,2,0:T(8,128)} %get-tuple-element.29, f32[8,128]{1,0:T(8,128)S(1)} %get-tuple-element.28), kind=kOutput, calls=%fused_computation.87 | convolution fusion | flops 169475072 | bytes 3055616 | tf_op jit(solution)/shard_map/hqk,kd->qhd/dot_general | solution.py:82
  61.4 1.4 multiply_reduce_fusion.1
  62.8 1.7 %fusion.9 = bf16[8,128,640]{1,2,0:T(8,128)(2,1)S(1)} fusion(bf16[128,8,128]{0,2,1:T(8,128)(2,1)} %bitcast.32, f32[8,128]{1,0:T(8,128)S(1)} %bitcast.247, f32[8,128,640]{1,2,0:T(8,128)S(1)} %copy-done.9, f32[8,128]{1,0:T(8,128)S(1)} %get-tuple-element.32, bf16[640,1024]{1,0:T(8,128)(2,1)S(1)} %constant_dynamic-update-slice_fusion), kind=kOutput, calls=%fused_computation.12 | convolution fusion | flops 171048960 | bytes 4366336 | tf_op jit(solution)/shard_map/qhd,kd->hqk/dot_general | solution.py:84
  64.6 1.4 convolution_bitcast_fusion.2
  66.6 1.4 multiply_reduce_fusion.2
  67.9 1.6 %fusion.12 = bf16[8,128,640]{1,2,0:T(8,128)(2,1)S(1)} fusion(bf16[128,8,128]{0,2,1:T(8,128)(2,1)} %bitcast.21, f32[8,128]{1,0:T(8,128)S(1)} %bitcast.248, f32[8,128,640]{1,2,0:T(8,128)S(1)} %copy-done.12, f32[8,128]{1,0:T(8,128)S(1)} %get-tuple-element.30, bf16[640,1024]{1,0:T(8,128)(2,1)S(1)} %copy-done.3), kind=kOutput, calls=%fused_computation.17 | convolution fusion | flops 171048960 | bytes 4366336 | tf_op jit(solution)/shard_map/qhd,kd->hqk/dot_general | solution.py:84
  71.3 1.4 multiply_reduce_fusion
  72.6 1.6 %fusion.6 = bf16[8,128,640]{1,2,0:T(8,128)(2,1)S(1)} fusion(bf16[128,8,128]{0,2,1:T(8,128)(2,1)} %bitcast.43, f32[8,128]{1,0:T(8,128)S(1)} %bitcast.249, f32[8,128,640]{1,2,0:T(8,128)S(1)} %copy-done.10, f32[8,128]{1,0:T(8,128)S(1)} %get-tuple-element.34, bf16[640,1024]{1,0:T(8,128)(2,1)S(1)} %copy-done.3), kind=kOutput, calls=%fused_computation.7 | convolution fusion | flops 171048960 | bytes 4366336 | tf_op jit(solution)/shard_map/qhd,kd->hqk/dot_general | solution.py:84
  75.7 1.5 %fusion.36 = f32[640,1024]{0,1:T(8,128)S(1)} fusion(f32[640,1024]{0,1:T(8,128)S(1)} %fusion.37, bf16[128,8,128]{0,2,1:T(8,128)(2,1)} %bitcast.21, f32[8,128,640]{1,2,0:T(8,128)S(1)} %copy-done.12, f32[8,128]{1,0:T(8,128)S(1)} %get-tuple-element.30), kind=kOutput, calls=%fused_computation.64 | convolution fusion | flops 169082880 | bytes 3215360 | tf_op jit(solution)/shard_map/hqk,qhd->kd/dot_general | solution.py:88
  77.3 1.5 %fusion.35 = f32[640,1024]{0,1:T(8,128)S(1)} fusion(f32[640,1024]{0,1:T(8,128)S(1)} %fusion.36, bf16[128,8,128]{0,2,1:T(8,128)(2,1)} %bitcast.32, f32[8,128,640]{1,2,0:T(8,128)S(1)} %copy-done.9, f32[8,128]{1,0:T(8,128)S(1)} %get-tuple-element.32), kind=kOutput, calls=%fused_computation.62 | convolution fusion | flops 169082880 | bytes 3215360 | tf_op jit(solution)/shard_map/hqk,qhd->kd/dot_general | solution.py:88
  78.8 1.5 %fusion.34 = f32[640,1024]{0,1:T(8,128)S(1)} fusion(f32[640,1024]{0,1:T(8,128)S(1)} %fusion.35, bf16[128,8,128]{0,2,1:T(8,128)(2,1)} %bitcast.43, f32[8,128,640]{1,2,0:T(8,128)S(1)} %copy-done.10, f32[8,128]{1,0:T(8,128)S(1)} %get-tuple-element.34), kind=kOutput, calls=%fused_computation.60 | convolution fusion | flops 169082880 | bytes 3215360 | tf_op jit(solution)/shard_map/hqk,qhd->kd/dot_general | solution.py:88
  80.3 1.5 %copy-done = f32[640,1024]{0,1:T(8,128)} copy-done((f32[640,1024]{0,1:T(8,128)}, f32[640,1024]{0,1:T(8,128)S(1)}, u32[]{:S(2)}) %copy-start) | copy-done | bytes 2621464
  82.1 0.8 fusion.32
  83.6 25.8 %all-to-all-start = ((f32[128,1,40]{2,1,0:T(1,128)}), f32[128,1,40]{2,1,0:T(1,128)S(1)}, u32[]{:S(2)}, u32[]{:S(2)}) async-start(f32[128,1,40]{2,1,0:T(1,128)} %bitcast.61), calls=%async_computation | async-start | bytes 131072 | tf_op jit(solution)/shard_map/all_to_all | solution.py:62
  109.4 1.1 fusion.104
  110.4 1.3 collective-permute-start.8
  111.7 2.8 %collective-permute-start.11 = (bf16[128,1024]{0,1:T(8,128)(2,1)}, bf16[128,1024]{0,1:T(8,128)(2,1)}, u32[]{:S(2)}, u32[]{:S(2)}) collective-permute-start(bf16[128,1024]{0,1:T(8,128)(2,1)} %get-tuple-element.19), channel_id=1, source_target_pairs={{4,0},{8,4},{12,8},{16,12},{20,16},{24,20},{28,24},{32,28},{36,32}... | collective-permute-start | bytes 786440 | tf_op jit(solution)/shard_map/ppermute | solution.py:25
  114.5 1.3 collective-permute-start.10
  115.8 1.3 collective-permute-start.9
  117.1 2.3 %all-to-all-done = f32[128,1,40]{2,1,0:T(1,128)S(1)} async-done(((f32[128,1,40]{2,1,0:T(1,128)}), f32[128,1,40]{2,1,0:T(1,128)S(1)}, u32[]{:S(2)}, u32[]{:S(2)}) %all-to-all-start) | async-done | bytes 20512 | tf_op jit(solution)/shard_map/all_to_all | solution.py:62
  120.4 13.9 %all-to-all-start.1 = ((f32[128,1,40]{2,1,0:T(1,128)}), f32[128,1,40]{2,1,0:T(1,128)S(1)}, u32[]{:S(2)}, u32[]{:S(2)}) async-start(f32[128,1,40]{2,1,0:T(1,128)} %broadcast_in_dim.85), calls=%async_computation.1 | async-start | bytes 131072 | tf_op jit(solution)/shard_map/all_to_all | solution.py:70
  134.5 1.3 copy.134
  135.9 8.6 %all-to-all-done.1 = f32[128,1,40]{2,1,0:T(1,128)S(1)} async-done(((f32[128,1,40]{2,1,0:T(1,128)}), f32[128,1,40]{2,1,0:T(1,128)S(1)}, u32[]{:S(2)}, u32[]{:S(2)}) %all-to-all-start.1) | async-done | bytes 20512 | tf_op jit(solution)/shard_map/all_to_all | solution.py:70
  144.6 0.7 div.50
  145.4 1.4 fusion.49
  146.9 0.8 copy.136
  147.6 0.8 copy.135
  (79 shorter events, 9.4 us)
Async XLA Ops:
  0.6 27.8 %copy-start.6 = (s32[1,4096]{1,0:T(1,128)S(1)}, s32[1,4096]{1,0:T(1,128)}, u32[]{:S(2)}) copy-start(s32[1,4096]{1,0:T(1,128)} %param.9) | copy-start | bytes 49156
  0.6 28.0 %copy-start.1 = (bf16[1,1,128,4096]{3,2,1,0:T(8,128)(2,1)S(1)}, bf16[1,1,128,4096]{3,2,1,0:T(8,128)(2,1)}, u32[]{:S(2)}) copy-start(bf16[1,1,128,4096]{3,2,1,0:T(8,128)(2,1)} %param.5) | copy-start | bytes 3145732
  2.4 37.7 %collective-permute-start.3 = (bf16[128,1024]{1,0:T(8,128)(2,1)}, bf16[128,1024]{1,0:T(8,128)(2,1)}, u32[]{:S(2)}, u32[]{:S(2)}) collective-permute-start(bf16[128,1024]{1,0:T(8,128)(2,1)} %pad_maximum_fusion.1), channel_id=1, source_target_pairs={{0,4},{4,8},{8,12},{12,16},{16,20},{20,24},{24,28},{28,32},{32,36}... | collective-permute-start | bytes 786440 | tf_op jit(solution)/shard_map/ppermute | solution.py:25
  7.8 29.5 %collective-permute-start.2 = (bf16[128,1024]{1,0:T(8,128)(2,1)}, bf16[128,1024]{1,0:T(8,128)(2,1)}, u32[]{:S(2)}, u32[]{:S(2)}) collective-permute-start(bf16[128,1024]{1,0:T(8,128)(2,1)} %pad_maximum_fusion.1), channel_id=1, source_target_pairs={{0,8},{4,12},{8,16},{12,20},{16,24},{20,28},{24,32},{28,36},{32,40... | collective-permute-start | bytes 786440 | tf_op jit(solution)/shard_map/ppermute | solution.py:25
  10.8 23.5 %collective-permute-start.1 = (bf16[128,1024]{1,0:T(8,128)(2,1)}, bf16[128,1024]{1,0:T(8,128)(2,1)}, u32[]{:S(2)}, u32[]{:S(2)}) collective-permute-start(bf16[128,1024]{1,0:T(8,128)(2,1)} %pad_maximum_fusion.1), channel_id=1, source_target_pairs={{0,12},{4,16},{8,20},{12,24},{16,28},{20,32},{24,36},{28,40},{32,4... | collective-permute-start | bytes 786440 | tf_op jit(solution)/shard_map/ppermute | solution.py:25
  13.9 17.3 %collective-permute-start = (bf16[128,1024]{1,0:T(8,128)(2,1)}, bf16[128,1024]{1,0:T(8,128)(2,1)}, u32[]{:S(2)}, u32[]{:S(2)}) collective-permute-start(bf16[128,1024]{1,0:T(8,128)(2,1)} %pad_maximum_fusion.1), channel_id=1, source_target_pairs={{0,16},{4,20},{8,24},{12,28},{16,32},{20,36},{24,40},{28,44},{32,4... | collective-permute-start | bytes 786440 | tf_op jit(solution)/shard_map/ppermute | solution.py:25
  18.6 52.4 %collective-permute-start.7 = (bf16[128,1024]{0,1:T(8,128)(2,1)S(1)}, bf16[128,1024]{0,1:T(8,128)(2,1)}, u32[]{:S(2)}, u32[]{:S(2)}) collective-permute-start(bf16[128,1024]{0,1:T(8,128)(2,1)S(1)} %bitcast.237), channel_id=1, source_target_pairs={{0,384},{128,0},{256,128},{384,256},{1,385},{129,1},{257,129},{385... | collective-permute-start | bytes 786440 | tf_op jit(solution)/shard_map/ppermute | solution.py:19
  28.6 12.5 %copy-start.4 = (bf16[1,1,128,512]{3,2,1,0:T(8,128)(2,1)S(1)}, bf16[1,1,128,512]{3,2,1,0:T(8,128)(2,1)}, u32[]{:S(2)}) copy-start(bf16[1,1,128,512]{3,2,1,0:T(8,128)(2,1)} %param.7) | copy-start | bytes 393220
  28.7 12.5 %copy-start.5 = (bf16[1,1,128,512]{3,2,1,0:T(8,128)(2,1)S(1)}, bf16[1,1,128,512]{3,2,1,0:T(8,128)(2,1)}, u32[]{:S(2)}) copy-start(bf16[1,1,128,512]{3,2,1,0:T(8,128)(2,1)} %param.6) | copy-start | bytes 393220
  31.2 35.3 %collective-permute-start.5 = (bf16[128,1024]{0,1:T(8,128)(2,1)}, bf16[128,1024]{0,1:T(8,128)(2,1)}, u32[]{:S(2)}, u32[]{:S(2)}) collective-permute-start(bf16[128,1024]{0,1:T(8,128)(2,1)} %bitcast.20), channel_id=1, source_target_pairs={{0,384},{128,0},{256,128},{384,256},{1,385},{129,1},{257,129},{385... | collective-permute-start | bytes 786440 | tf_op jit(solution)/shard_map/ppermute | solution.py:19
  34.4 26.3 %collective-permute-start.6 = (bf16[128,1024]{0,1:T(8,128)(2,1)}, bf16[128,1024]{0,1:T(8,128)(2,1)}, u32[]{:S(2)}, u32[]{:S(2)}) collective-permute-start(bf16[128,1024]{0,1:T(8,128)(2,1)} %bitcast.31), channel_id=1, source_target_pairs={{0,384},{128,0},{256,128},{384,256},{1,385},{129,1},{257,129},{385... | collective-permute-start | bytes 786440 | tf_op jit(solution)/shard_map/ppermute | solution.py:19
  37.3 19.8 %collective-permute-start.4 = (bf16[128,1024]{0,1:T(8,128)(2,1)S(1)}, bf16[128,1024]{0,1:T(8,128)(2,1)S(1)}, u32[]{:S(2)}, u32[]{:S(2)}) collective-permute-start(bf16[128,1024]{0,1:T(8,128)(2,1)S(1)} %bitcast.238), channel_id=1, source_target_pairs={{0,384},{128,0},{256,128},{384,256},{1,385},{129,1},{257,129},{385... | collective-permute-start | bytes 786440 | tf_op jit(solution)/shard_map/ppermute | solution.py:19
  41.2 21.6 %copy-start.2 = (bf16[640,1024]{1,0:T(8,128)(2,1)}, bf16[640,1024]{1,0:T(8,128)(2,1)S(1)}, u32[]{:S(2)}) copy-start(bf16[640,1024]{1,0:T(8,128)(2,1)S(1)} %constant_dynamic-update-slice_fusion) | copy-start | bytes 3932164
  57.0 2.3 %copy-start.7 = (bf16[128,1024]{0,1:T(8,128)(2,1)}, bf16[128,1024]{0,1:T(8,128)(2,1)S(1)}, u32[]{:S(2)}) copy-start(bf16[128,1024]{0,1:T(8,128)(2,1)S(1)} %collective-permute-done.4) | copy-start | bytes 786436
  57.0 2.6 %copy-start.11 = (f32[8,128,640]{1,2,0:T(8,128)S(1)}, f32[8,128,640]{1,2,0:T(8,128)}, u32[]{:S(2)}) copy-start(f32[8,128,640]{1,2,0:T(8,128)} %get-tuple-element.29) | copy-start | bytes 7864324
  59.7 1.7 %copy-start.9 = (f32[8,128,640]{1,2,0:T(8,128)S(1)}, f32[8,128,640]{1,2,0:T(8,128)}, u32[]{:S(2)}) copy-start(f32[8,128,640]{1,2,0:T(8,128)} %get-tuple-element.33) | copy-start | bytes 7864324
  62.8 3.7 %copy-start.12 = (f32[8,128,640]{1,2,0:T(8,128)S(1)}, f32[8,128,640]{1,2,0:T(8,128)}, u32[]{:S(2)}) copy-start(f32[8,128,640]{1,2,0:T(8,128)} %get-tuple-element.31) | copy-start | bytes 7864324
  64.5 2.0 %copy-start.3 = (bf16[640,1024]{1,0:T(8,128)(2,1)S(1)}, bf16[640,1024]{1,0:T(8,128)(2,1)}, u32[]{:S(2)}) copy-start(bf16[640,1024]{1,0:T(8,128)(2,1)} %copy-done.2) | copy-start | bytes 3932164
  69.5 1.7 %copy-start.10 = (f32[8,128,640]{1,2,0:T(8,128)S(1)}, f32[8,128,640]{1,2,0:T(8,128)}, u32[]{:S(2)}) copy-start(f32[8,128,640]{1,2,0:T(8,128)} %get-tuple-element.35) | copy-start | bytes 7864324
  74.2 1.0 copy-start.8
  80.3 1.5 %copy-start = (f32[640,1024]{0,1:T(8,128)}, f32[640,1024]{0,1:T(8,128)S(1)}, u32[]{:S(2)}) copy-start(f32[640,1024]{0,1:T(8,128)S(1)} %fusion.34) | copy-start | bytes 7864324
  83.6 35.9 %all-to-all-start = ((f32[128,1,40]{2,1,0:T(1,128)}), f32[128,1,40]{2,1,0:T(1,128)S(1)}, u32[]{:S(2)}, u32[]{:S(2)}) async-start(f32[128,1,40]{2,1,0:T(1,128)} %bitcast.61), calls=%async_computation | async-start | bytes 131072 | tf_op jit(solution)/shard_map/all_to_all | solution.py:62
  110.4 34.9 %collective-permute-start.8 = (bf16[128,1024]{0,1:T(8,128)(2,1)}, bf16[128,1024]{0,1:T(8,128)(2,1)S(1)}, u32[]{:S(2)}, u32[]{:S(2)}) collective-permute-start(bf16[128,1024]{0,1:T(8,128)(2,1)} %get-tuple-element.18), channel_id=1, source_target_pairs={{16,0},{20,4},{24,8},{28,12},{32,16},{36,20},{40,24},{44,28},{48,3... | collective-permute-start | bytes 786440 | tf_op jit(solution)/shard_map/ppermute | solution.py:25
  111.7 33.6 %collective-permute-start.11 = (bf16[128,1024]{0,1:T(8,128)(2,1)}, bf16[128,1024]{0,1:T(8,128)(2,1)}, u32[]{:S(2)}, u32[]{:S(2)}) collective-permute-start(bf16[128,1024]{0,1:T(8,128)(2,1)} %get-tuple-element.19), channel_id=1, source_target_pairs={{4,0},{8,4},{12,8},{16,12},{20,16},{24,20},{28,24},{32,28},{36,32}... | collective-permute-start | bytes 786440 | tf_op jit(solution)/shard_map/ppermute | solution.py:25
  114.5 30.8 %collective-permute-start.10 = (bf16[128,1024]{0,1:T(8,128)(2,1)}, bf16[128,1024]{0,1:T(8,128)(2,1)}, u32[]{:S(2)}, u32[]{:S(2)}) collective-permute-start(bf16[128,1024]{0,1:T(8,128)(2,1)} %get-tuple-element.20), channel_id=1, source_target_pairs={{8,0},{12,4},{16,8},{20,12},{24,16},{28,20},{32,24},{36,28},{40,32... | collective-permute-start | bytes 786440 | tf_op jit(solution)/shard_map/ppermute | solution.py:25
  115.8 29.5 %collective-permute-start.9 = (bf16[128,1024]{0,1:T(8,128)(2,1)}, bf16[128,1024]{0,1:T(8,128)(2,1)}, u32[]{:S(2)}, u32[]{:S(2)}) collective-permute-start(bf16[128,1024]{0,1:T(8,128)(2,1)} %get-tuple-element.21), channel_id=1, source_target_pairs={{12,0},{16,4},{20,8},{24,12},{28,16},{32,20},{36,24},{40,28},{44,3... | collective-permute-start | bytes 786440 | tf_op jit(solution)/shard_map/ppermute | solution.py:25
  120.4 24.0 %all-to-all-start.1 = ((f32[128,1,40]{2,1,0:T(1,128)}), f32[128,1,40]{2,1,0:T(1,128)S(1)}, u32[]{:S(2)}, u32[]{:S(2)}) async-start(f32[128,1,40]{2,1,0:T(1,128)} %broadcast_in_dim.85), calls=%async_computation.1 | async-start | bytes 131072 | tf_op jit(solution)/shard_map/all_to_all | solution.py:70

commit v7 on v5

--- a/solution.py
+++ b/solution.py
@@ -100,8 +100,14 @@
     anchor = here * shard_length
 
     group_cols = QUERY_PER_KEY * FEATURE_SIZE
+    per_chunk = SHARED_GROUPS
+    chunk_cols = per_chunk * group_cols
+    cot_chunks = [
+        passed_along(incoming[0, 0, :, k * chunk_cols : (k + 1) * chunk_cols], "pipe", -1)
+        for k in range(SHARED_GROUPS // per_chunk)
+    ]
     cot_groups = [
-        passed_along(incoming[0, 0, :, g * group_cols : (g + 1) * group_cols], "pipe", -1)
+        cot_chunks[g // per_chunk][:, (g % per_chunk) * group_cols : (g % per_chunk + 1) * group_cols]
         for g in range(SHARED_GROUPS)
     ]
     kv_own = jnp.concatenate([key_input[0, 0], value_input[0, 0]], axis=1)

time: 149 us -> 143 us (0.960)
  waiting for transfers between devices: 16.3 us -> 39.5 us
  starting transfers between devices: 76.8 us -> 57.6 us
  matrix products: 32.2 us -> 24.6 us
  local copies, waits for them, and re-layouts: 16.9 us -> 15.2 us
    ppermute x4 -> x1, waiting for transfers between devices: 5.33 us -> 28.6 us  [passed_along(): return lax.ppermute(value, axis, pairs)]
    all_to_all x1, starting transfers between devices: 25.8 us -> 12.4 us  [exchange_sum(): pieces = lax.all_to_all(value.reshape(count, -1), axes, 0, 0, tiled=True)]
    ppermute x4 -> x1, starting transfers between devices: 15.8 us -> 9.88 us  [passed_along(): return lax.ppermute(value, axis, pairs)]
    dot_general x4, matrix products: 5.46 us -> 2.49 us  [attend_group(): jnp.einsum('qhd,kd->hqk', cot_g, value_g, preferred_element_type=jnp.floa...]
    dot_general x4, matrix products: 5.05 us -> 2.2 us  [attend_group(): jnp.einsum('hqk,qhd->kd', probs_b, cot_g, preferred_element_type=jnp.floa...]
    dot_general x4, matrix products: 6.44 us -> 4.59 us  [attend_group(): jnp.einsum('hqk,kd->qhd', probs_b, value_g, preferred_element_type=jnp.fl...]
    unnamed x38 -> x31, local copies, waits for them, and re-layouts: 12.2 us -> 10.5 us
  transfers between devices with their start and end apart: 14 -> 11, of which waited for: 3 -> 3; matrix products, arithmetic and copies ran while one was open for 24% -> 14% of each run, Pallas kernels for 0% -> 0%
where the time goes in v7:
time: 143 us; the launch traced here: 142 us
  starting transfers between devices  57.6 us (40%)
  waiting for transfers between devices  39.5 us (28%)
  matrix products  24.6 us (17%)
  local copies, waits for them, and re-layouts  15.2 us (11%)
  other arithmetic  4.16 us (3%)
    ppermute x1, waiting for transfers between devices, passed_along(): return lax.ppermute(value, axis, pairs)  28.6 us
    ppermute x8, starting transfers between devices, shifted(): return lax.ppermute(value, axis, pairs)  21.4 us
    all_to_all x1, starting transfers between devices, exchange_sum(): return lax.all_to_all(mine, axes, 0, 0, tiled=True).reshape(-1)  13.9 us
    all_to_all x1, starting transfers between devices, exchange_sum(): pieces = lax.all_to_all(value.reshape(count, -1), axes, 0, 0, tiled=True)  12.4 us
    sub x4, matrix products, attend_group(): weights = jnp.where(visible[None], jnp.exp(scores - row_max), 0.0)  10.5 us
    unnamed x31, local copies, waits for them, and re-layouts  10.5 us
    ppermute x1, starting transfers between devices, passed_along(): return lax.ppermute(value, axis, pairs)  9.88 us
    all_to_all x1, waiting for transfers between devices, exchange_sum(): return lax.all_to_all(mine, axes, 0, 0, tiled=True).reshape(-1)  8.6 us
  transfers between devices with their start and end apart: 11, of which 3 were waited for; matrix products, arithmetic and copies ran while one was open for 14% of the time, Pallas kernels for 0%

profile of v7, /device:TPU:1, one launch (start us, length us, event | category | flops | bytes accessed | tf_op | source)
XLA Modules:
  0.0 142.3 jit_solution(7850781804051775939)
XLA Ops:
  0.7 1.1 pad_maximum_fusion.1
  1.7 5.4 %collective-permute-start.3 = (bf16[128,1024]{1,0:T(8,128)(2,1)S(1)}, bf16[128,1024]{1,0:T(8,128)(2,1)S(1)}, u32[]{:S(2)}, u32[]{:S(2)}) collective-permute-start(bf16[128,1024]{1,0:T(8,128)(2,1)S(1)} %pad_maximum_fusion.1), channel_id=1, source_target_pairs={{0,4},{4,8},{8,12},{12,16},{16,20},{20,24},{24,28},{28,32},{32,36}... | collective-permute-start | bytes 786440 | tf_op jit(solution)/shard_map/ppermute | solution.py:25
  7.1 2.3 %collective-permute-start.2 = (bf16[128,1024]{1,0:T(8,128)(2,1)S(1)}, bf16[128,1024]{1,0:T(8,128)(2,1)S(1)}, u32[]{:S(2)}, u32[]{:S(2)}) collective-permute-start(bf16[128,1024]{1,0:T(8,128)(2,1)S(1)} %pad_maximum_fusion.1), channel_id=1, source_target_pairs={{0,8},{4,12},{8,16},{12,20},{16,24},{20,28},{24,32},{28,36},{32,40... | collective-permute-start | bytes 786440 | tf_op jit(solution)/shard_map/ppermute | solution.py:25
  9.4 3.8 %collective-permute-start.1 = (bf16[128,1024]{1,0:T(8,128)(2,1)S(1)}, bf16[128,1024]{1,0:T(8,128)(2,1)}, u32[]{:S(2)}, u32[]{:S(2)}) collective-permute-start(bf16[128,1024]{1,0:T(8,128)(2,1)S(1)} %pad_maximum_fusion.1), channel_id=1, source_target_pairs={{0,12},{4,16},{8,20},{12,24},{16,28},{20,32},{24,36},{28,40},{32,4... | collective-permute-start | bytes 786440 | tf_op jit(solution)/shard_map/ppermute | solution.py:25
  13.2 3.2 %collective-permute-start = (bf16[128,1024]{1,0:T(8,128)(2,1)S(1)}, bf16[128,1024]{1,0:T(8,128)(2,1)}, u32[]{:S(2)}, u32[]{:S(2)}) collective-permute-start(bf16[128,1024]{1,0:T(8,128)(2,1)S(1)} %pad_maximum_fusion.1), channel_id=1, source_target_pairs={{0,16},{4,20},{8,24},{12,28},{16,32},{20,36},{24,40},{28,44},{32,4... | collective-permute-start | bytes 786440 | tf_op jit(solution)/shard_map/ppermute | solution.py:25
  16.5 2.3 %copy.91 = bf16[1,1,128,4096]{2,3,1,0:T(8,128)(2,1)} copy(bf16[1,1,128,4096]{3,2,1,0:T(8,128)(2,1)} %param.8) | data formatting | bytes 2097152 | tf_op args[3]
  18.7 9.9 %collective-permute-start.4 = (bf16[128,4096]{0,1:T(8,128)(2,1)}, bf16[128,4096]{0,1:T(8,128)(2,1)}, u32[]{:S(2)}, u32[]{:S(2)}) collective-permute-start(bf16[128,4096]{0,1:T(8,128)(2,1)} %bitcast.9), channel_id=1, source_target_pairs={{0,384},{128,0},{256,128},{384,256},{1,385},{129,1},{257,129},{385... | collective-permute-start | bytes 3145736 | tf_op jit(solution)/shard_map/ppermute | solution.py:19
  28.9 0.7 copy.89
  29.6 1.0 constant_dynamic-update-slice_fusion.4
  30.6 1.0 constant_dynamic-update-slice_fusion.3
  31.7 2.7 %fusion.106 = (f32[8,128]{1,0:T(8,128)S(1)}, f32[8,128,640]{1,2,0:T(8,128)}) fusion(pred[128,640]{0,1:T(8,128)(4,1)S(1)} %fusion.50, bf16[128,32,128]{0,2,1:T(8,128)(2,1)S(1)} %bitcast.222, bf16[640,1024]{1,0:T(8,128)(2,1)S(1)} %constant_dynamic-update-slice_fusion), kind=kOutput, calls=%fused_computation.143 | convolution fusion | flops 171049600 | bytes 3215360 | tf_op jit(solution)/shard_map/sub | solution.py:79
  34.3 2.6 %fusion.112 = (f32[8,128]{1,0:T(8,128)S(1)}, f32[8,128,640]{1,2,0:T(8,128)}) fusion(pred[128,640]{0,1:T(8,128)(4,1)S(1)} %fusion.50, bf16[128,32,128]{0,2,1:T(8,128)(2,1)S(1)} %bitcast.223, bf16[640,1024]{1,0:T(8,128)(2,1)S(1)} %constant_dynamic-update-slice_fusion), kind=kOutput, calls=%fused_computation.145 | convolution fusion | flops 171049600 | bytes 3215360 | tf_op jit(solution)/shard_map/sub | solution.py:79
  36.9 2.6 %fusion.109 = (f32[8,128]{1,0:T(8,128)S(1)}, f32[8,128,640]{1,2,0:T(8,128)}) fusion(pred[128,640]{0,1:T(8,128)(4,1)S(1)} %fusion.50, bf16[128,32,128]{0,2,1:T(8,128)(2,1)S(1)} %bitcast.224, bf16[640,1024]{1,0:T(8,128)(2,1)S(1)} %constant_dynamic-update-slice_fusion), kind=kOutput, calls=%fused_computation.144 | convolution fusion | flops 171049600 | bytes 3215360 | tf_op jit(solution)/shard_map/sub | solution.py:79
  39.6 2.6 %fusion.115 = (f32[8,128]{1,0:T(8,128)S(1)}, f32[8,128,640]{1,2,0:T(8,128)}) fusion(pred[128,640]{0,1:T(8,128)(4,1)S(1)} %fusion.50, bf16[128,32,128]{0,2,1:T(8,128)(2,1)S(1)} %bitcast.225, bf16[640,1024]{1,0:T(8,128)(2,1)S(1)} %constant_dynamic-update-slice_fusion), kind=kOutput, calls=%fused_computation.146 | convolution fusion | flops 171049600 | bytes 3215360 | tf_op jit(solution)/shard_map/sub | solution.py:79
  42.2 28.6 %collective-permute-done.4 = bf16[128,4096]{0,1:T(8,128)(2,1)} collective-permute-done((bf16[128,4096]{0,1:T(8,128)(2,1)}, bf16[128,4096]{0,1:T(8,128)(2,1)}, u32[]{:S(2)}, u32[]{:S(2)}) %collective-permute-start.4) | collective-permute-done | bytes 1048608 | tf_op jit(solution)/shard_map/ppermute | solution.py:19
  70.7 1.3 fusion.105
  72.0 2.3 %multiply_reduce_fusion.3 = f32[128,8]{0,1:T(8,128)S(1)} fusion(bf16[128,8,128]{0,2,1:T(8,128)(2,1)S(1)} %bitcast.245, bf16[640,1024]{1,0:T(8,128)(2,1)S(1)} %constant_dynamic-update-slice_fusion, f32[8,128,640]{1,2,0:T(8,128)} %get-tuple-element.29, f32[8,128]{1,0:T(8,128)S(1)} %get-tuple-element.28), kind=kOutput, calls=%fused_computation.87 | convolution fusion | flops 169475072 | bytes 3055616 | tf_op jit(solution)/shard_map/hqk,kd->qhd/dot_general | solution.py:82
  74.5 0.6 fusion.15
  75.6 0.5 fusion.41
  76.1 0.8 copy-done.7
  77.4 0.6 fusion.9
  78.0 1.5 %convolution_bitcast_fusion.2 = f32[128,8,128]{0,2,1:T(8,128)S(1)} fusion(bf16[8,128,640]{1,2,0:T(8,128)(2,1)S(1)} %fusion.9, bf16[640,1024]{1,0:T(8,128)(2,1)} %copy-done.2), kind=kOutput, calls=%fused_computation.51 | convolution fusion | flops 167772160 | bytes 1998848 | tf_op jit(solution)/shard_map/hqk,kd->qhd/dot_general | solution.py:86
  79.5 1.4 %multiply_reduce_fusion.2 = f32[128,8]{0,1:T(8,128)S(1)} fusion(bf16[128,8,128]{0,2,1:T(8,128)(2,1)S(1)} %bitcast.242, bf16[640,1024]{1,0:T(8,128)(2,1)} %copy-done.2, f32[8,128,640]{1,2,0:T(8,128)S(1)} %copy-done.10, f32[8,128]{1,0:T(8,128)S(1)} %get-tuple-element.30), kind=kOutput, calls=%fused_computation.86 | convolution fusion | flops 169475072 | bytes 3055616 | tf_op jit(solution)/shard_map/hqk,kd->qhd/dot_general | solution.py:82
  80.9 0.6 fusion.12
  82.0 0.5 fusion.40
  83.7 0.6 fusion.6
  85.3 0.5 fusion.37
  85.9 0.5 fusion.36
  86.4 0.6 fusion.35
  87.0 0.6 fusion.34
  87.5 1.5 %copy-done = f32[640,1024]{0,1:T(8,128)} copy-done((f32[640,1024]{0,1:T(8,128)}, f32[640,1024]{0,1:T(8,128)S(1)}, u32[]{:S(2)}) %copy-start) | copy-done | bytes 2621464
  89.3 0.8 fusion.32
  90.1 0.7 all_to_all.12
  90.9 12.4 %all-to-all-start = ((f32[128,1,40]{2,1,0:T(1,128)}), f32[128,1,40]{2,1,0:T(1,128)S(1)}, u32[]{:S(2)}, u32[]{:S(2)}) async-start(f32[128,1,40]{2,1,0:T(1,128)} %bitcast.58), calls=%async_computation | async-start | bytes 131072 | tf_op jit(solution)/shard_map/all_to_all | solution.py:62
  103.3 1.1 fusion.104
  104.4 1.3 collective-permute-start.5
  105.7 2.8 %collective-permute-start.8 = (bf16[128,1024]{0,1:T(8,128)(2,1)}, bf16[128,1024]{0,1:T(8,128)(2,1)}, u32[]{:S(2)}, u32[]{:S(2)}) collective-permute-start(bf16[128,1024]{0,1:T(8,128)(2,1)} %get-tuple-element.19), channel_id=1, source_target_pairs={{4,0},{8,4},{12,8},{16,12},{20,16},{24,20},{28,24},{32,28},{36,32}... | collective-permute-start | bytes 786440 | tf_op jit(solution)/shard_map/ppermute | solution.py:25
  108.5 1.3 collective-permute-start.7
  109.8 1.3 collective-permute-start.6
  111.1 2.3 %all-to-all-done = f32[128,1,40]{2,1,0:T(1,128)S(1)} async-done(((f32[128,1,40]{2,1,0:T(1,128)}), f32[128,1,40]{2,1,0:T(1,128)S(1)}, u32[]{:S(2)}, u32[]{:S(2)}) %all-to-all-start) | async-done | bytes 20512 | tf_op jit(solution)/shard_map/all_to_all | solution.py:62
  113.7 0.7 broadcast_in_dim.85
  114.3 13.9 %all-to-all-start.1 = ((f32[128,1,40]{2,1,0:T(1,128)}), f32[128,1,40]{2,1,0:T(1,128)S(1)}, u32[]{:S(2)}, u32[]{:S(2)}) async-start(f32[128,1,40]{2,1,0:T(1,128)} %broadcast_in_dim.85), calls=%async_computation.1 | async-start | bytes 131072 | tf_op jit(solution)/shard_map/all_to_all | solution.py:70
  128.5 1.3 copy.128
  129.8 8.6 %all-to-all-done.1 = f32[128,1,40]{2,1,0:T(1,128)S(1)} async-done(((f32[128,1,40]{2,1,0:T(1,128)}), f32[128,1,40]{2,1,0:T(1,128)S(1)}, u32[]{:S(2)}, u32[]{:S(2)}) %all-to-all-start.1) | async-done | bytes 20512 | tf_op jit(solution)/shard_map/all_to_all | solution.py:70
  138.6 0.7 div.50
  139.3 1.4 %fusion.49 = bf16[128,1024]{0,1:T(8,128)(2,1)S(1)} fusion(f32[640,1024]{0,1:T(8,128)} %copy-done, bf16[128,1024]{0,1:T(8,128)(2,1)} %collective-permute-done.8, bf16[128,1024]{0,1:T(8,128)(2,1)} %collective-permute-done.7, bf16[128,1024]{0,1:T(8,128)(2,1)} %collective-permute-done.6, bf16[128,1024]{0,1:T(8,128)(2,1)S(1)} %collective-permute-done.5), kind=kLoop, calls=%fused_computation.83 | loop fusion | flops 1179648 | bytes 1835008 | tf_op jit(solution)/shard_map/convert.1
  140.8 0.8 copy.130
  141.5 0.8 copy.129
  (66 shorter events, 4.9 us)
Async XLA Ops:
  0.6 28.0 %copy-start.6 = (s32[1,4096]{1,0:T(1,128)S(1)}, s32[1,4096]{1,0:T(1,128)}, u32[]{:S(2)}) copy-start(s32[1,4096]{1,0:T(1,128)} %param.9) | copy-start | bytes 49156
  0.6 28.2 %copy-start.1 = (bf16[1,1,128,4096]{3,2,1,0:T(8,128)(2,1)S(1)}, bf16[1,1,128,4096]{3,2,1,0:T(8,128)(2,1)}, u32[]{:S(2)}) copy-start(bf16[1,1,128,4096]{3,2,1,0:T(8,128)(2,1)} %param.5) | copy-start | bytes 3145732
  1.7 29.8 %collective-permute-start.3 = (bf16[128,1024]{1,0:T(8,128)(2,1)S(1)}, bf16[128,1024]{1,0:T(8,128)(2,1)S(1)}, u32[]{:S(2)}, u32[]{:S(2)}) collective-permute-start(bf16[128,1024]{1,0:T(8,128)(2,1)S(1)} %pad_maximum_fusion.1), channel_id=1, source_target_pairs={{0,4},{4,8},{8,12},{12,16},{16,20},{20,24},{24,28},{28,32},{32,36}... | collective-permute-start | bytes 786440 | tf_op jit(solution)/shard_map/ppermute | solution.py:25
  7.1 24.4 %collective-permute-start.2 = (bf16[128,1024]{1,0:T(8,128)(2,1)S(1)}, bf16[128,1024]{1,0:T(8,128)(2,1)S(1)}, u32[]{:S(2)}, u32[]{:S(2)}) collective-permute-start(bf16[128,1024]{1,0:T(8,128)(2,1)S(1)} %pad_maximum_fusion.1), channel_id=1, source_target_pairs={{0,8},{4,12},{8,16},{12,20},{16,24},{20,28},{24,32},{28,36},{32,40... | collective-permute-start | bytes 786440 | tf_op jit(solution)/shard_map/ppermute | solution.py:25
  9.4 21.1 %collective-permute-start.1 = (bf16[128,1024]{1,0:T(8,128)(2,1)S(1)}, bf16[128,1024]{1,0:T(8,128)(2,1)}, u32[]{:S(2)}, u32[]{:S(2)}) collective-permute-start(bf16[128,1024]{1,0:T(8,128)(2,1)S(1)} %pad_maximum_fusion.1), channel_id=1, source_target_pairs={{0,12},{4,16},{8,20},{12,24},{16,28},{20,32},{24,36},{28,40},{32,4... | collective-permute-start | bytes 786440 | tf_op jit(solution)/shard_map/ppermute | solution.py:25
  13.2 16.3 %collective-permute-start = (bf16[128,1024]{1,0:T(8,128)(2,1)S(1)}, bf16[128,1024]{1,0:T(8,128)(2,1)}, u32[]{:S(2)}, u32[]{:S(2)}) collective-permute-start(bf16[128,1024]{1,0:T(8,128)(2,1)S(1)} %pad_maximum_fusion.1), channel_id=1, source_target_pairs={{0,16},{4,20},{8,24},{12,28},{16,32},{20,36},{24,40},{28,44},{32,4... | collective-permute-start | bytes 786440 | tf_op jit(solution)/shard_map/ppermute | solution.py:25
  18.7 12.9 %copy-start.4 = (bf16[1,1,128,512]{3,2,1,0:T(8,128)(2,1)S(1)}, bf16[1,1,128,512]{3,2,1,0:T(8,128)(2,1)}, u32[]{:S(2)}) copy-start(bf16[1,1,128,512]{3,2,1,0:T(8,128)(2,1)} %param.7) | copy-start | bytes 393220
  18.7 12.9 %copy-start.5 = (bf16[1,1,128,512]{3,2,1,0:T(8,128)(2,1)S(1)}, bf16[1,1,128,512]{3,2,1,0:T(8,128)(2,1)}, u32[]{:S(2)}) copy-start(bf16[1,1,128,512]{3,2,1,0:T(8,128)(2,1)} %param.6) | copy-start | bytes 393220
  18.7 52.0 %collective-permute-start.4 = (bf16[128,4096]{0,1:T(8,128)(2,1)}, bf16[128,4096]{0,1:T(8,128)(2,1)}, u32[]{:S(2)}, u32[]{:S(2)}) collective-permute-start(bf16[128,4096]{0,1:T(8,128)(2,1)} %bitcast.9), channel_id=1, source_target_pairs={{0,384},{128,0},{256,128},{384,256},{1,385},{129,1},{257,129},{385... | collective-permute-start | bytes 3145736 | tf_op jit(solution)/shard_map/ppermute | solution.py:19
  31.6 45.7 %copy-start.2 = (bf16[640,1024]{1,0:T(8,128)(2,1)}, bf16[640,1024]{1,0:T(8,128)(2,1)S(1)}, u32[]{:S(2)}) copy-start(bf16[640,1024]{1,0:T(8,128)(2,1)S(1)} %constant_dynamic-update-slice_fusion) | copy-start | bytes 3932164
  72.0 2.5 %copy-start.9 = (f32[8,128,640]{1,2,0:T(8,128)S(1)}, f32[8,128,640]{1,2,0:T(8,128)}, u32[]{:S(2)}) copy-start(f32[8,128,640]{1,2,0:T(8,128)} %get-tuple-element.29) | copy-start | bytes 7864324
  75.2 1.7 %copy-start.7 = (f32[8,128,640]{1,2,0:T(8,128)S(1)}, f32[8,128,640]{1,2,0:T(8,128)}, u32[]{:S(2)}) copy-start(f32[8,128,640]{1,2,0:T(8,128)} %get-tuple-element.33) | copy-start | bytes 7864324
  77.3 2.1 %copy-start.10 = (f32[8,128,640]{1,2,0:T(8,128)S(1)}, f32[8,128,640]{1,2,0:T(8,128)}, u32[]{:S(2)}) copy-start(f32[8,128,640]{1,2,0:T(8,128)} %get-tuple-element.31) | copy-start | bytes 7864324
  79.5 1.5 %copy-start.3 = (bf16[640,1024]{1,0:T(8,128)(2,1)S(1)}, bf16[640,1024]{1,0:T(8,128)(2,1)}, u32[]{:S(2)}) copy-start(bf16[640,1024]{1,0:T(8,128)(2,1)} %copy-done.2) | copy-start | bytes 3932164
  81.6 1.7 %copy-start.8 = (f32[8,128,640]{1,2,0:T(8,128)S(1)}, f32[8,128,640]{1,2,0:T(8,128)}, u32[]{:S(2)}) copy-start(f32[8,128,640]{1,2,0:T(8,128)} %get-tuple-element.35) | copy-start | bytes 7864324
  87.5 1.5 %copy-start = (f32[640,1024]{0,1:T(8,128)}, f32[640,1024]{0,1:T(8,128)S(1)}, u32[]{:S(2)}) copy-start(f32[640,1024]{0,1:T(8,128)S(1)} %fusion.34) | copy-start | bytes 7864324
  90.9 22.5 %all-to-all-start = ((f32[128,1,40]{2,1,0:T(1,128)}), f32[128,1,40]{2,1,0:T(1,128)S(1)}, u32[]{:S(2)}, u32[]{:S(2)}) async-start(f32[128,1,40]{2,1,0:T(1,128)} %bitcast.58), calls=%async_computation | async-start | bytes 131072 | tf_op jit(solution)/shard_map/all_to_all | solution.py:62
  104.4 34.9 %collective-permute-start.5 = (bf16[128,1024]{0,1:T(8,128)(2,1)}, bf16[128,1024]{0,1:T(8,128)(2,1)S(1)}, u32[]{:S(2)}, u32[]{:S(2)}) collective-permute-start(bf16[128,1024]{0,1:T(8,128)(2,1)} %get-tuple-element.18), channel_id=1, source_target_pairs={{16,0},{20,4},{24,8},{28,12},{32,16},{36,20},{40,24},{44,28},{48,3... | collective-permute-start | bytes 786440 | tf_op jit(solution)/shard_map/ppermute | solution.py:25
  105.7 33.6 %collective-permute-start.8 = (bf16[128,1024]{0,1:T(8,128)(2,1)}, bf16[128,1024]{0,1:T(8,128)(2,1)}, u32[]{:S(2)}, u32[]{:S(2)}) collective-permute-start(bf16[128,1024]{0,1:T(8,128)(2,1)} %get-tuple-element.19), channel_id=1, source_target_pairs={{4,0},{8,4},{12,8},{16,12},{20,16},{24,20},{28,24},{32,28},{36,32}... | collective-permute-start | bytes 786440 | tf_op jit(solution)/shard_map/ppermute | solution.py:25
  108.5 30.8 %collective-permute-start.7 = (bf16[128,1024]{0,1:T(8,128)(2,1)}, bf16[128,1024]{0,1:T(8,128)(2,1)}, u32[]{:S(2)}, u32[]{:S(2)}) collective-permute-start(bf16[128,1024]{0,1:T(8,128)(2,1)} %get-tuple-element.20), channel_id=1, source_target_pairs={{8,0},{12,4},{16,8},{20,12},{24,16},{28,20},{32,24},{36,28},{40,32... | collective-permute-start | bytes 786440 | tf_op jit(solution)/shard_map/ppermute | solution.py:25
  109.8 29.5 %collective-permute-start.6 = (bf16[128,1024]{0,1:T(8,128)(2,1)}, bf16[128,1024]{0,1:T(8,128)(2,1)}, u32[]{:S(2)}, u32[]{:S(2)}) collective-permute-start(bf16[128,1024]{0,1:T(8,128)(2,1)} %get-tuple-element.21), channel_id=1, source_target_pairs={{12,0},{16,4},{20,8},{24,12},{28,16},{32,20},{36,24},{40,28},{44,3... | collective-permute-start | bytes 786440 | tf_op jit(solution)/shard_map/ppermute | solution.py:25
  114.3 24.0 %all-to-all-start.1 = ((f32[128,1,40]{2,1,0:T(1,128)}), f32[128,1,40]{2,1,0:T(1,128)S(1)}, u32[]{:S(2)}, u32[]{:S(2)}) async-start(f32[128,1,40]{2,1,0:T(1,128)} %broadcast_in_dim.85), calls=%async_computation.1 | async-start | bytes 131072 | tf_op jit(solution)/shard_map/all_to_all | solution.py:70
